TPU v7x, 256 devices: a whole 4x4x8 slice. The times are simulated.
256 devices in a mesh: slab: 32 (over z, x), coil: 8 (over y, core).
Axes of the slice: x: 4, y: 4, z: 8, core: 2. Of those that a mesh axis runs over, the one named last changes fastest.
Arguments:
- noisy: float32 [2, 64, 256, 128], P(None, 'slab', 'coil'), may hold values from -6 to 6
- step_index: int32 [], replicated, may hold values from 200 to 599
- w_in: bfloat16 [3, 3, 3, 32, 2], replicated, may hold values from -0.875 to 0.875
- w_mid: bfloat16 [3, 3, 3, 32, 32], replicated, may hold values from -0.21875 to 0.21875
- w_out: bfloat16 [3, 3, 3, 2, 32], replicated, may hold values from -0.21875 to 0.21875
- time_weight: float32 [32, 32], replicated, may hold values from -1 to 1
- sens: float32 [16, 2, 64, 256, 128], P('coil', None, 'slab')
- kdata: float32 [16, 2, 64, 256, 128], P('coil', None, None, 'slab'), may hold values from -4 to 4
- mask: int32 [64, 256], P(None, 'slab'), may hold values from 0 to 1, as said below
Outputs:
- recon: float32 [2, 64, 256, 128], P(None, 'slab', 'coil')
- next_sample: float32 [2, 64, 256, 128], P(None, 'slab', 'coil')
Inputs may be any that keep to these rules, and one draw needn't show every extreme that they name: mask[kz, ky] is 1 wherever min(kz, 64 - kz) < max(1, 4) and min(ky, 256 - ky) < max(1, 8); every other entry is 1 with chance one in three.
All inputs are finite; a program needn't handle non-finite values.
Results may differ from a plain program's by a relative error of at most 0.0023.
Values may be sent and summed in bfloat16 or wider, within the bound.
No kernel may reach another device: no remote copies, remote signals or barrier semaphores. Data moves between devices by JAX's collectives and lax.ppermute only.
A program may use at most 64 MiB of HBM per device.

v0:
```python
import math

import jax
import jax.numpy as jnp
from jax import lax
from jax.sharding import PartitionSpec as P

ITERS = 2
STEPS = 1000
STRIDE = 20


REG_WEIGHT = 0.5
HIGHEST_PRECISION = lax.Precision.HIGHEST


def extended(cells, sides, width):
    for axis, dim in sides:
        count = lax.axis_size(axis)
        ends = count - 1
        head = lax.slice_in_dim(cells, 0, width, axis=dim)
        tail = lax.slice_in_dim(cells, cells.shape[dim] - width, cells.shape[dim], axis=dim)
        cells = jnp.concatenate(
            [
                lax.ppermute(tail, axis, [(i, (i + 1) % count) for i in range(ends)]),
                cells,
                lax.ppermute(head, axis, [((i + 1) % count, i) for i in range(ends)]),
            ],
            axis=dim,
        )
    return cells


def plan_level(step_value):
    angle = (step_value / STEPS + 0.008) / 1.008 * (math.pi / 2)
    return jnp.cos(angle) ** 2


def time_bias(step_value, time_weight):
    half = time_weight.shape[0] // 2
    freqs = jnp.exp(-math.log(10000.0) * jnp.arange(half, dtype=jnp.float32) / half)
    phase = step_value * freqs
    embed = jnp.concatenate([jnp.sin(phase), jnp.cos(phase)])
    return jnp.dot(embed, time_weight, precision=HIGHEST_PRECISION)


def conv_layer(inputs, weights):
    depth, rows, width = (inputs.shape[1], inputs.shape[2], inputs.shape[3])
    padded = extended(inputs, (("slab", 1), ("coil", 2)), 1)
    total = jnp.zeros((weights.shape[3], depth, rows, width), jnp.float32)
    for depth_shift in range(3):
        for row_shift in range(3):
            window = padded[:, depth_shift : depth_shift + depth, row_shift : row_shift + rows, :]
            taps = jnp.einsum(
                "aoc,czyx->aozyx",
                weights[depth_shift, row_shift],
                window,
                preferred_element_type=jnp.float32,
            )
            shifted = jnp.pad(taps, ((0, 0), (0, 0), (0, 0), (0, 0), (1, 1)))
            total = (
                total
                + shifted[0, ..., 0:width]
                + shifted[1, ..., 1 : width + 1]
                + shifted[2, ..., 2 : width + 2]
            )
    return total


def dft_blocks(length, inverse):
    index = jnp.arange(length, dtype=jnp.int32)
    product = index[:, None] * index[None, :] % length
    theta = product.astype(jnp.float32) * (2.0 * math.pi / length)
    cosine = jnp.cos(theta) / math.sqrt(length)
    sine = jnp.sin(theta) / math.sqrt(length)
    if inverse:
        sine = -sine
    upper = jnp.stack([cosine, sine], axis=1)
    lower = jnp.stack([-sine, cosine], axis=1)
    return jnp.stack([upper, lower], axis=0)


def along_last(data, blocks):
    return jnp.einsum("pkqn,cqzyn->cpzyk", blocks, data, precision=HIGHEST_PRECISION)


def along_rows(data, blocks):
    return jnp.einsum("pkqn,cqzny->cpzky", blocks, data, precision=HIGHEST_PRECISION)


def along_depth(data, blocks):
    return jnp.einsum("pkqn,cqnyx->cpkyx", blocks, data, precision=HIGHEST_PRECISION)


def times_sens(sens, image):
    real_part = sens[:, 0] * image[0] - sens[:, 1] * image[1]
    imag_part = sens[:, 0] * image[1] + sens[:, 1] * image[0]
    return jnp.stack([real_part, imag_part], axis=1)


def times_conj(sens, images):
    real_part = jnp.sum(sens[:, 0] * images[:, 0] + sens[:, 1] * images[:, 1], axis=0)
    imag_part = jnp.sum(sens[:, 0] * images[:, 1] - sens[:, 1] * images[:, 0], axis=0)
    return jnp.stack([real_part, imag_part])


def coil_term(image_full, sens, kdata, weight, blocks, with_data):
    forward_x, forward_y, forward_z, inverse_x, inverse_y, inverse_z = blocks
    coil_images = times_sens(sens, image_full)
    spectrum = along_rows(along_last(coil_images, forward_x), forward_y)
    pencils = lax.all_to_all(spectrum, "slab", split_axis=3, concat_axis=2, tiled=True)
    kspace = along_depth(pencils, forward_z)
    if with_data:
        kspace = weight * (kdata - kspace)
    else:
        kspace = weight * kspace
    back = along_depth(kspace, inverse_z)
    slabs = lax.all_to_all(back, "slab", split_axis=2, concat_axis=3, tiled=True)
    images = along_last(along_rows(slabs, inverse_y), inverse_x)
    return times_conj(sens, images)


def combine_coils(partial_value):
    return lax.psum(partial_value, "coil")


def global_sums(values):
    return lax.psum(values, "slab")


def body(noisy, step_index, w_in, w_mid, w_out, time_weight, sens, kdata, mask):
    step_value = step_index.astype(jnp.float32)
    signal_level = plan_level(step_value)
    prior_level = plan_level(step_value - STRIDE)
    bias = time_bias(step_value, time_weight)
    hidden = jax.nn.silu(
        conv_layer(noisy.astype(jnp.bfloat16), w_in) + bias[:, None, None, None]
    ).astype(jnp.bfloat16)
    mixed = (hidden.astype(jnp.float32) + jax.nn.silu(conv_layer(hidden, w_mid))).astype(
        jnp.bfloat16
    )
    noise_pred = conv_layer(mixed, w_out)
    estimate = (noisy - jnp.sqrt(1.0 - signal_level) * noise_pred) / jnp.sqrt(signal_level)
    full_estimate = lax.all_gather(estimate, "coil", axis=2, tiled=True)
    depth_full = kdata.shape[2]
    rows_full = sens.shape[3]
    width = sens.shape[4]
    rows_share = noisy.shape[2]
    blocks = (
        dft_blocks(width, False),
        dft_blocks(rows_full, False),
        dft_blocks(depth_full, False),
        dft_blocks(width, True),
        dft_blocks(rows_full, True),
        dft_blocks(depth_full, True),
    )
    weight = mask.astype(jnp.float32)[None, None, :, :, None]

    def operator(image, with_data):
        return coil_term(image, sens, kdata, weight, blocks, with_data)

    solution = full_estimate
    residual = combine_coils(operator(full_estimate, True))
    direction = residual
    norm_now = global_sums(jnp.stack([jnp.sum(residual * residual)]))[0]
    for iteration in range(ITERS):
        final_turn = iteration + 1 == ITERS
        image = combine_coils(operator(direction, False)) + REG_WEIGHT * direction
        curvature = global_sums(jnp.stack([jnp.sum(direction * image)]))[0]
        step_size = norm_now / curvature
        solution = solution + step_size * direction
        if not final_turn:
            residual = residual - step_size * image
            norm_next = global_sums(jnp.stack([jnp.sum(residual * residual)]))[0]
            direction = residual + norm_next / norm_now * direction
            norm_now = norm_next
    recon = lax.dynamic_slice_in_dim(solution, lax.axis_index("coil") * rows_share, rows_share, 2)
    next_sample = jnp.sqrt(prior_level) * recon + jnp.sqrt(1.0 - prior_level) * noise_pred
    return (recon, next_sample)


def solution(mesh):
    return jax.shard_map(
        body,
        mesh=mesh,
        in_specs=(
            P(None, "slab", "coil", None),
            P(),
            P(),
            P(),
            P(),
            P(),
            P("coil", None, "slab", None, None),
            P("coil", None, None, "slab", None),
            P(None, "slab"),
        ),
        out_specs=(P(None, "slab", "coil", None), P(None, "slab", "coil", None)),
        check_vma=False,
    )
```

profile of v0, /device:TPU:0, one launch (start us, length us, event | category | flops | bytes accessed | tf_op | source)
XLA Modules:
  0.0 818.5 jit_solution(9040750834225640643)
XLA Ops:
  8.7 2.3 collective-permute-start
  14.1 1.8 sine_multiply_fusion
  26.9 1.8 collective-permute-start.3
  35.1 2.2 convolution_bitcast_fusion.14
  37.3 2.3 convolution_bitcast_fusion.16
  39.6 7.1 multiply_convert_fusion
  46.7 2.0 multiply_convert_fusion.1
  48.7 4.6 collective-permute-start.4
  55.2 3.2 collective-permute-done.4
  58.3 4.7 collective-permute-done.5
  63.0 3.1 collective-permute-start.6
  67.6 2.2 convolution_bitcast_fusion.7
  69.8 2.2 convolution_bitcast_fusion.1
  75.5 7.0 add_convert_fusion.1
  82.5 2.8 collective-permute-start.8
  86.7 3.9 convolution_bitcast_fusion.35
  90.6 4.3 collective-permute-done.9
  95.0 4.6 collective-permute-start.10
  101.7 4.9 collective-permute-done.11
  111.0 13.4 %all_gather.3 = f32[2,2,256,128]{3,0,2,1:T(2,128)S(1)} all-gather(f32[2,2,32,128]{3,0,2,1:T(2,128)S(1)} %get-tuple-element.22), channel_id=1, replica_groups=mesh['slab'=32,'coil'=8] {'coil'}, dimensions={2}, use_global_device_ids=true | all-gather | bytes 589824 | tf_op jit(solution)/shard_map/all_gather | solution.py:144
  126.3 4.5 convolution_bitcast_fusion.33
  130.8 2.3 copy.252
  133.1 17.1 %all-to-all-start = ((f32[2,2,2,256,128]{4,1,2,0,3:T(2,128)}), f32[2,2,2,256,128]{4,1,2,0,3:T(2,128)S(1)}, u32[]{:S(2)}, u32[]{:S(2)}) async-start(f32[2,2,2,256,128]{4,1,2,0,3:T(2,128)} %copy.252), calls=%async_computation | async-start | bytes 2097152 | tf_op jit(solution)/shard_map/all_to_all | solution.py:111
  151.7 27.1 %all-to-all-done = f32[2,2,2,256,128]{4,1,2,0,3:T(2,128)S(1)} async-done(((f32[2,2,2,256,128]{4,1,2,0,3:T(2,128)}), f32[2,2,2,256,128]{4,1,2,0,3:T(2,128)S(1)}, u32[]{:S(2)}, u32[]{:S(2)}) %all-to-all-start) | async-done | bytes 1048608 | tf_op jit(solution)/shard_map/all_to_all | solution.py:111
  183.3 32.5 %all_to_all.108 = f32[2,2,64,8,128]{4,1,3,0,2:T(2,128)S(1)} all-to-all(f32[2,2,64,8,128]{4,1,3,0,2:T(2,128)S(1)} %copy.257), channel_id=1, replica_groups=mesh['slab'=32,'coil'=8] {'slab'}, dimensions={2} | all-to-all | bytes 2097152 | tf_op jit(solution)/shard_map/all_to_all | solution.py:118
  215.8 3.5 convolution_bitcast_fusion.30
  219.3 1.8 convolution_bitcast_fusion.29
  222.8 62.5 %all-reduce.32.cloned.1.call-done = f32[2,2,256,128]{3,0,2,1:T(2,128)} async-done(((f32[2,2,256,128]{3,0,2,1:T(2,128)}), f32[2,2,256,128]{3,0,2,1:T(2,128)}) %all-reduce.32.cloned.1.call-update) | async-done | bytes 524304 | tf_op jit(solution)/shard_map/psum | solution.py:124
  288.2 4.5 convolution_bitcast_fusion.27
  292.7 2.3 copy.263
  295.0 36.0 %all_to_all.109 = f32[2,2,2,256,128]{4,1,2,0,3:T(2,128)S(1)} all-to-all(f32[2,2,2,256,128]{4,1,2,0,3:T(2,128)} %copy.263), channel_id=1, replica_groups=mesh['slab'=32,'coil'=8] {'slab'}, dimensions={3} | all-to-all | bytes 2097152 | tf_op jit(solution)/shard_map/all_to_all | solution.py:111
  334.4 31.3 %all_to_all.110 = f32[2,2,64,8,128]{4,1,3,0,2:T(2,128)S(1)} all-to-all(f32[2,2,64,8,128]{4,1,3,0,2:T(2,128)S(1)} %copy.267), channel_id=1, replica_groups=mesh['slab'=32,'coil'=8] {'slab'}, dimensions={2} | all-to-all | bytes 2097152 | tf_op jit(solution)/shard_map/all_to_all | solution.py:118
  365.9 3.5 convolution_bitcast_fusion.24
  369.3 1.8 convolution_bitcast_fusion.23
  372.7 65.7 %all-reduce.34.cloned.1.call-done = f32[2,2,256,128]{3,0,2,1:T(2,128)} async-done(((f32[2,2,256,128]{3,0,2,1:T(2,128)}), f32[2,2,256,128]{3,0,2,1:T(2,128)}) %all-reduce.34.cloned.1.call-update) | async-done | bytes 524304 | tf_op jit(solution)/shard_map/psum | solution.py:124
  438.4 2.2 multiply_reduce_fusion.2
  440.6 75.6 %all-reduce.27 = (f32[1]{0:T(128)}, f32[1]{0:T(128)}) all-reduce(f32[1]{0:T(128)} %bitcast.253, f32[1]{0:T(128)} %bitcast.297), channel_id=1, replica_groups=mesh['slab'=32,'coil'=8] {'slab'}, use_global_device_ids=true, to_apply=%region_4.5 | all-reduce | flops 2 | bytes 16 | tf_op jit(solution)/shard_map/psum | solution.py:128
  517.4 2.2 multiply_reduce_fusion.1
  519.6 71.3 %psum.53 = f32[1]{0:T(128)} all-reduce(f32[1]{0:T(128)} %bitcast.299), channel_id=1, replica_groups=mesh['slab'=32,'coil'=8] {'slab'}, use_global_device_ids=true, to_apply=%region_11.12 | all-reduce | flops 1 | bytes 8 | tf_op jit(solution)/shard_map/psum | solution.py:128
  595.9 4.5 convolution_bitcast_fusion.21
  600.4 2.3 copy.273
  602.7 29.3 %all_to_all.111 = f32[2,2,2,256,128]{4,1,2,0,3:T(2,128)S(1)} all-to-all(f32[2,2,2,256,128]{4,1,2,0,3:T(2,128)} %copy.273), channel_id=1, replica_groups=mesh['slab'=32,'coil'=8] {'slab'}, dimensions={3} | all-to-all | bytes 2097152 | tf_op jit(solution)/shard_map/all_to_all | solution.py:111
  635.4 23.9 %all_to_all.112 = f32[2,2,64,8,128]{4,1,3,0,2:T(2,128)S(1)} all-to-all(f32[2,2,64,8,128]{4,1,3,0,2:T(2,128)S(1)} %copy.277), channel_id=1, replica_groups=mesh['slab'=32,'coil'=8] {'slab'}, dimensions={2} | all-to-all | bytes 2097152 | tf_op jit(solution)/shard_map/all_to_all | solution.py:118
  659.4 3.5 convolution_bitcast_fusion.18
  662.9 1.8 convolution_bitcast_fusion.17
  666.4 63.8 %all-reduce.36.cloned.1.call-done = f32[2,2,256,128]{3,0,2,1:T(2,128)} async-done(((f32[2,2,256,128]{3,0,2,1:T(2,128)}), f32[2,2,256,128]{3,0,2,1:T(2,128)}) %all-reduce.36.cloned.1.call-update) | async-done | bytes 524304 | tf_op jit(solution)/shard_map/psum | solution.py:124
  730.2 2.2 multiply_reduce_fusion
  732.3 75.7 %psum.55 = f32[1]{0:T(128)} all-reduce(f32[1]{0:T(128)} %bitcast.338), channel_id=1, replica_groups=mesh['slab'=32,'coil'=8] {'slab'}, use_global_device_ids=true, to_apply=%region_16.17 | all-reduce | flops 1 | bytes 8 | tf_op jit(solution)/shard_map/psum | solution.py:128
  (214 shorter events, 63.7 us)
Async XLA Ops:
  7.2 16.6 %copy-start = (f32[32,32]{1,0:T(8,128)S(1)}, f32[32,32]{1,0:T(8,128)}, u32[]{:S(2)}) copy-start(f32[32,32]{1,0:T(8,128)} %param.14) | copy-start | bytes 12292
  7.2 12.6 %copy-start.42 = (bf16[3,3,3,2,32]{4,3,2,1,0:T(2,128)(2,1)S(1)}, bf16[3,3,3,2,32]{4,3,2,1,0:T(2,128)(2,1)}, u32[]{:S(2)}) copy-start(bf16[3,3,3,2,32]{4,3,2,1,0:T(2,128)(2,1)} %param.13) | copy-start | bytes 10372
  8.1 13.5 %copy-start.17 = (bf16[2,2,32,128]{3,0,2,1:T(2,128)(2,1)}, bf16[2,2,32,128]{3,0,2,1:T(2,128)(2,1)S(1)}, u32[]{:S(2)}) copy-start(bf16[2,2,32,128]{3,0,2,1:T(2,128)(2,1)S(1)} %copy.460) | copy-start | bytes 98308
  8.7 16.0 %collective-permute-start = (bf16[2,1,32,128]{3,0,2,1:T(2,128)(2,1)}, bf16[2,1,32,128]{3,0,2,1:T(2,128)(2,1)}, u32[]{:S(2)}, u32[]{:S(2)}) collective-permute-start(bf16[2,1,32,128]{3,0,2,1:T(2,128)(2,1)} %get-tuple-element.76), channel_id=1, source_target_pairs={{0,8},{8,16},{16,24},{24,32},{32,40},{40,48},{48,56},{56,64},{64,7... | collective-permute-start | bytes 49160 | tf_op jit(solution)/shard_map/ppermute | solution.py:25
  11.0 13.7 %collective-permute-start.1 = (bf16[2,1,32,128]{3,0,2,1:T(2,128)(2,1)}, bf16[2,1,32,128]{3,0,2,1:T(2,128)(2,1)}, u32[]{:S(2)}, u32[]{:S(2)}) collective-permute-start(bf16[2,1,32,128]{3,0,2,1:T(2,128)(2,1)} %get-tuple-element.77), channel_id=1, source_target_pairs={{8,0},{16,8},{24,16},{32,24},{40,32},{48,40},{56,48},{64,56},{72,6... | collective-permute-start | bytes 49160 | tf_op jit(solution)/shard_map/ppermute | solution.py:27
  24.7 5.4 copy-start.18
  25.5 6.0 collective-permute-start.2
  26.9 5.7 copy-start.41
  26.9 4.7 collective-permute-start.3
  35.1 4.5 copy-start.51
  46.7 7.9 copy-start.15
  46.7 7.9 copy-start.40
  48.7 9.6 %collective-permute-start.4 = (bf16[32,1,32,128]{3,0,2,1:T(8,128)(2,1)S(1)}, bf16[32,1,32,128]{3,0,2,1:T(8,128)(2,1)S(1)}, u32[]{:S(2)}, u32[]{:S(2)}) collective-permute-start(bf16[32,1,32,128]{3,0,2,1:T(8,128)(2,1)S(1)} %get-tuple-element.54), channel_id=1, source_target_pairs={{0,8},{8,16},{16,24},{24,32},{32,40},{40,48},{48,56},{56,64},{64,7... | collective-permute-start | bytes 786440 | tf_op jit(solution)/shard_map/ppermute | solution.py:25
  53.3 9.7 %collective-permute-start.5 = (bf16[32,1,32,128]{3,0,2,1:T(8,128)(2,1)S(1)}, bf16[32,1,32,128]{3,0,2,1:T(8,128)(2,1)S(1)}, u32[]{:S(2)}, u32[]{:S(2)}) collective-permute-start(bf16[32,1,32,128]{3,0,2,1:T(8,128)(2,1)S(1)} %get-tuple-element.55), channel_id=1, source_target_pairs={{8,0},{16,8},{24,16},{32,24},{40,32},{48,40},{56,48},{64,56},{72,6... | collective-permute-start | bytes 786440 | tf_op jit(solution)/shard_map/ppermute | solution.py:27
  63.0 8.9 %collective-permute-start.6 = (bf16[32,4,1,128]{3,0,2,1:T(8,128)(2,1)S(1)}, bf16[32,4,1,128]{3,0,2,1:T(8,128)(2,1)S(1)}, u32[]{:S(2)}, u32[]{:S(2)}) collective-permute-start(bf16[32,4,1,128]{3,0,2,1:T(8,128)(2,1)S(1)} %get-tuple-element.40), channel_id=1, source_target_pairs={{0,1},{1,2},{2,3},{3,4},{4,5},{5,6},{6,7},{8,9},{9,10},{10,11},{11... | collective-permute-start | bytes 98312 | tf_op jit(solution)/shard_map/ppermute | solution.py:25
  66.1 5.9 collective-permute-start.7
  75.5 11.2 %copy-start.16 = (bf16[1,32,2,32,128]{4,1,0,3,2:T(8,128)(2,1)S(1)}, bf16[1,32,2,32,128]{4,1,0,3,2:T(8,128)(2,1)}, u32[]{:S(2)}) copy-start(bf16[1,32,2,32,128]{4,1,0,3,2:T(8,128)(2,1)} %copy-done.15) | copy-start | bytes 1572868
  75.5 11.2 %copy-start.53 = (bf16[1,1,3,2,32]{4,3,2,1,0:T(2,128)(2,1)S(1)}, bf16[1,1,3,2,32]{4,3,2,1,0:T(2,128)(2,1)}, u32[]{:S(2)}) copy-start(bf16[1,1,3,2,32]{4,3,2,1,0:T(2,128)(2,1)} %get-tuple-element.82) | copy-start | bytes 1156
  82.5 8.1 collective-permute-start.8
  85.3 9.6 %collective-permute-start.9 = (bf16[32,1,32,128]{3,0,2,1:T(8,128)(2,1)S(1)}, bf16[32,1,32,128]{3,0,2,1:T(8,128)(2,1)S(1)}, u32[]{:S(2)}, u32[]{:S(2)}) collective-permute-start(bf16[32,1,32,128]{3,0,2,1:T(8,128)(2,1)S(1)} %get-tuple-element.53), channel_id=1, source_target_pairs={{8,0},{16,8},{24,16},{32,24},{40,32},{48,40},{56,48},{64,56},{72,6... | collective-permute-start | bytes 786440 | tf_op jit(solution)/shard_map/ppermute | solution.py:27
  86.7 14.5 %copy-start.46 = (bf16[1,1,3,2,32]{4,3,2,1,0:T(2,128)(2,1)S(1)}, bf16[1,1,3,2,32]{4,3,2,1,0:T(2,128)(2,1)}, u32[]{:S(2)}) copy-start(bf16[1,1,3,2,32]{4,3,2,1,0:T(2,128)(2,1)} %get-tuple-element.85) | copy-start | bytes 1156
  86.7 14.7 %copy-start.50 = (bf16[3,2,32,1,1]{2,0,1,3,4:T(4,128)(2,1)S(1)}, bf16[3,2,32,1,1]{2,0,1,3,4:T(4,128)(2,1)}, u32[]{:S(2)}) copy-start(bf16[3,2,32,1,1]{2,0,1,3,4:T(4,128)(2,1)} %get-tuple-element.90) | copy-start | bytes 1156
  90.6 16.2 %copy-start.49 = (bf16[3,2,32,1,1]{2,0,1,3,4:T(4,128)(2,1)S(1)}, bf16[3,2,32,1,1]{2,0,1,3,4:T(4,128)(2,1)}, u32[]{:S(2)}) copy-start(bf16[3,2,32,1,1]{2,0,1,3,4:T(4,128)(2,1)} %get-tuple-element.92) | copy-start | bytes 1156
  95.0 6.7 collective-permute-start.10
  99.6 7.0 collective-permute-start.11
  101.1 6.1 copy-start.45
  101.4 6.1 copy-start.44
  101.6 6.0 copy-start.43
  101.6 6.2 copy-start.47
  101.6 6.5 copy-start.48
  107.9 17.0 %copy-start.2 = (f32[2,2,2,256,128]{4,3,2,1,0:T(8,128)S(1)}, f32[2,2,2,256,128]{4,3,2,1,0:T(8,128)}, u32[]{:S(2)}) copy-start(f32[2,2,2,256,128]{4,3,2,1,0:T(8,128)} %param.15) | copy-start | bytes 3145732
  109.8 15.4 %copy-start.12 = (f32[1,128,2,128]{3,1,2,0:T(8,128)S(1)}, f32[1,128,2,128]{3,1,2,0:T(8,128)}, u32[]{:S(2)}) copy-start(f32[1,128,2,128]{3,1,2,0:T(8,128)} %get-tuple-element.64) | copy-start | bytes 393220
  126.3 24.3 %copy-start.52 = (s32[64,8]{0,1:T(8,128)S(1)}, s32[64,8]{0,1:T(8,128)}, u32[]{:S(2)}) copy-start(s32[64,8]{0,1:T(8,128)} %param.17) | copy-start | bytes 6148
  133.1 45.7 %all-to-all-start = ((f32[2,2,2,256,128]{4,1,2,0,3:T(2,128)}), f32[2,2,2,256,128]{4,1,2,0,3:T(2,128)S(1)}, u32[]{:S(2)}, u32[]{:S(2)}) async-start(f32[2,2,2,256,128]{4,1,2,0,3:T(2,128)} %copy.252), calls=%async_computation | async-start | bytes 2097152 | tf_op jit(solution)/shard_map/all_to_all | solution.py:111
  150.2 135.2 %all-reduce.32.cloned.1.call-start = ((), (), s32[]{:S(2)}) async-start(), calls=%async_computation.6 | async-start | bytes 1048576 | tf_op jit(solution)/shard_map/psum | solution.py:124
  182.4 33.4 %copy-start.4 = (f32[1,256,2,256]{3,1,2,0:T(8,128)S(1)}, f32[1,256,2,256]{3,1,2,0:T(8,128)}, u32[]{:S(2)}) copy-start(f32[1,256,2,256]{3,1,2,0:T(8,128)} %get-tuple-element.46) | copy-start | bytes 1572868
  182.4 33.4 %copy-start.5 = (f32[1,256,2,256]{3,1,2,0:T(8,128)S(1)}, f32[1,256,2,256]{3,1,2,0:T(8,128)}, u32[]{:S(2)}) copy-start(f32[1,256,2,256]{3,1,2,0:T(8,128)} %get-tuple-element.57) | copy-start | bytes 1572868
  222.6 215.8 %all-reduce.34.cloned.1.call-start = ((), (), s32[]{:S(2)}) async-start(), calls=%async_computation.7 | async-start | bytes 1048576 | tf_op jit(solution)/shard_map/psum | solution.py:124
  295.0 36.3 %copy-start.27 = (f32[1,64,2,64]{3,1,2,0:T(8,128)S(1)}, f32[1,64,2,64]{3,1,2,0:T(8,128)}, u32[]{:S(2)}) copy-start(f32[1,64,2,64]{3,1,2,0:T(8,128)} %get-tuple-element.67) | copy-start | bytes 98308
  295.0 36.3 %copy-start.30 = (f32[1,64,2,64]{3,1,2,0:T(8,128)S(1)}, f32[1,64,2,64]{3,1,2,0:T(8,128)}, u32[]{:S(2)}) copy-start(f32[1,64,2,64]{3,1,2,0:T(8,128)} %get-tuple-element.74) | copy-start | bytes 98308
  369.3 69.0 %copy-start.3 = (f32[2,2,256,128]{3,0,2,1:T(2,128)S(1)}, f32[2,2,256,128]{3,0,2,1:T(2,128)}, u32[]{:S(2)}) copy-start(f32[2,2,256,128]{3,0,2,1:T(2,128)} %all-reduce.32.cloned.1.call-done) | copy-start | bytes 1572868
  372.7 357.5 %all-reduce.36.cloned.1.call-start = ((), (), s32[]{:S(2)}) async-start(), calls=%async_computation.8 | async-start | bytes 1048576 | tf_op jit(solution)/shard_map/psum | solution.py:124
  590.8 4.1 copy-start.14
  602.7 29.6 %copy-start.28 = (f32[1,64,2,64]{3,1,2,0:T(8,128)S(1)}, f32[1,64,2,64]{3,1,2,0:T(8,128)}, u32[]{:S(2)}) copy-start(f32[1,64,2,64]{3,1,2,0:T(8,128)} %get-tuple-element.67) | copy-start | bytes 98308
  602.7 29.6 %copy-start.31 = (f32[1,64,2,64]{3,1,2,0:T(8,128)S(1)}, f32[1,64,2,64]{3,1,2,0:T(8,128)}, u32[]{:S(2)}) copy-start(f32[1,64,2,64]{3,1,2,0:T(8,128)} %get-tuple-element.74) | copy-start | bytes 98308
  662.9 67.3 %copy-start.10 = (f32[2,2,256,128]{3,0,2,1:T(2,128)S(1)}, f32[2,2,256,128]{3,0,2,1:T(2,128)}, u32[]{:S(2)}) copy-start(f32[2,2,256,128]{3,0,2,1:T(2,128)} %copy-done.9) | copy-start | bytes 1572868
  662.9 148.6 %copy-start.1 = (f32[32,32]{1,0:T(8,128)S(1)}, f32[32,32]{1,0:T(8,128)}, u32[]{:S(2)}) copy-start(f32[32,32]{1,0:T(8,128)} %param.14) | copy-start | bytes 12292
  664.7 144.5 %copy-start.36 = (f32[2,2,32,128]{3,0,2,1:T(2,128)S(1)}, f32[2,2,32,128]{3,0,2,1:T(2,128)}, u32[]{:S(2)}) copy-start(f32[2,2,32,128]{3,0,2,1:T(2,128)} %get-tuple-element.23) | copy-start | bytes 196612
  (22 other events, 48.0 us)
Sparse Core Ops, SparseCore 0:
  222.7 62.5 all-reduce.31
  372.8 65.5 all-reduce.33
  666.4 63.7 all-reduce.35
where the time goes:
time: 823 us; the launch traced here: 818 us
  blocking collectives  389 us (47%)
  waiting for transfers between devices  236 us (29%)
  matrix products  65.1 us (8%)
  starting transfers between devices  45.3 us (6%)
  other arithmetic  43 us (5%)
  between operations  20.1 us (2%)
  local copies, waits for them, and re-layouts  19.8 us (2%)
    psum x3, blocking collectives, global_sums(): return lax.psum(values, 'slab')  223 us
    psum x3, waiting for transfers between devices, combine_coils(): return lax.psum(partial_value, 'coil')  192 us
    all_to_all x3, blocking collectives, coil_term(): lax.all_to_all(back, 'slab', split_axis=2, concat_axis=3, tiled=True)  87.7 us
    all_to_all x2, blocking collectives, coil_term(): lax.all_to_all(spectrum, 'slab', split_axis=3, concat_axis=2, tiled=True)  65.3 us
    all_to_all x1, waiting for transfers between devices, coil_term(): lax.all_to_all(spectrum, 'slab', split_axis=3, concat_axis=2, tiled=True)  27.1 us
    dot_general x27, matrix products, conv_layer(): jnp.einsum('aoc,czyx->aozyx', weights[depth_shift, row_shift], window, pr...  24.9 us
    dot_general x6, matrix products, along_rows(): jnp.einsum('pkqn,cqzny->cpzky', blocks, data, precision=HIGHEST_PRECISION)  23.9 us
    ppermute x6, starting transfers between devices, extended(): lax.ppermute(tail, axis, [(i, (i + 1) % count) for i in range(ends)])  18.8 us
  transfers between devices with their start and end apart: 16, of which 9 were waited for; matrix products, arithmetic and copies ran while one was open for 3% of the time, Pallas kernels for 0%

commit v1 on v0

--- a/solution.py
+++ b/solution.py
@@ -104,28 +104,38 @@
     return jnp.stack([real_part, imag_part])
 
 
-def coil_term(image_full, sens, kdata, weight, blocks, with_data):
-    forward_x, forward_y, forward_z, inverse_x, inverse_y, inverse_z = blocks
+def coil_term(image_full, sens, kdata_x, weight, blocks, with_data):
+    forward_y, forward_z, inverse_y, inverse_z = blocks
     coil_images = times_sens(sens, image_full)
-    spectrum = along_rows(along_last(coil_images, forward_x), forward_y)
+    spectrum = along_rows(coil_images, forward_y)
     pencils = lax.all_to_all(spectrum, "slab", split_axis=3, concat_axis=2, tiled=True)
     kspace = along_depth(pencils, forward_z)
     if with_data:
-        kspace = weight * (kdata - kspace)
+        kspace = weight * (kdata_x - kspace)
     else:
         kspace = weight * kspace
     back = along_depth(kspace, inverse_z)
     slabs = lax.all_to_all(back, "slab", split_axis=2, concat_axis=3, tiled=True)
-    images = along_last(along_rows(slabs, inverse_y), inverse_x)
+    images = along_rows(slabs, inverse_y)
     return times_conj(sens, images)
 
 
 def combine_coils(partial_value):
-    return lax.psum(partial_value, "coil")
+    count = lax.axis_size("coil")
+    pieces = lax.all_to_all(partial_value, "coil", split_axis=2, concat_axis=0, tiled=True)
+    pieces = pieces.reshape((count, partial_value.shape[0]) + pieces.shape[1:])
+    return jnp.sum(pieces, axis=0)
+
+
+def gather_rows(value):
+    return lax.all_gather(value, "coil", axis=2, tiled=True)
 
 
 def global_sums(values):
-    return lax.psum(values, "slab")
+    axes = ("slab", "coil")
+    count = lax.axis_size("slab") * lax.axis_size("coil")
+    spread = jnp.broadcast_to(values[None], (count,) + values.shape)
+    return jnp.sum(lax.all_to_all(spread, axes, split_axis=0, concat_axis=0, tiled=True), axis=0)
 
 
 def body(noisy, step_index, w_in, w_mid, w_out, time_weight, sens, kdata, mask):
@@ -141,32 +151,35 @@
     )
     noise_pred = conv_layer(mixed, w_out)
     estimate = (noisy - jnp.sqrt(1.0 - signal_level) * noise_pred) / jnp.sqrt(signal_level)
-    full_estimate = lax.all_gather(estimate, "coil", axis=2, tiled=True)
     depth_full = kdata.shape[2]
     rows_full = sens.shape[3]
     width = sens.shape[4]
-    rows_share = noisy.shape[2]
     blocks = (
-        dft_blocks(width, False),
         dft_blocks(rows_full, False),
         dft_blocks(depth_full, False),
-        dft_blocks(width, True),
         dft_blocks(rows_full, True),
         dft_blocks(depth_full, True),
     )
+    kdata_x = along_last(kdata, dft_blocks(width, True))
     weight = mask.astype(jnp.float32)[None, None, :, :, None]
 
     def operator(image, with_data):
-        return coil_term(image, sens, kdata, weight, blocks, with_data)
-
-    solution = full_estimate
-    residual = combine_coils(operator(full_estimate, True))
+        return combine_coils(
+            coil_term(gather_rows(image), sens, kdata_x, weight, blocks, with_data)
+        )
+
+    solution = estimate
+    residual = operator(estimate, True)
     direction = residual
-    norm_now = global_sums(jnp.stack([jnp.sum(residual * residual)]))[0]
+    norm_now = None
     for iteration in range(ITERS):
         final_turn = iteration + 1 == ITERS
-        image = combine_coils(operator(direction, False)) + REG_WEIGHT * direction
-        curvature = global_sums(jnp.stack([jnp.sum(direction * image)]))[0]
+        image = operator(direction, False) + REG_WEIGHT * direction
+        if norm_now is None:
+            sums = global_sums(jnp.stack([jnp.sum(residual * residual), jnp.sum(direction * image)]))
+            norm_now, curvature = sums[0], sums[1]
+        else:
+            curvature = global_sums(jnp.stack([jnp.sum(direction * image)]))[0]
         step_size = norm_now / curvature
         solution = solution + step_size * direction
         if not final_turn:
@@ -174,7 +187,7 @@
             norm_next = global_sums(jnp.stack([jnp.sum(residual * residual)]))[0]
             direction = residual + norm_next / norm_now * direction
             norm_now = norm_next
-    recon = lax.dynamic_slice_in_dim(solution, lax.axis_index("coil") * rows_share, rows_share, 2)
+    recon = solution
     next_sample = jnp.sqrt(prior_level) * recon + jnp.sqrt(1.0 - prior_level) * noise_pred
     return (recon, next_sample)
 

time: 823 us -> 542 us (0.66)
  the two profiles are of different devices: /device:TPU:0 before, /device:TPU:1 now
where the time goes in v1:
time: 542 us; the launch traced here: 536 us
  blocking collectives  268 us (49%)
  starting transfers between devices  69.5 us (13%)
  waiting for transfers between devices  59.4 us (11%)
  matrix products  57.7 us (11%)
  other arithmetic  40.4 us (7%)
  local copies, waits for them, and re-layouts  34.2 us (6%)
  between operations  7.03 us (1%)
    all_to_all x3, blocking collectives, coil_term(): lax.all_to_all(back, 'slab', split_axis=2, concat_axis=3, tiled=True)  93 us
    all_to_all x2, blocking collectives, coil_term(): lax.all_to_all(spectrum, 'slab', split_axis=3, concat_axis=2, tiled=True)  63.8 us
    all_to_all x2, blocking collectives, global_sums(): lax.all_to_all(spread, axes, split_axis=0, concat_axis=0, tiled=True)  39.3 us
    all_gather x3, blocking collectives, gather_rows(): return lax.all_gather(value, 'coil', axis=2, tiled=True)  39.2 us
    all_to_all x2, blocking collectives, combine_coils(): lax.all_to_all(partial_value, 'coil', split_axis=2, concat_axis=0, tiled=...  33 us
    ppermute x6, starting transfers between devices, extended(): lax.ppermute(tail, axis, [(i, (i + 1) % count) for i in range(ends)])  26.6 us
    dot_general x27, matrix products, conv_layer(): jnp.einsum('aoc,czyx->aozyx', weights[depth_shift, row_shift], window, pr...  25.7 us
    all_to_all x1, waiting for transfers between devices, coil_term(): lax.all_to_all(spectrum, 'slab', split_axis=3, concat_axis=2, tiled=True)  24 us
  transfers between devices with their start and end apart: 15, of which 8 were waited for; matrix products, arithmetic and copies ran while one was open for 4% of the time, Pallas kernels for 0%

profile of v1, /device:TPU:1, one launch (start us, length us, event | category | flops | bytes accessed | tf_op | source)
XLA Modules:
  0.0 536.4 jit_solution(5735750924494911319)
XLA Ops:
  1.7 3.9 collective-permute-start
  9.7 3.0 fusion.136
  16.0 4.0 collective-permute-start.2
  20.0 2.4 collective-permute-start.3
  27.6 2.3 convolution_bitcast_fusion.14
  29.9 2.3 convolution_bitcast_fusion.16
  32.2 7.1 %multiply_convert_fusion = (bf16[1,32,2,32,128]{4,1,0,3,2:T(8,128)(2,1)S(1)}, f32[1,32,2,32,128]{4,1,0,3,2:T(8,128)S(1)}) fusion(f32[3,32,2,32,128]{4,1,3,2,0:T(8,128)S(1)} %convolution_bitcast_fusion.9, f32[3,32,2,32,128]{4,1,3,2,0:T(8,128)S(1)} %convolution_bitcast_fusion.10, f32[3,32,2,32,128]{4,1,3,2,0:T(8,128)S(1)} %convolution_bitcast_fusion.11, ...), kind=kLoop, calls=%fused_computation.180 | loop fusion | flops 8388608 | bytes 39322112 | tf_op jit(solution)/shard_map/convert_element_type | solution.py:148
  41.4 4.3 collective-permute-start.4
  47.5 2.8 collective-permute-done.4
  50.4 4.1 collective-permute-done.5
  54.5 4.9 collective-permute-start.6
  59.4 2.1 collective-permute-start.7
  61.5 2.2 convolution_bitcast_fusion.7
  63.7 2.2 convolution_bitcast_fusion.1
  69.4 7.6 %add_convert_fusion.1 = (bf16[32,2,32,128]{3,0,2,1:T(8,128)(2,1)S(1)}, f32[1,32,2,32,128]{4,1,3,2,0:T(8,128)}) fusion(bf16[32,2,32,128]{3,0,2,1:T(8,128)(2,1)S(1)} %multiply_convert_fusion.1, f32[3,32,2,32,128]{4,1,3,2,0:T(8,128)S(1)} %convolution_bitcast_fusion, f32[3,32,2,32,128]{4,1,3,2,0:T(8,128)} %convolution_bitcast_fusion.1, ...), kind=kLoop, calls=%fused_computation.179 | loop fusion | flops 8650752 | bytes 39845888 | tf_op jit(solution)/shard_map/convert_element_type | solution.py:149
  77.1 3.1 collective-permute-start.8
  81.5 4.4 convolution_bitcast_fusion.30
  85.9 3.0 collective-permute-done.9
  88.9 6.4 %collective-permute-start.10 = (bf16[32,4,1,128]{3,0,2,1:T(8,128)(2,1)S(1)}, bf16[32,4,1,128]{3,0,2,1:T(8,128)(2,1)S(1)}, u32[]{:S(2)}, u32[]{:S(2)}) collective-permute-start(bf16[32,4,1,128]{3,0,2,1:T(8,128)(2,1)S(1)} %get-tuple-element.42), channel_id=1, source_target_pairs={{0,1},{1,2},{2,3},{3,4},{4,5},{5,6},{6,7},{8,9},{9,10},{10,11},{11... | collective-permute-start | bytes 98312 | tf_op jit(solution)/shard_map/ppermute | solution.py:25
  95.3 2.1 collective-permute-start.11
  97.9 2.6 collective-permute-done.11
  104.9 11.1 %all_gather.9 = f32[2,2,256,128]{3,0,2,1:T(2,128)S(1)} all-gather(f32[2,2,32,128]{3,0,2,1:T(2,128)S(1)} %get-tuple-element.26), channel_id=1, replica_groups=mesh['slab'=32,'coil'=8] {'coil'}, dimensions={2}, use_global_device_ids=true | all-gather | bytes 589824 | tf_op jit(solution)/shard_map/all_gather | solution.py:131
  121.2 3.9 convolution_bitcast_fusion.28
  125.1 2.3 copy.624
  127.3 17.4 %all-to-all-start = ((f32[2,2,2,256,128]{4,1,2,0,3:T(2,128)}), f32[2,2,2,256,128]{4,1,2,0,3:T(2,128)}, u32[]{:S(2)}, u32[]{:S(2)}) async-start(f32[2,2,2,256,128]{4,1,2,0,3:T(2,128)} %copy.624), calls=%async_computation | async-start | bytes 2097152 | tf_op jit(solution)/shard_map/all_to_all | solution.py:111
  147.7 24.0 %all-to-all-done = f32[2,2,2,256,128]{4,1,2,0,3:T(2,128)} async-done(((f32[2,2,2,256,128]{4,1,2,0,3:T(2,128)}), f32[2,2,2,256,128]{4,1,2,0,3:T(2,128)}, u32[]{:S(2)}, u32[]{:S(2)}) %all-to-all-start) | async-done | bytes 1048608 | tf_op jit(solution)/shard_map/all_to_all | solution.py:111
  176.6 30.9 %all_to_all.162 = f32[2,2,64,8,128]{4,1,3,0,2:T(2,128)S(1)} all-to-all(f32[2,2,64,8,128]{4,1,3,0,2:T(2,128)S(1)} %copy.628), channel_id=1, replica_groups=mesh['slab'=32,'coil'=8] {'slab'}, dimensions={2} | all-to-all | bytes 2097152 | tf_op jit(solution)/shard_map/all_to_all | solution.py:118
  207.5 3.5 convolution_bitcast_fusion.25
  214.1 16.9 %all_to_all.163 = f32[2,2,256,128]{3,1,0,2:T(2,128)} all-to-all(f32[2,2,256,128]{3,1,0,2:T(2,128)} %copy.632), channel_id=1, replica_groups=mesh['slab'=32,'coil'=8] {'coil'}, dimensions={2} | all-to-all | bytes 1048576 | tf_op jit(solution)/shard_map/all_to_all | solution.py:125
  232.3 14.2 %all_gather.10 = f32[2,2,256,128]{3,1,0,2:T(2,128)S(1)} all-gather(f32[2,2,32,128]{3,1,0,2:T(2,128)S(1)} %reduce_sum.146), channel_id=1, replica_groups=mesh['slab'=32,'coil'=8] {'coil'}, dimensions={2}, use_global_device_ids=true | all-gather | bytes 589824 | tf_op jit(solution)/shard_map/all_gather | solution.py:131
  251.4 4.0 convolution_bitcast_fusion.24
  255.4 2.2 copy.635
  257.6 32.5 %all_to_all.164 = f32[2,2,2,256,128]{4,1,2,0,3:T(2,128)S(1)} all-to-all(f32[2,2,2,256,128]{4,1,2,0,3:T(2,128)} %copy.635), channel_id=1, replica_groups=mesh['slab'=32,'coil'=8] {'slab'}, dimensions={3} | all-to-all | bytes 2097152 | tf_op jit(solution)/shard_map/all_to_all | solution.py:111
  293.6 30.9 %all_to_all.165 = f32[2,2,64,8,128]{4,1,3,0,2:T(2,128)S(1)} all-to-all(f32[2,2,64,8,128]{4,1,3,0,2:T(2,128)S(1)} %copy.639), channel_id=1, replica_groups=mesh['slab'=32,'coil'=8] {'slab'}, dimensions={2} | all-to-all | bytes 2097152 | tf_op jit(solution)/shard_map/all_to_all | solution.py:118
  324.6 3.5 convolution_bitcast_fusion.21
  331.2 7.4 %all-to-all-start.5 = ((f32[2,2,256,128]{3,1,0,2:T(2,128)}), f32[2,2,256,128]{3,1,0,2:T(2,128)}, u32[]{:S(2)}, u32[]{:S(2)}) async-start(f32[2,2,256,128]{3,1,0,2:T(2,128)} %copy.643), calls=%async_computation.5 | async-start | bytes 1048576 | tf_op jit(solution)/shard_map/all_to_all | solution.py:125
  339.4 8.8 %all-to-all-done.5 = f32[2,2,256,128]{3,1,0,2:T(2,128)} async-done(((f32[2,2,256,128]{3,1,0,2:T(2,128)}), f32[2,2,256,128]{3,1,0,2:T(2,128)}, u32[]{:S(2)}, u32[]{:S(2)}) %all-to-all-start.5) | async-done | bytes 524320 | tf_op jit(solution)/shard_map/all_to_all | solution.py:125
  351.4 20.0 %all_to_all.166 = f32[256,1,2]{2,1,0:T(1,128)} all-to-all(f32[256,1,2]{2,1,0:T(1,128)S(1)} %broadcast_in_dim.6), channel_id=1, replica_groups=mesh['slab'=32,'coil'=8] {'slab','coil'}, dimensions={0} | all-to-all | bytes 4096 | tf_op jit(solution)/shard_map/all_to_all | solution.py:138
  375.9 19.2 %all_to_all.167 = f32[256,1,1]{2,1,0:T(1,128)} all-to-all(f32[256,1,1]{2,1,0:T(1,128)S(1)} %broadcast_in_dim.7), channel_id=1, replica_groups=mesh['slab'=32,'coil'=8] {'slab','coil'}, dimensions={0} | all-to-all | bytes 2048 | tf_op jit(solution)/shard_map/all_to_all | solution.py:138
  398.4 13.9 %all_gather.11 = f32[2,2,256,128]{3,0,2,1:T(2,128)S(1)} all-gather(f32[2,2,32,128]{3,0,2,1:T(2,128)S(1)} %multiply_add_fusion.5), channel_id=1, replica_groups=mesh['slab'=32,'coil'=8] {'coil'}, dimensions={2}, use_global_device_ids=true | all-gather | bytes 589824 | tf_op jit(solution)/shard_map/all_gather | solution.py:131
  417.5 4.0 convolution_bitcast_fusion.20
  421.5 2.2 copy.654
  423.8 31.3 %all_to_all.168 = f32[2,2,2,256,128]{4,1,2,0,3:T(2,128)S(1)} all-to-all(f32[2,2,2,256,128]{4,1,2,0,3:T(2,128)} %copy.654), channel_id=1, replica_groups=mesh['slab'=32,'coil'=8] {'slab'}, dimensions={3} | all-to-all | bytes 2097152 | tf_op jit(solution)/shard_map/all_to_all | solution.py:111
  458.5 31.2 %all_to_all.169 = f32[2,2,64,8,128]{4,1,3,0,2:T(2,128)S(1)} all-to-all(f32[2,2,64,8,128]{4,1,3,0,2:T(2,128)S(1)} %copy.658), channel_id=1, replica_groups=mesh['slab'=32,'coil'=8] {'slab'}, dimensions={2} | all-to-all | bytes 2097152 | tf_op jit(solution)/shard_map/all_to_all | solution.py:118
  489.8 3.5 convolution_bitcast_fusion.17
  493.8 16.0 %all_to_all.170 = f32[2,2,256,128]{3,1,0,2:T(2,128)S(1)} all-to-all(f32[2,2,256,128]{3,1,0,2:T(2,128)S(1)} %copy.662), channel_id=1, replica_groups=mesh['slab'=32,'coil'=8] {'coil'}, dimensions={2} | all-to-all | bytes 1048576 | tf_op jit(solution)/shard_map/all_to_all | solution.py:125
  512.1 7.4 %all-to-all-start.11 = ((f32[256,1,1]{2,1,0:T(1,128)}), f32[256,1,1]{2,1,0:T(1,128)S(1)}, u32[]{:S(2)}, u32[]{:S(2)}) async-start(f32[256,1,1]{2,1,0:T(1,128)} %broadcast_in_dim.8), calls=%async_computation.11 | async-start | bytes 262144 | tf_op jit(solution)/shard_map/all_to_all | solution.py:138
  519.7 12.8 %all-to-all-done.11 = f32[256,1,1]{2,1,0:T(1,128)S(1)} async-done(((f32[256,1,1]{2,1,0:T(1,128)}), f32[256,1,1]{2,1,0:T(1,128)S(1)}, u32[]{:S(2)}, u32[]{:S(2)}) %all-to-all-start.11) | async-done | bytes 1056 | tf_op jit(solution)/shard_map/all_to_all | solution.py:138
  (181 shorter events, 77.1 us)
Async XLA Ops:
  0.6 145.1 %copy-start = (f32[2,2,64,8,128]{4,3,2,1,0:T(8,128)S(1)}, f32[2,2,64,8,128]{4,3,2,1,0:T(8,128)}, u32[]{:S(2)}) copy-start(f32[2,2,64,8,128]{4,3,2,1,0:T(8,128)} %param.16) | copy-start | bytes 3145732
  0.6 12.1 %copy-start.25 = (bf16[3,3,3,2,32]{4,3,2,1,0:T(2,128)(2,1)S(1)}, bf16[3,3,3,2,32]{4,3,2,1,0:T(2,128)(2,1)}, u32[]{:S(2)}) copy-start(bf16[3,3,3,2,32]{4,3,2,1,0:T(2,128)(2,1)} %param.13) | copy-start | bytes 10372
  1.7 14.3 %collective-permute-start = (bf16[2,1,32,128]{3,0,2,1:T(2,128)(2,1)S(1)}, bf16[2,1,32,128]{3,0,2,1:T(2,128)(2,1)S(1)}, u32[]{:S(2)}, u32[]{:S(2)}) collective-permute-start(bf16[2,1,32,128]{3,0,2,1:T(2,128)(2,1)S(1)} %get-tuple-element.78), channel_id=1, source_target_pairs={{0,8},{8,16},{16,24},{24,32},{32,40},{40,48},{48,56},{56,64},{64,7... | collective-permute-start | bytes 49160 | tf_op jit(solution)/shard_map/ppermute | solution.py:25
  5.6 10.3 %collective-permute-start.1 = (bf16[2,1,32,128]{3,0,2,1:T(2,128)(2,1)S(1)}, bf16[2,1,32,128]{3,0,2,1:T(2,128)(2,1)S(1)}, u32[]{:S(2)}, u32[]{:S(2)}) collective-permute-start(bf16[2,1,32,128]{3,0,2,1:T(2,128)(2,1)S(1)} %get-tuple-element.79), channel_id=1, source_target_pairs={{8,0},{16,8},{24,16},{32,24},{40,32},{48,40},{56,48},{64,56},{72,6... | collective-permute-start | bytes 49160 | tf_op jit(solution)/shard_map/ppermute | solution.py:27
  9.6 3.7 copy-start.17
  12.7 1.9 copy-start.23
  13.3 9.2 %copy-start.24 = (bf16[3,3,3,32,2]{3,4,2,1,0:T(2,128)(2,1)S(1)}, bf16[3,3,3,32,2]{3,4,2,1,0:T(2,128)(2,1)}, u32[]{:S(2)}) copy-start(bf16[3,3,3,32,2]{3,4,2,1,0:T(2,128)(2,1)} %param.11) | copy-start | bytes 10372
  16.0 7.7 %collective-permute-start.2 = (bf16[2,4,1,128]{3,0,2,1:T(2,128)(2,1)S(1)}, bf16[2,4,1,128]{3,0,2,1:T(2,128)(2,1)S(1)}, u32[]{:S(2)}, u32[]{:S(2)}) collective-permute-start(bf16[2,4,1,128]{3,0,2,1:T(2,128)(2,1)S(1)} %get-tuple-element.74), channel_id=1, source_target_pairs={{0,1},{1,2},{2,3},{3,4},{4,5},{5,6},{6,7},{8,9},{9,10},{10,11},{11... | collective-permute-start | bytes 6152 | tf_op jit(solution)/shard_map/ppermute | solution.py:25
  20.0 4.9 collective-permute-start.3
  27.6 4.7 copy-start.1
  27.6 4.7 copy-start.26
  39.3 7.6 %copy-start.5 = (bf16[1,32,2,32,128]{4,1,0,3,2:T(8,128)(2,1)}, bf16[1,32,2,32,128]{4,1,0,3,2:T(8,128)(2,1)S(1)}, u32[]{:S(2)}) copy-start(bf16[1,32,2,32,128]{4,1,0,3,2:T(8,128)(2,1)S(1)} %get-tuple-element.30) | copy-start | bytes 1572868
  39.3 7.6 %copy-start.22 = (bf16[3,3,3,32,32]{4,3,2,1,0:T(8,128)(2,1)S(1)}, bf16[3,3,3,32,32]{4,3,2,1,0:T(8,128)(2,1)}, u32[]{:S(2)}) copy-start(bf16[3,3,3,32,32]{4,3,2,1,0:T(8,128)(2,1)} %param.12) | copy-start | bytes 165892
  41.4 9.0 %collective-permute-start.4 = (bf16[32,1,32,128]{3,0,2,1:T(8,128)(2,1)S(1)}, bf16[32,1,32,128]{3,0,2,1:T(8,128)(2,1)S(1)}, u32[]{:S(2)}, u32[]{:S(2)}) collective-permute-start(bf16[32,1,32,128]{3,0,2,1:T(8,128)(2,1)S(1)} %get-tuple-element.60), channel_id=1, source_target_pairs={{0,8},{8,16},{16,24},{24,32},{32,40},{40,48},{48,56},{56,64},{64,7... | collective-permute-start | bytes 786440 | tf_op jit(solution)/shard_map/ppermute | solution.py:25
  45.6 8.8 %collective-permute-start.5 = (bf16[32,1,32,128]{3,0,2,1:T(8,128)(2,1)S(1)}, bf16[32,1,32,128]{3,0,2,1:T(8,128)(2,1)S(1)}, u32[]{:S(2)}, u32[]{:S(2)}) collective-permute-start(bf16[32,1,32,128]{3,0,2,1:T(8,128)(2,1)S(1)} %get-tuple-element.61), channel_id=1, source_target_pairs={{8,0},{16,8},{24,16},{32,24},{40,32},{48,40},{56,48},{64,56},{72,6... | collective-permute-start | bytes 786440 | tf_op jit(solution)/shard_map/ppermute | solution.py:27
  54.5 11.4 %collective-permute-start.6 = (bf16[32,4,1,128]{3,0,2,1:T(8,128)(2,1)S(1)}, bf16[32,4,1,128]{3,0,2,1:T(8,128)(2,1)S(1)}, u32[]{:S(2)}, u32[]{:S(2)}) collective-permute-start(bf16[32,4,1,128]{3,0,2,1:T(8,128)(2,1)S(1)} %get-tuple-element.46), channel_id=1, source_target_pairs={{0,1},{1,2},{2,3},{3,4},{4,5},{5,6},{6,7},{8,9},{9,10},{10,11},{11... | collective-permute-start | bytes 98312 | tf_op jit(solution)/shard_map/ppermute | solution.py:25
  59.4 6.5 %collective-permute-start.7 = (bf16[32,4,1,128]{3,0,2,1:T(8,128)(2,1)S(1)}, bf16[32,4,1,128]{3,0,2,1:T(8,128)(2,1)S(1)}, u32[]{:S(2)}, u32[]{:S(2)}) collective-permute-start(bf16[32,4,1,128]{3,0,2,1:T(8,128)(2,1)S(1)} %get-tuple-element.47), channel_id=1, source_target_pairs={{1,0},{2,1},{3,2},{4,3},{5,4},{6,5},{7,6},{9,8},{10,9},{11,10},{12... | collective-permute-start | bytes 98312 | tf_op jit(solution)/shard_map/ppermute | solution.py:27
  69.4 12.1 %copy-start.28 = (bf16[1,1,3,2,32]{4,3,2,1,0:T(2,128)(2,1)S(1)}, bf16[1,1,3,2,32]{4,3,2,1,0:T(2,128)(2,1)}, u32[]{:S(2)}) copy-start(bf16[1,1,3,2,32]{4,3,2,1,0:T(2,128)(2,1)} %get-tuple-element.84) | copy-start | bytes 1156
  77.1 8.8 %collective-permute-start.8 = (bf16[32,1,32,128]{3,0,2,1:T(8,128)(2,1)S(1)}, bf16[32,1,32,128]{3,0,2,1:T(8,128)(2,1)S(1)}, u32[]{:S(2)}, u32[]{:S(2)}) collective-permute-start(bf16[32,1,32,128]{3,0,2,1:T(8,128)(2,1)S(1)} %get-tuple-element.58), channel_id=1, source_target_pairs={{0,8},{8,16},{16,24},{24,32},{32,40},{40,48},{48,56},{56,64},{64,7... | collective-permute-start | bytes 786440 | tf_op jit(solution)/shard_map/ppermute | solution.py:25
  80.2 8.7 %collective-permute-start.9 = (bf16[32,1,32,128]{3,0,2,1:T(8,128)(2,1)S(1)}, bf16[32,1,32,128]{3,0,2,1:T(8,128)(2,1)S(1)}, u32[]{:S(2)}, u32[]{:S(2)}) collective-permute-start(bf16[32,1,32,128]{3,0,2,1:T(8,128)(2,1)S(1)} %get-tuple-element.59), channel_id=1, source_target_pairs={{8,0},{16,8},{24,16},{32,24},{40,32},{48,40},{56,48},{64,56},{72,6... | collective-permute-start | bytes 786440 | tf_op jit(solution)/shard_map/ppermute | solution.py:27
  88.9 9.0 %collective-permute-start.10 = (bf16[32,4,1,128]{3,0,2,1:T(8,128)(2,1)S(1)}, bf16[32,4,1,128]{3,0,2,1:T(8,128)(2,1)S(1)}, u32[]{:S(2)}, u32[]{:S(2)}) collective-permute-start(bf16[32,4,1,128]{3,0,2,1:T(8,128)(2,1)S(1)} %get-tuple-element.42), channel_id=1, source_target_pairs={{0,1},{1,2},{2,3},{3,4},{4,5},{5,6},{6,7},{8,9},{9,10},{10,11},{11... | collective-permute-start | bytes 98312 | tf_op jit(solution)/shard_map/ppermute | solution.py:25
  95.3 5.2 collective-permute-start.11
  101.0 2.7 copy-start.20
  103.7 17.5 %copy-start.3 = (f32[1,256,2,256]{3,1,2,0:T(8,128)S(1)}, f32[1,256,2,256]{3,1,2,0:T(8,128)}, u32[]{:S(2)}) copy-start(f32[1,256,2,256]{3,1,2,0:T(8,128)} %get-tuple-element.53) | copy-start | bytes 1572868
  104.9 12.3 %copy-start.18 = (f32[2,2,32,128]{3,0,2,1:T(2,128)}, f32[2,2,32,128]{3,0,2,1:T(2,128)S(1)}, u32[]{:S(2)}) copy-start(f32[2,2,32,128]{3,0,2,1:T(2,128)S(1)} %get-tuple-element.26) | copy-start | bytes 196612
  121.2 23.5 %copy-start.27 = (s32[64,8]{0,1:T(8,128)S(1)}, s32[64,8]{0,1:T(8,128)}, u32[]{:S(2)}) copy-start(s32[64,8]{0,1:T(8,128)} %param.17) | copy-start | bytes 6148
  127.3 44.4 %all-to-all-start = ((f32[2,2,2,256,128]{4,1,2,0,3:T(2,128)}), f32[2,2,2,256,128]{4,1,2,0,3:T(2,128)}, u32[]{:S(2)}, u32[]{:S(2)}) async-start(f32[2,2,2,256,128]{4,1,2,0,3:T(2,128)} %copy.624), calls=%async_computation | async-start | bytes 2097152 | tf_op jit(solution)/shard_map/all_to_all | solution.py:111
  145.6 27.8 %copy-start.9 = (f32[1,64,2,64]{3,1,2,0:T(8,128)}, f32[1,64,2,64]{3,1,2,0:T(8,128)S(1)}, u32[]{:S(2)}) copy-start(f32[1,64,2,64]{3,1,2,0:T(8,128)S(1)} %get-tuple-element.67) | copy-start | bytes 98308
  145.6 27.8 %copy-start.12 = (f32[1,64,2,64]{3,1,2,0:T(8,128)}, f32[1,64,2,64]{3,1,2,0:T(8,128)S(1)}, u32[]{:S(2)}) copy-start(f32[1,64,2,64]{3,1,2,0:T(8,128)S(1)} %get-tuple-element.76) | copy-start | bytes 98308
  145.7 29.0 %copy-start.6 = (f32[1,64,2,64]{3,1,2,0:T(8,128)}, f32[1,64,2,64]{3,1,2,0:T(8,128)S(1)}, u32[]{:S(2)}) copy-start(f32[1,64,2,64]{3,1,2,0:T(8,128)S(1)} %get-tuple-element.77) | copy-start | bytes 98308
  171.8 1.6 copy-start.4
  175.8 31.8 %copy-start.2 = (f32[1,256,2,256]{3,1,2,0:T(8,128)S(1)}, f32[1,256,2,256]{3,1,2,0:T(8,128)}, u32[]{:S(2)}) copy-start(f32[1,256,2,256]{3,1,2,0:T(8,128)} %get-tuple-element.63) | copy-start | bytes 1572868
  257.6 32.8 %copy-start.10 = (f32[1,64,2,64]{3,1,2,0:T(8,128)S(1)}, f32[1,64,2,64]{3,1,2,0:T(8,128)}, u32[]{:S(2)}) copy-start(f32[1,64,2,64]{3,1,2,0:T(8,128)} %copy-done.9) | copy-start | bytes 98308
  257.6 32.8 %copy-start.13 = (f32[1,64,2,64]{3,1,2,0:T(8,128)S(1)}, f32[1,64,2,64]{3,1,2,0:T(8,128)}, u32[]{:S(2)}) copy-start(f32[1,64,2,64]{3,1,2,0:T(8,128)} %copy-done.12) | copy-start | bytes 98308
  290.2 1.5 copy-start.7
  331.2 16.9 %all-to-all-start.5 = ((f32[2,2,256,128]{3,1,0,2:T(2,128)}), f32[2,2,256,128]{3,1,0,2:T(2,128)}, u32[]{:S(2)}, u32[]{:S(2)}) async-start(f32[2,2,256,128]{3,1,0,2:T(2,128)} %copy.643), calls=%async_computation.5 | async-start | bytes 1048576 | tf_op jit(solution)/shard_map/all_to_all | solution.py:125
  398.4 15.1 %copy-start.15 = (f32[2,2,32,128]{3,0,2,1:T(2,128)}, f32[2,2,32,128]{3,0,2,1:T(2,128)S(1)}, u32[]{:S(2)}) copy-start(f32[2,2,32,128]{3,0,2,1:T(2,128)S(1)} %multiply_add_fusion.5) | copy-start | bytes 196612
  423.8 31.6 %copy-start.11 = (f32[1,64,2,64]{3,1,2,0:T(8,128)S(1)}, f32[1,64,2,64]{3,1,2,0:T(8,128)}, u32[]{:S(2)}) copy-start(f32[1,64,2,64]{3,1,2,0:T(8,128)} %copy-done.9) | copy-start | bytes 98308
  423.8 31.6 %copy-start.14 = (f32[1,64,2,64]{3,1,2,0:T(8,128)S(1)}, f32[1,64,2,64]{3,1,2,0:T(8,128)}, u32[]{:S(2)}) copy-start(f32[1,64,2,64]{3,1,2,0:T(8,128)} %copy-done.12) | copy-start | bytes 98308
  455.1 1.5 copy-start.8
  493.3 16.8 %copy-start.16 = (f32[2,2,32,128]{3,0,2,1:T(2,128)S(1)}, f32[2,2,32,128]{3,0,2,1:T(2,128)}, u32[]{:S(2)}) copy-start(f32[2,2,32,128]{3,0,2,1:T(2,128)} %copy-done.15) | copy-start | bytes 196612
  493.3 41.5 %copy-start.19 = (f32[2,2,32,128]{3,0,2,1:T(2,128)S(1)}, f32[2,2,32,128]{3,0,2,1:T(2,128)}, u32[]{:S(2)}) copy-start(f32[2,2,32,128]{3,0,2,1:T(2,128)} %copy-done.18) | copy-start | bytes 196612
  493.3 41.5 %copy-start.21 = (f32[2,2,32,128]{3,0,2,1:T(2,128)S(1)}, f32[2,2,32,128]{3,0,2,1:T(2,128)}, u32[]{:S(2)}) copy-start(f32[2,2,32,128]{3,0,2,1:T(2,128)} %get-tuple-element.27) | copy-start | bytes 196612
  512.1 20.4 %all-to-all-start.11 = ((f32[256,1,1]{2,1,0:T(1,128)}), f32[256,1,1]{2,1,0:T(1,128)S(1)}, u32[]{:S(2)}, u32[]{:S(2)}) async-start(f32[256,1,1]{2,1,0:T(1,128)} %broadcast_in_dim.8), calls=%async_computation.11 | async-start | bytes 262144 | tf_op jit(solution)/shard_map/all_to_all | solution.py:138

commit v2 on v1

--- a/solution.py
+++ b/solution.py
@@ -108,14 +108,18 @@
     forward_y, forward_z, inverse_y, inverse_z = blocks
     coil_images = times_sens(sens, image_full)
     spectrum = along_rows(coil_images, forward_y)
-    pencils = lax.all_to_all(spectrum, "slab", split_axis=3, concat_axis=2, tiled=True)
+    pencils = lax.all_to_all(
+        spectrum.astype(jnp.bfloat16), "slab", split_axis=3, concat_axis=2, tiled=True
+    ).astype(jnp.float32)
     kspace = along_depth(pencils, forward_z)
     if with_data:
         kspace = weight * (kdata_x - kspace)
     else:
         kspace = weight * kspace
     back = along_depth(kspace, inverse_z)
-    slabs = lax.all_to_all(back, "slab", split_axis=2, concat_axis=3, tiled=True)
+    slabs = lax.all_to_all(
+        back.astype(jnp.bfloat16), "slab", split_axis=2, concat_axis=3, tiled=True
+    ).astype(jnp.float32)
     images = along_rows(slabs, inverse_y)
     return times_conj(sens, images)
 

time: 542 us -> 463 us (0.85)
  blocking collectives: 268 us -> 213 us
  waiting for transfers between devices: 59.4 us -> 49.8 us
  matrix products: 57.7 us -> 50 us
    all_to_all x5, blocking collectives: 157 us -> 103 us  [the longest x3 60.9 us: coil_term(): lax.all_to_all(back.astype(jnp.bfloat16), 'slab', split_axis=2, concat_ax...]
    all_to_all x1, waiting for transfers between devices: 24 us -> 13.7 us  [coil_term(): lax.all_to_all(spectrum.astype(jnp.bfloat16), 'slab', split_axis=3, conca...]
    transpose x6 -> x0, local copies, waits for them, and re-layouts: 9.18 us -> none  [the longest x3 6.74 us: along_rows(): jnp.einsum('pkqn,cqzny->cpzky', blocks, data, precision=HIGHEST_PRECISION)]
    convert_element_type x0 -> x6, local copies, waits for them, and re-layouts: none -> 7.73 us  [the longest x3 6.11 us: coil_term(): spectrum.astype(jnp.bfloat16)]
    dot_general x6, matrix products: 22.4 us -> 15.2 us  [along_rows(): jnp.einsum('pkqn,cqzny->cpzky', blocks, data, precision=HIGHEST_PRECISION)]
  transfers between devices with their start and end apart: 15 -> 15, of which waited for: 8 -> 8; matrix products, arithmetic and copies ran while one was open for 4% -> 5% of each run, Pallas kernels for 0% -> 0%
where the time goes in v2:
time: 463 us; the launch traced here: 458 us
  blocking collectives  213 us (46%)
  starting transfers between devices  67.4 us (15%)
  matrix products  50 us (11%)
  waiting for transfers between devices  49.8 us (11%)
  other arithmetic  40.4 us (9%)
  local copies, waits for them, and re-layouts  31 us (7%)
  between operations  6.82 us (1%)
    all_to_all x3, blocking collectives, coil_term(): lax.all_to_all(back.astype(jnp.bfloat16), 'slab', split_axis=2, concat_ax...  60.9 us
    all_to_all x2, blocking collectives, coil_term(): lax.all_to_all(spectrum.astype(jnp.bfloat16), 'slab', split_axis=3, conca...  41.9 us
    all_gather x3, blocking collectives, gather_rows(): return lax.all_gather(value, 'coil', axis=2, tiled=True)  39.2 us
    all_to_all x2, blocking collectives, global_sums(): lax.all_to_all(spread, axes, split_axis=0, concat_axis=0, tiled=True)  38.7 us
    all_to_all x2, blocking collectives, combine_coils(): lax.all_to_all(partial_value, 'coil', split_axis=2, concat_axis=0, tiled=...  32 us
    dot_general x27, matrix products, conv_layer(): jnp.einsum('aoc,czyx->aozyx', weights[depth_shift, row_shift], window, pr...  25.7 us
    ppermute x6, starting transfers between devices, extended(): lax.ppermute(tail, axis, [(i, (i + 1) % count) for i in range(ends)])  25.7 us
    all_to_all x1, starting transfers between devices, coil_term(): lax.all_to_all(spectrum.astype(jnp.bfloat16), 'slab', split_axis=3, conca...  17.5 us
  transfers between devices with their start and end apart: 15, of which 8 were waited for; matrix products, arithmetic and copies ran while one was open for 5% of the time, Pallas kernels for 0%

profile of v2, /device:TPU:1, one launch (start us, length us, event | category | flops | bytes accessed | tf_op | source)
XLA Modules:
  0.0 458.2 jit_solution(11248679061134013120)
XLA Ops:
  1.7 3.9 collective-permute-start
  9.7 3.0 fusion.148
  16.0 4.0 collective-permute-start.2
  20.1 2.1 collective-permute-start.3
  27.6 2.3 convolution_bitcast_fusion.14
  29.9 2.3 convolution_bitcast_fusion.16
  32.3 7.1 %multiply_convert_fusion = (bf16[1,32,2,32,128]{4,1,0,3,2:T(8,128)(2,1)S(1)}, f32[1,32,2,32,128]{4,1,0,3,2:T(8,128)S(1)}) fusion(f32[3,32,2,32,128]{4,1,3,2,0:T(8,128)S(1)} %convolution_bitcast_fusion.9, f32[3,32,2,32,128]{4,1,3,2,0:T(8,128)S(1)} %convolution_bitcast_fusion.10, f32[3,32,2,32,128]{4,1,3,2,0:T(8,128)S(1)} %convolution_bitcast_fusion.11, ...), kind=kLoop, calls=%fused_computation.180 | loop fusion | flops 8388608 | bytes 39322112 | tf_op jit(solution)/shard_map/convert_element_type | solution.py:152
  41.4 4.3 collective-permute-start.4
  47.5 2.9 collective-permute-done.4
  50.4 4.1 collective-permute-done.5
  54.5 4.4 collective-permute-start.6
  58.9 2.1 collective-permute-start.7
  61.0 2.2 convolution_bitcast_fusion.7
  63.3 2.2 convolution_bitcast_fusion.1
  68.9 7.6 %add_convert_fusion.1 = (bf16[32,2,32,128]{3,0,2,1:T(8,128)(2,1)S(1)}, f32[1,32,2,32,128]{4,1,3,2,0:T(8,128)}) fusion(bf16[32,2,32,128]{3,0,2,1:T(8,128)(2,1)S(1)} %multiply_convert_fusion.1, f32[3,32,2,32,128]{4,1,3,2,0:T(8,128)S(1)} %convolution_bitcast_fusion, f32[3,32,2,32,128]{4,1,3,2,0:T(8,128)} %convolution_bitcast_fusion.1, ...), kind=kLoop, calls=%fused_computation.179 | loop fusion | flops 8650752 | bytes 39845888 | tf_op jit(solution)/shard_map/convert_element_type | solution.py:153
  76.6 3.1 collective-permute-start.8
  81.0 4.4 convolution_bitcast_fusion.30
  85.5 3.5 collective-permute-done.9
  88.9 5.9 %collective-permute-start.10 = (bf16[32,4,1,128]{3,0,2,1:T(8,128)(2,1)S(1)}, bf16[32,4,1,128]{3,0,2,1:T(8,128)(2,1)S(1)}, u32[]{:S(2)}, u32[]{:S(2)}) collective-permute-start(bf16[32,4,1,128]{3,0,2,1:T(8,128)(2,1)S(1)} %get-tuple-element.42), channel_id=1, source_target_pairs={{0,1},{1,2},{2,3},{3,4},{4,5},{5,6},{6,7},{8,9},{9,10},{10,11},{11... | collective-permute-start | bytes 98312 | tf_op jit(solution)/shard_map/ppermute | solution.py:25
  94.9 2.3 collective-permute-start.11
  97.7 2.4 collective-permute-done.11
  104.5 11.2 %all_gather.9 = f32[2,2,256,128]{3,0,2,1:T(2,128)S(1)} all-gather(f32[2,2,32,128]{3,0,2,1:T(2,128)S(1)} %get-tuple-element.26), channel_id=1, replica_groups=mesh['slab'=32,'coil'=8] {'coil'}, dimensions={2}, use_global_device_ids=true | all-gather | bytes 589824 | tf_op jit(solution)/shard_map/all_gather | solution.py:135
  120.9 3.7 fusion.15
  124.6 2.0 copy.624
  126.6 17.5 %all-to-all-start = ((bf16[2,2,2,256,128]{4,1,2,0,3:T(2,128)(2,1)}), bf16[2,2,2,256,128]{4,1,2,0,3:T(2,128)(2,1)S(1)}, u32[]{:S(2)}, u32[]{:S(2)}) async-start(bf16[2,2,2,256,128]{4,1,2,0,3:T(2,128)(2,1)} %copy.624), calls=%async_computation | async-start | bytes 1048576 | tf_op jit(solution)/shard_map/all_to_all | solution.py:111
  145.0 2.0 convolution_bitcast_fusion.26
  147.1 13.7 %all-to-all-done = bf16[2,2,2,256,128]{4,1,2,0,3:T(2,128)(2,1)S(1)} async-done(((bf16[2,2,2,256,128]{4,1,2,0,3:T(2,128)(2,1)}), bf16[2,2,2,256,128]{4,1,2,0,3:T(2,128)(2,1)S(1)}, u32[]{:S(2)}, u32[]{:S(2)}) %all-to-all-start) | async-done | bytes 524320 | tf_op jit(solution)/shard_map/all_to_all | solution.py:111
  164.6 20.3 %all_to_all.162 = bf16[2,2,64,8,128]{4,1,3,0,2:T(2,128)(2,1)S(1)} all-to-all(bf16[2,2,64,8,128]{4,1,3,0,2:T(2,128)(2,1)S(1)} %copy.628), channel_id=1, replica_groups=mesh['slab'=32,'coil'=8] {'slab'}, dimensions={2} | all-to-all | bytes 1048576 | tf_op jit(solution)/shard_map/all_to_all | solution.py:120
  187.2 2.0 copy.632
  189.3 16.8 %all_to_all.163 = f32[2,2,256,128]{3,1,0,2:T(2,128)} all-to-all(f32[2,2,256,128]{3,1,0,2:T(2,128)} %copy.632), channel_id=1, replica_groups=mesh['slab'=32,'coil'=8] {'coil'}, dimensions={2} | all-to-all | bytes 1048576 | tf_op jit(solution)/shard_map/all_to_all | solution.py:129
  207.3 14.0 %all_gather.10 = f32[2,2,256,128]{3,1,0,2:T(2,128)S(1)} all-gather(f32[2,2,32,128]{3,1,0,2:T(2,128)S(1)} %reduce_sum.146), channel_id=1, replica_groups=mesh['slab'=32,'coil'=8] {'coil'}, dimensions={2}, use_global_device_ids=true | all-gather | bytes 589824 | tf_op jit(solution)/shard_map/all_gather | solution.py:135
  226.2 3.9 fusion.14
  230.1 2.1 copy.635
  232.1 21.2 %all_to_all.164 = bf16[2,2,2,256,128]{4,1,2,0,3:T(2,128)(2,1)S(1)} all-to-all(bf16[2,2,2,256,128]{4,1,2,0,3:T(2,128)(2,1)} %copy.635), channel_id=1, replica_groups=mesh['slab'=32,'coil'=8] {'slab'}, dimensions={3} | all-to-all | bytes 1048576 | tf_op jit(solution)/shard_map/all_to_all | solution.py:111
  255.8 20.3 %all_to_all.165 = bf16[2,2,64,8,128]{4,1,3,0,2:T(2,128)(2,1)S(1)} all-to-all(bf16[2,2,64,8,128]{4,1,3,0,2:T(2,128)(2,1)S(1)} %copy.639), channel_id=1, replica_groups=mesh['slab'=32,'coil'=8] {'slab'}, dimensions={2} | all-to-all | bytes 1048576 | tf_op jit(solution)/shard_map/all_to_all | solution.py:120
  278.5 2.0 copy.643
  280.5 7.4 %all-to-all-start.5 = ((f32[2,2,256,128]{3,1,0,2:T(2,128)}), f32[2,2,256,128]{3,1,0,2:T(2,128)}, u32[]{:S(2)}, u32[]{:S(2)}) async-start(f32[2,2,256,128]{3,1,0,2:T(2,128)} %copy.643), calls=%async_computation.5 | async-start | bytes 1048576 | tf_op jit(solution)/shard_map/all_to_all | solution.py:129
  288.6 8.8 %all-to-all-done.5 = f32[2,2,256,128]{3,1,0,2:T(2,128)} async-done(((f32[2,2,256,128]{3,1,0,2:T(2,128)}), f32[2,2,256,128]{3,1,0,2:T(2,128)}, u32[]{:S(2)}, u32[]{:S(2)}) %all-to-all-start.5) | async-done | bytes 524320 | tf_op jit(solution)/shard_map/all_to_all | solution.py:129
  300.7 19.4 %all_to_all.166 = f32[256,1,2]{2,1,0:T(1,128)} all-to-all(f32[256,1,2]{2,1,0:T(1,128)S(1)} %broadcast_in_dim.6), channel_id=1, replica_groups=mesh['slab'=32,'coil'=8] {'slab','coil'}, dimensions={0} | all-to-all | bytes 4096 | tf_op jit(solution)/shard_map/all_to_all | solution.py:142
  324.4 19.3 %all_to_all.167 = f32[256,1,1]{2,1,0:T(1,128)} all-to-all(f32[256,1,1]{2,1,0:T(1,128)S(1)} %broadcast_in_dim.7), channel_id=1, replica_groups=mesh['slab'=32,'coil'=8] {'slab','coil'}, dimensions={0} | all-to-all | bytes 2048 | tf_op jit(solution)/shard_map/all_to_all | solution.py:142
  346.8 14.0 %all_gather.11 = f32[2,2,256,128]{3,0,2,1:T(2,128)S(1)} all-gather(f32[2,2,32,128]{3,0,2,1:T(2,128)S(1)} %multiply_add_fusion.5), channel_id=1, replica_groups=mesh['slab'=32,'coil'=8] {'coil'}, dimensions={2}, use_global_device_ids=true | all-gather | bytes 589824 | tf_op jit(solution)/shard_map/all_gather | solution.py:135
  366.0 3.9 fusion.13
  369.9 2.1 copy.654
  372.0 20.8 %all_to_all.168 = bf16[2,2,2,256,128]{4,1,2,0,3:T(2,128)(2,1)S(1)} all-to-all(bf16[2,2,2,256,128]{4,1,2,0,3:T(2,128)(2,1)} %copy.654), channel_id=1, replica_groups=mesh['slab'=32,'coil'=8] {'slab'}, dimensions={3} | all-to-all | bytes 1048576 | tf_op jit(solution)/shard_map/all_to_all | solution.py:111
  395.2 20.3 %all_to_all.169 = bf16[2,2,64,8,128]{4,1,3,0,2:T(2,128)(2,1)S(1)} all-to-all(bf16[2,2,64,8,128]{4,1,3,0,2:T(2,128)(2,1)S(1)} %copy.658), channel_id=1, replica_groups=mesh['slab'=32,'coil'=8] {'slab'}, dimensions={2} | all-to-all | bytes 1048576 | tf_op jit(solution)/shard_map/all_to_all | solution.py:120
  417.4 15.2 %all_to_all.170 = f32[2,2,256,128]{3,1,0,2:T(2,128)S(1)} all-to-all(f32[2,2,256,128]{3,1,0,2:T(2,128)S(1)} %copy.662), channel_id=1, replica_groups=mesh['slab'=32,'coil'=8] {'coil'}, dimensions={2} | all-to-all | bytes 1048576 | tf_op jit(solution)/shard_map/all_to_all | solution.py:129
  434.8 6.5 %all-to-all-start.11 = ((f32[256,1,1]{2,1,0:T(1,128)}), f32[256,1,1]{2,1,0:T(1,128)S(1)}, u32[]{:S(2)}, u32[]{:S(2)}) async-start(f32[256,1,1]{2,1,0:T(1,128)} %broadcast_in_dim.8), calls=%async_computation.11 | async-start | bytes 262144 | tf_op jit(solution)/shard_map/all_to_all | solution.py:142
  441.5 12.8 %all-to-all-done.11 = f32[256,1,1]{2,1,0:T(1,128)S(1)} async-done(((f32[256,1,1]{2,1,0:T(1,128)}), f32[256,1,1]{2,1,0:T(1,128)S(1)}, u32[]{:S(2)}, u32[]{:S(2)}) %all-to-all-start.11) | async-done | bytes 1056 | tf_op jit(solution)/shard_map/all_to_all | solution.py:142
  (179 shorter events, 72.1 us)
Async XLA Ops:
  0.6 144.4 %copy-start = (f32[2,2,64,8,128]{4,3,2,1,0:T(8,128)S(1)}, f32[2,2,64,8,128]{4,3,2,1,0:T(8,128)}, u32[]{:S(2)}) copy-start(f32[2,2,64,8,128]{4,3,2,1,0:T(8,128)} %param.16) | copy-start | bytes 3145732
  0.6 12.1 %copy-start.24 = (bf16[3,3,3,2,32]{4,3,2,1,0:T(2,128)(2,1)S(1)}, bf16[3,3,3,2,32]{4,3,2,1,0:T(2,128)(2,1)}, u32[]{:S(2)}) copy-start(bf16[3,3,3,2,32]{4,3,2,1,0:T(2,128)(2,1)} %param.13) | copy-start | bytes 10372
  1.7 14.3 %collective-permute-start = (bf16[2,1,32,128]{3,0,2,1:T(2,128)(2,1)S(1)}, bf16[2,1,32,128]{3,0,2,1:T(2,128)(2,1)S(1)}, u32[]{:S(2)}, u32[]{:S(2)}) collective-permute-start(bf16[2,1,32,128]{3,0,2,1:T(2,128)(2,1)S(1)} %get-tuple-element.78), channel_id=1, source_target_pairs={{0,8},{8,16},{16,24},{24,32},{32,40},{40,48},{48,56},{56,64},{64,7... | collective-permute-start | bytes 49160 | tf_op jit(solution)/shard_map/ppermute | solution.py:25
  5.6 10.4 %collective-permute-start.1 = (bf16[2,1,32,128]{3,0,2,1:T(2,128)(2,1)S(1)}, bf16[2,1,32,128]{3,0,2,1:T(2,128)(2,1)S(1)}, u32[]{:S(2)}, u32[]{:S(2)}) collective-permute-start(bf16[2,1,32,128]{3,0,2,1:T(2,128)(2,1)S(1)} %get-tuple-element.79), channel_id=1, source_target_pairs={{8,0},{16,8},{24,16},{32,24},{40,32},{48,40},{56,48},{64,56},{72,6... | collective-permute-start | bytes 49160 | tf_op jit(solution)/shard_map/ppermute | solution.py:27
  9.6 3.7 copy-start.5
  12.7 2.0 copy-start.22
  13.3 8.9 %copy-start.23 = (bf16[3,3,3,32,2]{3,4,2,1,0:T(2,128)(2,1)S(1)}, bf16[3,3,3,32,2]{3,4,2,1,0:T(2,128)(2,1)}, u32[]{:S(2)}) copy-start(bf16[3,3,3,32,2]{3,4,2,1,0:T(2,128)(2,1)} %param.11) | copy-start | bytes 10372
  16.0 7.4 %collective-permute-start.2 = (bf16[2,4,1,128]{3,0,2,1:T(2,128)(2,1)S(1)}, bf16[2,4,1,128]{3,0,2,1:T(2,128)(2,1)S(1)}, u32[]{:S(2)}, u32[]{:S(2)}) collective-permute-start(bf16[2,4,1,128]{3,0,2,1:T(2,128)(2,1)S(1)} %get-tuple-element.74), channel_id=1, source_target_pairs={{0,1},{1,2},{2,3},{3,4},{4,5},{5,6},{6,7},{8,9},{9,10},{10,11},{11... | collective-permute-start | bytes 6152 | tf_op jit(solution)/shard_map/ppermute | solution.py:25
  20.1 4.9 %collective-permute-start.3 = (bf16[2,4,1,128]{3,0,2,1:T(2,128)(2,1)S(1)}, bf16[2,4,1,128]{3,0,2,1:T(2,128)(2,1)S(1)}, u32[]{:S(2)}, u32[]{:S(2)}) collective-permute-start(bf16[2,4,1,128]{3,0,2,1:T(2,128)(2,1)S(1)} %get-tuple-element.75), channel_id=1, source_target_pairs={{1,0},{2,1},{3,2},{4,3},{5,4},{6,5},{7,6},{9,8},{10,9},{11,10},{12... | collective-permute-start | bytes 6152 | tf_op jit(solution)/shard_map/ppermute | solution.py:27
  27.6 4.6 %copy-start.1 = (f32[3,32,2,32,128]{4,1,0,3,2:T(8,128)S(1)}, f32[3,32,2,32,128]{4,1,0,3,2:T(8,128)}, u32[]{:S(2)}) copy-start(f32[3,32,2,32,128]{4,1,0,3,2:T(8,128)} %fusion.148) | copy-start | bytes 9437188
  27.6 4.6 %copy-start.25 = (f32[32]{0:T(128)S(1)}, f32[32]{0:T(128)}, u32[]{:S(2)}) copy-start(f32[32]{0:T(128)} %convolution_bitcast_fusion.39) | copy-start | bytes 388
  39.3 7.6 %copy-start.4 = (bf16[1,32,2,32,128]{4,1,0,3,2:T(8,128)(2,1)}, bf16[1,32,2,32,128]{4,1,0,3,2:T(8,128)(2,1)S(1)}, u32[]{:S(2)}) copy-start(bf16[1,32,2,32,128]{4,1,0,3,2:T(8,128)(2,1)S(1)} %get-tuple-element.30) | copy-start | bytes 1572868
  39.3 7.6 %copy-start.21 = (bf16[3,3,3,32,32]{4,3,2,1,0:T(8,128)(2,1)S(1)}, bf16[3,3,3,32,32]{4,3,2,1,0:T(8,128)(2,1)}, u32[]{:S(2)}) copy-start(bf16[3,3,3,32,32]{4,3,2,1,0:T(8,128)(2,1)} %param.12) | copy-start | bytes 165892
  41.4 9.0 %collective-permute-start.4 = (bf16[32,1,32,128]{3,0,2,1:T(8,128)(2,1)S(1)}, bf16[32,1,32,128]{3,0,2,1:T(8,128)(2,1)S(1)}, u32[]{:S(2)}, u32[]{:S(2)}) collective-permute-start(bf16[32,1,32,128]{3,0,2,1:T(8,128)(2,1)S(1)} %get-tuple-element.60), channel_id=1, source_target_pairs={{0,8},{8,16},{16,24},{24,32},{32,40},{40,48},{48,56},{56,64},{64,7... | collective-permute-start | bytes 786440 | tf_op jit(solution)/shard_map/ppermute | solution.py:25
  45.7 8.8 %collective-permute-start.5 = (bf16[32,1,32,128]{3,0,2,1:T(8,128)(2,1)S(1)}, bf16[32,1,32,128]{3,0,2,1:T(8,128)(2,1)S(1)}, u32[]{:S(2)}, u32[]{:S(2)}) collective-permute-start(bf16[32,1,32,128]{3,0,2,1:T(8,128)(2,1)S(1)} %get-tuple-element.61), channel_id=1, source_target_pairs={{8,0},{16,8},{24,16},{32,24},{40,32},{48,40},{56,48},{64,56},{72,6... | collective-permute-start | bytes 786440 | tf_op jit(solution)/shard_map/ppermute | solution.py:27
  54.5 10.9 %collective-permute-start.6 = (bf16[32,4,1,128]{3,0,2,1:T(8,128)(2,1)S(1)}, bf16[32,4,1,128]{3,0,2,1:T(8,128)(2,1)S(1)}, u32[]{:S(2)}, u32[]{:S(2)}) collective-permute-start(bf16[32,4,1,128]{3,0,2,1:T(8,128)(2,1)S(1)} %get-tuple-element.46), channel_id=1, source_target_pairs={{0,1},{1,2},{2,3},{3,4},{4,5},{5,6},{6,7},{8,9},{9,10},{10,11},{11... | collective-permute-start | bytes 98312 | tf_op jit(solution)/shard_map/ppermute | solution.py:25
  58.9 6.6 %collective-permute-start.7 = (bf16[32,4,1,128]{3,0,2,1:T(8,128)(2,1)S(1)}, bf16[32,4,1,128]{3,0,2,1:T(8,128)(2,1)S(1)}, u32[]{:S(2)}, u32[]{:S(2)}) collective-permute-start(bf16[32,4,1,128]{3,0,2,1:T(8,128)(2,1)S(1)} %get-tuple-element.47), channel_id=1, source_target_pairs={{1,0},{2,1},{3,2},{4,3},{5,4},{6,5},{7,6},{9,8},{10,9},{11,10},{12... | collective-permute-start | bytes 98312 | tf_op jit(solution)/shard_map/ppermute | solution.py:27
  68.9 12.1 %copy-start.27 = (bf16[1,1,3,2,32]{4,3,2,1,0:T(2,128)(2,1)S(1)}, bf16[1,1,3,2,32]{4,3,2,1,0:T(2,128)(2,1)}, u32[]{:S(2)}) copy-start(bf16[1,1,3,2,32]{4,3,2,1,0:T(2,128)(2,1)} %get-tuple-element.84) | copy-start | bytes 1156
  76.6 8.8 %collective-permute-start.8 = (bf16[32,1,32,128]{3,0,2,1:T(8,128)(2,1)S(1)}, bf16[32,1,32,128]{3,0,2,1:T(8,128)(2,1)S(1)}, u32[]{:S(2)}, u32[]{:S(2)}) collective-permute-start(bf16[32,1,32,128]{3,0,2,1:T(8,128)(2,1)S(1)} %get-tuple-element.58), channel_id=1, source_target_pairs={{0,8},{8,16},{16,24},{24,32},{32,40},{40,48},{48,56},{56,64},{64,7... | collective-permute-start | bytes 786440 | tf_op jit(solution)/shard_map/ppermute | solution.py:25
  79.7 9.2 %collective-permute-start.9 = (bf16[32,1,32,128]{3,0,2,1:T(8,128)(2,1)S(1)}, bf16[32,1,32,128]{3,0,2,1:T(8,128)(2,1)S(1)}, u32[]{:S(2)}, u32[]{:S(2)}) collective-permute-start(bf16[32,1,32,128]{3,0,2,1:T(8,128)(2,1)S(1)} %get-tuple-element.59), channel_id=1, source_target_pairs={{8,0},{16,8},{24,16},{32,24},{40,32},{48,40},{56,48},{64,56},{72,6... | collective-permute-start | bytes 786440 | tf_op jit(solution)/shard_map/ppermute | solution.py:27
  88.9 8.7 %collective-permute-start.10 = (bf16[32,4,1,128]{3,0,2,1:T(8,128)(2,1)S(1)}, bf16[32,4,1,128]{3,0,2,1:T(8,128)(2,1)S(1)}, u32[]{:S(2)}, u32[]{:S(2)}) collective-permute-start(bf16[32,4,1,128]{3,0,2,1:T(8,128)(2,1)S(1)} %get-tuple-element.42), channel_id=1, source_target_pairs={{0,1},{1,2},{2,3},{3,4},{4,5},{5,6},{6,7},{8,9},{9,10},{10,11},{11... | collective-permute-start | bytes 98312 | tf_op jit(solution)/shard_map/ppermute | solution.py:25
  94.9 5.2 %collective-permute-start.11 = (bf16[32,4,1,128]{3,0,2,1:T(8,128)(2,1)S(1)}, bf16[32,4,1,128]{3,0,2,1:T(8,128)(2,1)S(1)}, u32[]{:S(2)}, u32[]{:S(2)}) collective-permute-start(bf16[32,4,1,128]{3,0,2,1:T(8,128)(2,1)S(1)} %get-tuple-element.43), channel_id=1, source_target_pairs={{1,0},{2,1},{3,2},{4,3},{5,4},{6,5},{7,6},{9,8},{10,9},{11,10},{12... | collective-permute-start | bytes 98312 | tf_op jit(solution)/shard_map/ppermute | solution.py:27
  100.5 2.7 copy-start.19
  103.3 17.6 %copy-start.3 = (f32[1,256,2,256]{3,1,2,0:T(8,128)S(1)}, f32[1,256,2,256]{3,1,2,0:T(8,128)}, u32[]{:S(2)}) copy-start(f32[1,256,2,256]{3,1,2,0:T(8,128)} %get-tuple-element.52) | copy-start | bytes 1572868
  104.5 12.4 %copy-start.17 = (f32[2,2,32,128]{3,0,2,1:T(2,128)}, f32[2,2,32,128]{3,0,2,1:T(2,128)S(1)}, u32[]{:S(2)}) copy-start(f32[2,2,32,128]{3,0,2,1:T(2,128)S(1)} %get-tuple-element.26) | copy-start | bytes 196612
  119.8 24.3 %copy-start.26 = (s32[64,8]{0,1:T(8,128)S(1)}, s32[64,8]{0,1:T(8,128)}, u32[]{:S(2)}) copy-start(s32[64,8]{0,1:T(8,128)} %param.17) | copy-start | bytes 6148
  126.6 34.2 %all-to-all-start = ((bf16[2,2,2,256,128]{4,1,2,0,3:T(2,128)(2,1)}), bf16[2,2,2,256,128]{4,1,2,0,3:T(2,128)(2,1)S(1)}, u32[]{:S(2)}, u32[]{:S(2)}) async-start(bf16[2,2,2,256,128]{4,1,2,0,3:T(2,128)(2,1)} %copy.624), calls=%async_computation | async-start | bytes 1048576 | tf_op jit(solution)/shard_map/all_to_all | solution.py:111
  145.0 17.9 %copy-start.8 = (f32[1,64,2,64]{3,1,2,0:T(8,128)}, f32[1,64,2,64]{3,1,2,0:T(8,128)S(1)}, u32[]{:S(2)}) copy-start(f32[1,64,2,64]{3,1,2,0:T(8,128)S(1)} %get-tuple-element.76) | copy-start | bytes 98308
  145.0 17.9 %copy-start.11 = (f32[1,64,2,64]{3,1,2,0:T(8,128)}, f32[1,64,2,64]{3,1,2,0:T(8,128)S(1)}, u32[]{:S(2)}) copy-start(f32[1,64,2,64]{3,1,2,0:T(8,128)S(1)} %get-tuple-element.66) | copy-start | bytes 98308
  145.0 17.9 %copy-start.14 = (f32[1,64,2,64]{3,1,2,0:T(8,128)}, f32[1,64,2,64]{3,1,2,0:T(8,128)S(1)}, u32[]{:S(2)}) copy-start(f32[1,64,2,64]{3,1,2,0:T(8,128)S(1)} %get-tuple-element.77) | copy-start | bytes 98308
  145.0 108.5 %copy-start.6 = (f32[1,64,2,64]{3,1,2,0:T(8,128)}, f32[1,64,2,64]{3,1,2,0:T(8,128)S(1)}, u32[]{:S(2)}) copy-start(f32[1,64,2,64]{3,1,2,0:T(8,128)S(1)} %get-tuple-element.67) | copy-start | bytes 98308
  160.9 24.0 %copy-start.2 = (f32[1,256,2,256]{3,1,2,0:T(8,128)S(1)}, f32[1,256,2,256]{3,1,2,0:T(8,128)}, u32[]{:S(2)}) copy-start(f32[1,256,2,256]{3,1,2,0:T(8,128)} %get-tuple-element.62) | copy-start | bytes 1572868
  226.2 27.3 %copy-start.9 = (f32[1,64,2,64]{3,1,2,0:T(8,128)S(1)}, f32[1,64,2,64]{3,1,2,0:T(8,128)}, u32[]{:S(2)}) copy-start(f32[1,64,2,64]{3,1,2,0:T(8,128)} %copy-done.8) | copy-start | bytes 98308
  230.1 24.1 %copy-start.12 = (f32[1,64,2,64]{3,1,2,0:T(8,128)S(1)}, f32[1,64,2,64]{3,1,2,0:T(8,128)}, u32[]{:S(2)}) copy-start(f32[1,64,2,64]{3,1,2,0:T(8,128)} %copy-done.11) | copy-start | bytes 98308
  230.1 24.1 %copy-start.15 = (f32[1,64,2,64]{3,1,2,0:T(8,128)S(1)}, f32[1,64,2,64]{3,1,2,0:T(8,128)}, u32[]{:S(2)}) copy-start(f32[1,64,2,64]{3,1,2,0:T(8,128)} %copy-done.14) | copy-start | bytes 98308
  280.5 16.8 %all-to-all-start.5 = ((f32[2,2,256,128]{3,1,0,2:T(2,128)}), f32[2,2,256,128]{3,1,0,2:T(2,128)}, u32[]{:S(2)}, u32[]{:S(2)}) async-start(f32[2,2,256,128]{3,1,0,2:T(2,128)} %copy.643), calls=%async_computation.5 | async-start | bytes 1048576 | tf_op jit(solution)/shard_map/all_to_all | solution.py:129
  366.0 26.9 %copy-start.7 = (f32[1,64,2,64]{3,1,2,0:T(8,128)S(1)}, f32[1,64,2,64]{3,1,2,0:T(8,128)}, u32[]{:S(2)}) copy-start(f32[1,64,2,64]{3,1,2,0:T(8,128)} %copy-done.6) | copy-start | bytes 98308
  366.0 26.9 %copy-start.10 = (f32[1,64,2,64]{3,1,2,0:T(8,128)S(1)}, f32[1,64,2,64]{3,1,2,0:T(8,128)}, u32[]{:S(2)}) copy-start(f32[1,64,2,64]{3,1,2,0:T(8,128)} %copy-done.8) | copy-start | bytes 98308
  369.9 23.6 %copy-start.13 = (f32[1,64,2,64]{3,1,2,0:T(8,128)S(1)}, f32[1,64,2,64]{3,1,2,0:T(8,128)}, u32[]{:S(2)}) copy-start(f32[1,64,2,64]{3,1,2,0:T(8,128)} %copy-done.11) | copy-start | bytes 98308
  369.9 23.6 %copy-start.16 = (f32[1,64,2,64]{3,1,2,0:T(8,128)S(1)}, f32[1,64,2,64]{3,1,2,0:T(8,128)}, u32[]{:S(2)}) copy-start(f32[1,64,2,64]{3,1,2,0:T(8,128)} %copy-done.14) | copy-start | bytes 98308
  416.9 39.7 %copy-start.18 = (f32[2,2,32,128]{3,0,2,1:T(2,128)S(1)}, f32[2,2,32,128]{3,0,2,1:T(2,128)}, u32[]{:S(2)}) copy-start(f32[2,2,32,128]{3,0,2,1:T(2,128)} %copy-done.17) | copy-start | bytes 196612
  416.9 39.7 %copy-start.20 = (f32[2,2,32,128]{3,0,2,1:T(2,128)S(1)}, f32[2,2,32,128]{3,0,2,1:T(2,128)}, u32[]{:S(2)}) copy-start(f32[2,2,32,128]{3,0,2,1:T(2,128)} %get-tuple-element.27) | copy-start | bytes 196612
  434.8 19.5 %all-to-all-start.11 = ((f32[256,1,1]{2,1,0:T(1,128)}), f32[256,1,1]{2,1,0:T(1,128)S(1)}, u32[]{:S(2)}, u32[]{:S(2)}) async-start(f32[256,1,1]{2,1,0:T(1,128)} %broadcast_in_dim.8), calls=%async_computation.11 | async-start | bytes 262144 | tf_op jit(solution)/shard_map/all_to_all | solution.py:142

commit v3 on v2

--- a/solution.py
+++ b/solution.py
@@ -45,26 +45,17 @@
 
 
 def conv_layer(inputs, weights):
-    depth, rows, width = (inputs.shape[1], inputs.shape[2], inputs.shape[3])
     padded = extended(inputs, (("slab", 1), ("coil", 2)), 1)
-    total = jnp.zeros((weights.shape[3], depth, rows, width), jnp.float32)
-    for depth_shift in range(3):
-        for row_shift in range(3):
-            window = padded[:, depth_shift : depth_shift + depth, row_shift : row_shift + rows, :]
-            taps = jnp.einsum(
-                "aoc,czyx->aozyx",
-                weights[depth_shift, row_shift],
-                window,
-                preferred_element_type=jnp.float32,
-            )
-            shifted = jnp.pad(taps, ((0, 0), (0, 0), (0, 0), (0, 0), (1, 1)))
-            total = (
-                total
-                + shifted[0, ..., 0:width]
-                + shifted[1, ..., 1 : width + 1]
-                + shifted[2, ..., 2 : width + 2]
-            )
-    return total
+    kernel = jnp.transpose(weights, (3, 4, 0, 1, 2))
+    result = lax.conv_general_dilated(
+        padded[None],
+        kernel,
+        (1, 1, 1),
+        ((0, 0), (0, 0), (1, 1)),
+        dimension_numbers=("NCDHW", "OIDHW", "NCDHW"),
+        preferred_element_type=jnp.float32,
+    )
+    return result[0]
 
 
 def dft_blocks(length, inverse):

time: 463 us -> 697 us (1.51); the launches traced: 458 us -> 685 us
  matrix products: 50 us -> 181 us
  local copies, waits for them, and re-layouts: 31 us -> 123 us
  blocking collectives: 213 us -> 233 us
  waiting for transfers between devices: 49.8 us -> 36.7 us
  starting transfers between devices: 67.4 us -> 57.9 us
    conv_general_dilated x0 -> x3, matrix products: none -> 156 us  [conv_layer(): lax.conv_general_dilated(padded[None], kernel, (1, 1, 1), ((0, 0), (0, 0)...]
    conv_general_dilated x0 -> x9, local copies, waits for them, and re-layouts: none -> 26 us  [conv_layer(): lax.conv_general_dilated(padded[None], kernel, (1, 1, 1), ((0, 0), (0, 0)...]
    dot_general x27 -> x0, matrix products: 25.7 us -> none  [conv_layer(): jnp.einsum('aoc,czyx->aozyx', weights[depth_shift, row_shift], window, pr...]
    unnamed x61 -> x69, local copies, waits for them, and re-layouts: 2.78 us -> 23.1 us
    all_to_all x2 -> x3, blocking collectives: 32 us -> 48.8 us  [combine_coils(): lax.all_to_all(partial_value, 'coil', split_axis=2, concat_axis=0, tiled=...]
    ppermute x0 -> x4, local copies, waits for them, and re-layouts: none -> 14.3 us  [the longest x2 7.17 us: extended(): lax.ppermute(tail, axis, [(i, (i + 1) % count) for i in range(ends)])]
    broadcast_in_dim x0 -> x3, other arithmetic: none -> 10.9 us  [conv_layer(): padded[None]]
    broadcast_in_dim x0 -> x3, local copies, waits for them, and re-layouts: none -> 10.5 us  [conv_layer(): padded[None]]
  transfers between devices with their start and end apart: 15 -> 14, of which waited for: 8 -> 8; matrix products, arithmetic and copies ran while one was open for 5% -> 4% of each run, Pallas kernels for 0% -> 0%
where the time goes in v3:
time: 697 us; the launch traced here: 685 us
  blocking collectives  233 us (33%)
  matrix products  181 us (26%)
  local copies, waits for them, and re-layouts  123 us (18%)
  starting transfers between devices  57.9 us (8%)
  other arithmetic  46.4 us (7%)
  waiting for transfers between devices  36.7 us (5%)
    conv_general_dilated x3, matrix products, conv_layer(): lax.conv_general_dilated(padded[None], kernel, (1, 1, 1), ((0, 0), (0, 0)...  156 us
    all_to_all x3, blocking collectives, coil_term(): lax.all_to_all(back.astype(jnp.bfloat16), 'slab', split_axis=2, concat_ax...  60.9 us
    all_to_all x3, blocking collectives, combine_coils(): lax.all_to_all(partial_value, 'coil', split_axis=2, concat_axis=0, tiled=...  48.8 us
    all_to_all x2, blocking collectives, coil_term(): lax.all_to_all(spectrum.astype(jnp.bfloat16), 'slab', split_axis=3, conca...  42.1 us
    all_gather x3, blocking collectives, gather_rows(): return lax.all_gather(value, 'coil', axis=2, tiled=True)  42 us
    all_to_all x2, blocking collectives, global_sums(): lax.all_to_all(spread, axes, split_axis=0, concat_axis=0, tiled=True)  39 us
    ppermute x6, starting transfers between devices, extended(): lax.ppermute(tail, axis, [(i, (i + 1) % count) for i in range(ends)])  27 us
    conv_general_dilated x9, local copies, waits for them, and re-layouts, conv_layer(): lax.conv_general_dilated(padded[None], kernel, (1, 1, 1), ((0, 0), (0, 0)...  26 us
  transfers between devices with their start and end apart: 14, of which 8 were waited for; matrix products, arithmetic and copies ran while one was open for 4% of the time, Pallas kernels for 0%

profile of v3, /device:TPU:1, one launch (start us, length us, event | category | flops | bytes accessed | tf_op | source)
XLA Modules:
  0.0 684.9 jit_solution(6342718819612224770)
XLA Ops:
  1.6 3.9 collective-permute-start
  7.5 2.5 collective-permute-done.1
  10.0 5.2 collective-permute-start.2
  22.7 7.8 %broadcast_select_fusion.1 = f32[2,32,8,17,32]{4,2,3,1,0:T(8,128)S(1)} fusion(pred[8,17]{0,1:T(8,128)(4,1)} %constant.113, bf16[3,3,3,32,2]{3,4,2,1,0:T(2,128)(2,1)} %param.11, bf16[2,4,34,1,7,2]{4,0,5,2,1,3:T(2,128)(2,1)S(1)} %slice.155, bf16[2,4,34,1,8,17]{4,0,5,2,1,3:T(2,128)(2,1)S(1)} %copy.378), kind=kOutput, calls=%fused_computation.23 | convolution fusion | flops 30607616 | bytes 1199304 | tf_op jit(solution)/shard_map/conv_general_dilated | solution.py:50
  34.2 2.6 copy.380
  36.8 4.1 collective-permute-start.4
  40.9 3.3 copy.381
  47.3 3.6 copy.382
  53.4 3.5 copy.383
  58.9 4.1 collective-permute-start.6
  66.6 4.1 collective-permute-done.7
  70.6 4.6 maximum_bitcast_fusion
  75.3 8.1 %copy.497 = bf16[32,4,34,1,128]{2,0,4,1,3:T(8,128)(2,1)} copy(bf16[32,4,34,1,128]{0,2,4,1,3:T(8,128)(2,1)} %maximum_bitcast_fusion) | data formatting | bytes 2228224
  83.3 5.2 pad.2.clone
  88.5 8.7 %copy.386 = bf16[32,4,34,1,8,17]{0,4,5,2,1,3:T(8,128)(2,1)} copy(bf16[32,4,34,1,8,17]{2,0,5,4,1,3:T(8,128)(2,1)} %bitcast.328) | data formatting | bytes 2367488 | tf_op jit(solution)/shard_map/conv_general_dilated | solution.py:50
  98.5 8.6 %broadcast_select_fusion = f32[2,32,8,17,32]{4,2,3,1,0:T(8,128)S(1)} fusion(pred[8,17]{0,1:T(8,128)(4,1)S(1)} %copy-done.25, bf16[3,3,3,32,32]{4,3,2,1,0:T(8,128)(2,1)S(1)} %copy-done.26, bf16[32,4,34,1,7,2]{0,4,5,2,1,3:T(8,128)(2,1)S(1)} %slice.159, bf16[32,4,34,1,8,17]{0,4,5,2,1,3:T(8,128)(2,1)} %copy.386), kind=kOutput, calls=%fused_computation.22 | convolution fusion | flops 485543936 | bytes 2475144 | tf_op jit(solution)/shard_map/conv_general_dilated | solution.py:50
  112.1 3.3 copy.388
  115.4 4.5 collective-permute-start.8
  119.9 3.3 copy.389
  126.9 3.6 copy.390
  130.7 3.6 copy.391
  134.3 2.7 pad_maximum_fusion.9
  137.0 5.1 collective-permute-start.10
  150.1 6.3 maximum_bitcast_fusion.1
  156.4 8.1 %copy.498 = bf16[32,4,34,1,128]{2,0,4,1,3:T(8,128)(2,1)} copy(bf16[32,4,34,1,128]{0,2,4,1,3:T(8,128)(2,1)} %maximum_bitcast_fusion.1) | data formatting | bytes 2228224
  164.4 5.1 pad.4.clone
  169.6 8.7 %copy.394 = bf16[32,4,34,1,8,17]{0,4,5,2,1,3:T(8,128)(2,1)} copy(bf16[32,4,34,1,8,17]{2,0,5,4,1,3:T(8,128)(2,1)} %bitcast.327) | data formatting | bytes 2367488 | tf_op jit(solution)/shard_map/conv_general_dilated | solution.py:50
  179.5 139.8 %fusion.11 = f32[2,32,8,17,2]{2,4,3,1,0:T(2,128)} fusion(bf16[3,3,3,2,32]{4,3,2,1,0:T(2,128)(2,1)S(1)} %copy-done.27, bf16[32,4,34,1,7,2]{0,4,5,2,1,3:T(8,128)(2,1)S(1)} %slice.163, bf16[32,4,34,1,8,17]{0,4,5,2,1,3:T(8,128)(2,1)} %copy.394), kind=kOutput, calls=%fused_computation.11 | convolution fusion | flops 34050048 | bytes 1378688 | tf_op jit(solution)/shard_map/conv_general_dilated | solution.py:50
  325.5 14.1 %all_gather.9 = f32[2,2,256,128]{3,1,0,2:T(2,128)S(1)} all-gather(f32[2,2,32,128]{3,1,0,2:T(2,128)S(1)} %fusion.74), channel_id=1, replica_groups=mesh['slab'=32,'coil'=8] {'coil'}, dimensions={2}, use_global_device_ids=true | all-gather | bytes 589824 | tf_op jit(solution)/shard_map/all_gather | solution.py:126
  345.4 2.7 fusion.36
  350.0 14.7 %all-to-all-start = ((bf16[2,2,2,256,128]{4,1,2,0,3:T(2,128)(2,1)}), bf16[2,2,2,256,128]{4,1,2,0,3:T(2,128)(2,1)S(1)}, u32[]{:S(2)}, u32[]{:S(2)}) async-start(bf16[2,2,2,256,128]{4,1,2,0,3:T(2,128)(2,1)} %copy.404), calls=%async_computation | async-start | bytes 1048576 | tf_op jit(solution)/shard_map/all_to_all | solution.py:102
  369.0 12.5 %all-to-all-done = bf16[2,2,2,256,128]{4,1,2,0,3:T(2,128)(2,1)S(1)} async-done(((bf16[2,2,2,256,128]{4,1,2,0,3:T(2,128)(2,1)}), bf16[2,2,2,256,128]{4,1,2,0,3:T(2,128)(2,1)S(1)}, u32[]{:S(2)}, u32[]{:S(2)}) %all-to-all-start) | async-done | bytes 524320 | tf_op jit(solution)/shard_map/all_to_all | solution.py:102
  385.3 20.3 %all_to_all.162 = bf16[2,2,64,8,128]{4,1,3,0,2:T(2,128)(2,1)S(1)} all-to-all(bf16[2,2,64,8,128]{4,1,3,0,2:T(2,128)(2,1)S(1)} %copy.408), channel_id=1, replica_groups=mesh['slab'=32,'coil'=8] {'slab'}, dimensions={2} | all-to-all | bytes 1048576 | tf_op jit(solution)/shard_map/all_to_all | solution.py:111
  410.0 16.8 %all_to_all.163 = f32[2,2,256,128]{3,1,0,2:T(2,128)} all-to-all(f32[2,2,256,128]{3,1,0,2:T(2,128)} %copy.412), channel_id=1, replica_groups=mesh['slab'=32,'coil'=8] {'coil'}, dimensions={2} | all-to-all | bytes 1048576 | tf_op jit(solution)/shard_map/all_to_all | solution.py:120
  428.1 14.2 %all_gather.10 = f32[2,2,256,128]{3,1,0,2:T(2,128)S(1)} all-gather(f32[2,2,32,128]{3,1,0,2:T(2,128)S(1)} %reduce_sum.146), channel_id=1, replica_groups=mesh['slab'=32,'coil'=8] {'coil'}, dimensions={2}, use_global_device_ids=true | all-gather | bytes 589824 | tf_op jit(solution)/shard_map/all_gather | solution.py:126
  448.0 3.9 fusion.35
  453.8 21.1 %all_to_all.164 = bf16[2,2,2,256,128]{4,1,2,0,3:T(2,128)(2,1)S(1)} all-to-all(bf16[2,2,2,256,128]{4,1,2,0,3:T(2,128)(2,1)} %copy.415), channel_id=1, replica_groups=mesh['slab'=32,'coil'=8] {'slab'}, dimensions={3} | all-to-all | bytes 1048576 | tf_op jit(solution)/shard_map/all_to_all | solution.py:102
  478.3 20.3 %all_to_all.165 = bf16[2,2,64,8,128]{4,1,3,0,2:T(2,128)(2,1)S(1)} all-to-all(bf16[2,2,64,8,128]{4,1,3,0,2:T(2,128)(2,1)S(1)} %copy.419), channel_id=1, replica_groups=mesh['slab'=32,'coil'=8] {'slab'}, dimensions={2} | all-to-all | bytes 1048576 | tf_op jit(solution)/shard_map/all_to_all | solution.py:111
  503.0 16.8 %all_to_all.166 = f32[2,2,256,128]{3,1,0,2:T(2,128)} all-to-all(f32[2,2,256,128]{3,1,0,2:T(2,128)} %copy.423), channel_id=1, replica_groups=mesh['slab'=32,'coil'=8] {'coil'}, dimensions={2} | all-to-all | bytes 1048576 | tf_op jit(solution)/shard_map/all_to_all | solution.py:120
  523.3 19.5 %all_to_all.167 = f32[256,1,2]{2,1,0:T(1,128)} all-to-all(f32[256,1,2]{2,1,0:T(1,128)S(1)} %broadcast_in_dim.15), channel_id=1, replica_groups=mesh['slab'=32,'coil'=8] {'slab','coil'}, dimensions={0} | all-to-all | bytes 4096 | tf_op jit(solution)/shard_map/all_to_all | solution.py:133
  548.7 19.5 %all_to_all.168 = f32[256,1,1]{2,1,0:T(1,128)} all-to-all(f32[256,1,1]{2,1,0:T(1,128)S(1)} %broadcast_in_dim.16), channel_id=1, replica_groups=mesh['slab'=32,'coil'=8] {'slab','coil'}, dimensions={0} | all-to-all | bytes 2048 | tf_op jit(solution)/shard_map/all_to_all | solution.py:133
  572.2 13.6 %all_gather.11 = f32[2,2,256,128]{3,1,0,2:T(2,128)S(1)} all-gather(f32[2,2,32,128]{3,1,0,2:T(2,128)S(1)} %multiply_add_fusion.4), channel_id=1, replica_groups=mesh['slab'=32,'coil'=8] {'coil'}, dimensions={2}, use_global_device_ids=true | all-gather | bytes 589824 | tf_op jit(solution)/shard_map/all_gather | solution.py:126
  591.6 3.9 fusion.34
  597.4 21.0 %all_to_all.169 = bf16[2,2,2,256,128]{4,1,2,0,3:T(2,128)(2,1)S(1)} all-to-all(bf16[2,2,2,256,128]{4,1,2,0,3:T(2,128)(2,1)} %copy.428), channel_id=1, replica_groups=mesh['slab'=32,'coil'=8] {'slab'}, dimensions={3} | all-to-all | bytes 1048576 | tf_op jit(solution)/shard_map/all_to_all | solution.py:102
  621.8 20.3 %all_to_all.170 = bf16[2,2,64,8,128]{4,1,3,0,2:T(2,128)(2,1)S(1)} all-to-all(bf16[2,2,64,8,128]{4,1,3,0,2:T(2,128)(2,1)S(1)} %copy.432), channel_id=1, replica_groups=mesh['slab'=32,'coil'=8] {'slab'}, dimensions={2} | all-to-all | bytes 1048576 | tf_op jit(solution)/shard_map/all_to_all | solution.py:111
  644.0 15.2 %all_to_all.171 = f32[2,2,256,128]{3,1,0,2:T(2,128)S(1)} all-to-all(f32[2,2,256,128]{3,1,0,2:T(2,128)S(1)} %copy.436), channel_id=1, replica_groups=mesh['slab'=32,'coil'=8] {'coil'}, dimensions={2} | all-to-all | bytes 1048576 | tf_op jit(solution)/shard_map/all_to_all | solution.py:120
  661.4 6.5 all-to-all-start.11
  668.3 12.6 %all-to-all-done.11 = f32[256,1,1]{2,1,0:T(1,128)S(1)} async-done(((f32[256,1,1]{2,1,0:T(1,128)}), f32[256,1,1]{2,1,0:T(1,128)S(1)}, u32[]{:S(2)}, u32[]{:S(2)}) %all-to-all-start.11) | async-done | bytes 1056 | tf_op jit(solution)/shard_map/all_to_all | solution.py:133
  (182 shorter events, 114.6 us)
Async XLA Ops:
  0.6 366.3 %copy-start = (f32[2,2,64,8,128]{4,3,2,1,0:T(8,128)S(1)}, f32[2,2,64,8,128]{4,3,2,1,0:T(8,128)}, u32[]{:S(2)}) copy-start(f32[2,2,64,8,128]{4,3,2,1,0:T(8,128)} %param.16) | copy-start | bytes 3145732
  1.6 5.9 collective-permute-start
  5.5 4.5 collective-permute-start.1
  10.0 8.1 %collective-permute-start.2 = (bf16[2,4,1,128]{3,2,1,0:T(2,128)(2,1)S(1)}, bf16[2,4,1,128]{3,2,1,0:T(2,128)(2,1)S(1)}, u32[]{:S(2)}, u32[]{:S(2)}) collective-permute-start(bf16[2,4,1,128]{3,2,1,0:T(2,128)(2,1)S(1)} %get-tuple-element.62), channel_id=1, source_target_pairs={{0,1},{1,2},{2,3},{3,4},{4,5},{5,6},{6,7},{8,9},{9,10},{10,11},{11... | collective-permute-start | bytes 6152 | tf_op jit(solution)/shard_map/ppermute | solution.py:25
  15.2 4.9 collective-permute-start.3
  31.4 2.8 copy-start.1
  36.8 10.5 %collective-permute-start.4 = (bf16[32,1,32,128]{3,2,1,0:T(8,128)(2,1)S(1)}, bf16[32,1,32,128]{3,2,1,0:T(8,128)(2,1)}, u32[]{:S(2)}, u32[]{:S(2)}) collective-permute-start(bf16[32,1,32,128]{3,2,1,0:T(8,128)(2,1)S(1)} %copy.380), channel_id=1, source_target_pairs={{0,8},{8,16},{16,24},{24,32},{32,40},{40,48},{48,56},{56,64},{64,7... | collective-permute-start | bytes 786440 | tf_op jit(solution)/shard_map/ppermute | solution.py:25
  44.2 9.1 %collective-permute-start.5 = (bf16[32,1,32,128]{3,2,1,0:T(8,128)(2,1)}, bf16[32,1,32,128]{3,2,1,0:T(8,128)(2,1)}, u32[]{:S(2)}, u32[]{:S(2)}) collective-permute-start(bf16[32,1,32,128]{3,2,1,0:T(8,128)(2,1)} %copy.381), channel_id=1, source_target_pairs={{8,0},{16,8},{24,16},{32,24},{40,32},{48,40},{56,48},{64,56},{72,6... | collective-permute-start | bytes 786440 | tf_op jit(solution)/shard_map/ppermute | solution.py:27
  56.9 13.7 %copy-start.4 = (bf16[32,1,32,128]{0,2,3,1:T(8,128)(2,1)S(1)}, bf16[32,1,32,128]{0,2,3,1:T(8,128)(2,1)}, u32[]{:S(2)}) copy-start(bf16[32,1,32,128]{0,2,3,1:T(8,128)(2,1)} %copy.382) | copy-start | bytes 786436
  56.9 13.7 %copy-start.5 = (bf16[32,1,32,128]{0,2,3,1:T(8,128)(2,1)S(1)}, bf16[32,1,32,128]{0,2,3,1:T(8,128)(2,1)}, u32[]{:S(2)}) copy-start(bf16[32,1,32,128]{0,2,3,1:T(8,128)(2,1)} %copy.383) | copy-start | bytes 786436
  58.9 7.7 %collective-permute-start.6 = (bf16[32,4,1,128]{0,2,3,1:T(2,128)(2,1)S(1)}, bf16[32,4,1,128]{0,2,3,1:T(2,128)(2,1)S(1)}, u32[]{:S(2)}, u32[]{:S(2)}) collective-permute-start(bf16[32,4,1,128]{0,2,3,1:T(2,128)(2,1)S(1)} %get-tuple-element.28), channel_id=1, source_target_pairs={{0,1},{1,2},{2,3},{3,4},{4,5},{5,6},{6,7},{8,9},{9,10},{10,11},{11... | collective-permute-start | bytes 98312 | tf_op jit(solution)/shard_map/ppermute | solution.py:25
  63.0 7.7 %collective-permute-start.7 = (bf16[32,4,1,128]{0,2,3,1:T(2,128)(2,1)S(1)}, bf16[32,4,1,128]{0,2,3,1:T(2,128)(2,1)S(1)}, u32[]{:S(2)}, u32[]{:S(2)}) collective-permute-start(bf16[32,4,1,128]{0,2,3,1:T(2,128)(2,1)S(1)} %get-tuple-element.29), channel_id=1, source_target_pairs={{1,0},{2,1},{3,2},{4,3},{5,4},{6,5},{7,6},{9,8},{10,9},{11,10},{12... | collective-permute-start | bytes 98312 | tf_op jit(solution)/shard_map/ppermute | solution.py:27
  88.5 10.0 %copy-start.25 = (pred[8,17]{0,1:T(8,128)(4,1)S(1)}, pred[8,17]{0,1:T(8,128)(4,1)}, u32[]{:S(2)}) copy-start(pred[8,17]{0,1:T(8,128)(4,1)} %constant.113) | copy-start | bytes 412
  88.5 10.0 %copy-start.26 = (bf16[3,3,3,32,32]{4,3,2,1,0:T(8,128)(2,1)S(1)}, bf16[3,3,3,32,32]{4,3,2,1,0:T(8,128)(2,1)}, u32[]{:S(2)}) copy-start(bf16[3,3,3,32,32]{4,3,2,1,0:T(8,128)(2,1)} %param.12) | copy-start | bytes 165892
  88.5 19.4 %slice-start = ((s8[4456448]{0:T(1024)(128)(4,1)}), s8[262144]{0:T(1024)(128)(4,1)S(1)}, s32[]{:S(2)}) async-start(s8[4456448]{0:T(1024)(128)(4,1)} %bitcast.324), calls=%async_computation.12 | async-start | bytes 524288
  98.5 9.5 %slice-start.1 = ((s8[4456448]{0:T(1024)(128)(4,1)}), s8[4194304]{0:T(1024)(128)(4,1)S(1)}, s32[]{:S(2)}) async-start(s8[4456448]{0:T(1024)(128)(4,1)} %bitcast.324), calls=%async_computation.13 | async-start | bytes 8388608
  115.4 11.5 %collective-permute-start.8 = (bf16[32,1,32,128]{3,2,1,0:T(8,128)(2,1)}, bf16[32,1,32,128]{3,2,1,0:T(8,128)(2,1)}, u32[]{:S(2)}, u32[]{:S(2)}) collective-permute-start(bf16[32,1,32,128]{3,2,1,0:T(8,128)(2,1)} %copy.388), channel_id=1, source_target_pairs={{0,8},{8,16},{16,24},{24,32},{32,40},{40,48},{48,56},{56,64},{64,7... | collective-permute-start | bytes 786440 | tf_op jit(solution)/shard_map/ppermute | solution.py:25
  123.2 20.8 %copy-start.11 = (f32[256,1,256]{2,0,1:T(8,128)S(1)}, f32[256,1,256]{2,0,1:T(8,128)}, u32[]{:S(2)}) copy-start(f32[256,1,256]{2,0,1:T(8,128)} %get-tuple-element.70) | copy-start | bytes 786436
  123.2 7.6 %collective-permute-start.9 = (bf16[32,1,32,128]{3,2,1,0:T(8,128)(2,1)}, bf16[32,1,32,128]{3,2,1,0:T(8,128)(2,1)}, u32[]{:S(2)}, u32[]{:S(2)}) collective-permute-start(bf16[32,1,32,128]{3,2,1,0:T(8,128)(2,1)} %copy.389), channel_id=1, source_target_pairs={{8,0},{16,8},{24,16},{32,24},{40,32},{48,40},{56,48},{64,56},{72,6... | collective-permute-start | bytes 786440 | tf_op jit(solution)/shard_map/ppermute | solution.py:27
  134.3 9.7 %copy-start.12 = (f32[256,1,256]{2,0,1:T(8,128)S(1)}, f32[256,1,256]{2,0,1:T(8,128)}, u32[]{:S(2)}) copy-start(f32[256,1,256]{2,0,1:T(8,128)} %get-tuple-element.71) | copy-start | bytes 786436
  134.3 9.7 %copy-start.13 = (f32[256,1,256]{2,0,1:T(8,128)S(1)}, f32[256,1,256]{2,0,1:T(8,128)}, u32[]{:S(2)}) copy-start(f32[256,1,256]{2,0,1:T(8,128)} %fusion.66) | copy-start | bytes 786436
  137.0 12.9 %collective-permute-start.10 = (bf16[32,4,1,128]{0,2,3,1:T(2,128)(2,1)}, bf16[32,4,1,128]{0,2,3,1:T(2,128)(2,1)}, u32[]{:S(2)}, u32[]{:S(2)}) collective-permute-start(bf16[32,4,1,128]{0,2,3,1:T(2,128)(2,1)} %get-tuple-element.26), channel_id=1, source_target_pairs={{0,1},{1,2},{2,3},{3,4},{4,5},{5,6},{6,7},{8,9},{9,10},{10,11},{11... | collective-permute-start | bytes 98312 | tf_op jit(solution)/shard_map/ppermute | solution.py:25
  142.1 8.0 %collective-permute-start.11 = (bf16[32,4,1,128]{0,2,3,1:T(2,128)(2,1)}, bf16[32,4,1,128]{0,2,3,1:T(2,128)(2,1)}, u32[]{:S(2)}, u32[]{:S(2)}) collective-permute-start(bf16[32,4,1,128]{0,2,3,1:T(2,128)(2,1)} %get-tuple-element.27), channel_id=1, source_target_pairs={{1,0},{2,1},{3,2},{4,3},{5,4},{6,5},{7,6},{9,8},{10,9},{11,10},{12... | collective-permute-start | bytes 98312 | tf_op jit(solution)/shard_map/ppermute | solution.py:27
  169.6 9.9 %copy-start.27 = (bf16[3,3,3,2,32]{4,3,2,1,0:T(2,128)(2,1)S(1)}, bf16[3,3,3,2,32]{4,3,2,1,0:T(2,128)(2,1)}, u32[]{:S(2)}) copy-start(bf16[3,3,3,2,32]{4,3,2,1,0:T(2,128)(2,1)} %param.13) | copy-start | bytes 10372
  319.3 24.9 %copy-start.2 = (f32[2,1,2,256,128]{3,4,1,2,0:T(8,128)S(1)}, f32[2,1,2,256,128]{3,4,1,2,0:T(8,128)}, u32[]{:S(2)}) copy-start(f32[2,1,2,256,128]{3,4,1,2,0:T(8,128)} %copy.490) | copy-start | bytes 1572868
  319.3 24.9 %copy-start.3 = (f32[2,1,2,256,128]{3,4,1,2,0:T(8,128)S(1)}, f32[2,1,2,256,128]{3,4,1,2,0:T(8,128)}, u32[]{:S(2)}) copy-start(f32[2,1,2,256,128]{3,4,1,2,0:T(8,128)} %copy.492) | copy-start | bytes 1572868
  319.3 26.1 %copy-start.8 = (f32[1,256,2,256]{3,1,2,0:T(8,128)S(1)}, f32[1,256,2,256]{3,1,2,0:T(8,128)}, u32[]{:S(2)}) copy-start(f32[1,256,2,256]{3,1,2,0:T(8,128)} %get-tuple-element.46) | copy-start | bytes 1572868
  319.3 26.1 %copy-start.9 = (f32[1,256,2,256]{3,1,2,0:T(8,128)S(1)}, f32[1,256,2,256]{3,1,2,0:T(8,128)}, u32[]{:S(2)}) copy-start(f32[1,256,2,256]{3,1,2,0:T(8,128)} %get-tuple-element.55) | copy-start | bytes 1572868
  325.5 24.5 %copy-start.22 = (f32[2,2,32,128]{3,1,0,2:T(2,128)}, f32[2,2,32,128]{3,1,0,2:T(2,128)S(1)}, u32[]{:S(2)}) copy-start(f32[2,2,32,128]{3,1,0,2:T(2,128)S(1)} %fusion.74) | copy-start | bytes 196612
  340.6 24.1 %copy-start.24 = (s32[64,8]{0,1:T(8,128)S(1)}, s32[64,8]{0,1:T(8,128)}, u32[]{:S(2)}) copy-start(s32[64,8]{0,1:T(8,128)} %param.17) | copy-start | bytes 6148
  350.0 31.4 %all-to-all-start = ((bf16[2,2,2,256,128]{4,1,2,0,3:T(2,128)(2,1)}), bf16[2,2,2,256,128]{4,1,2,0,3:T(2,128)(2,1)S(1)}, u32[]{:S(2)}, u32[]{:S(2)}) async-start(bf16[2,2,2,256,128]{4,1,2,0,3:T(2,128)(2,1)} %copy.404), calls=%async_computation | async-start | bytes 1048576 | tf_op jit(solution)/shard_map/all_to_all | solution.py:102
  366.9 17.8 %copy-start.15 = (f32[1,64,2,64]{3,1,2,0:T(8,128)}, f32[1,64,2,64]{3,1,2,0:T(8,128)S(1)}, u32[]{:S(2)}) copy-start(f32[1,64,2,64]{3,1,2,0:T(8,128)S(1)} %get-tuple-element.64) | copy-start | bytes 98308
  366.9 108.2 %copy-start.14 = (f32[1,64,2,64]{3,1,2,0:T(8,128)}, f32[1,64,2,64]{3,1,2,0:T(8,128)S(1)}, u32[]{:S(2)}) copy-start(f32[1,64,2,64]{3,1,2,0:T(8,128)S(1)} %get-tuple-element.57) | copy-start | bytes 98308
  381.4 2.1 copy-start.16
  381.4 2.2 copy-start.19
  381.5 24.1 %copy-start.6 = (f32[1,256,2,256]{3,1,2,0:T(8,128)S(1)}, f32[1,256,2,256]{3,1,2,0:T(8,128)}, u32[]{:S(2)}) copy-start(f32[1,256,2,256]{3,1,2,0:T(8,128)} %get-tuple-element.47) | copy-start | bytes 1572868
  381.5 24.1 %copy-start.7 = (f32[1,256,2,256]{3,1,2,0:T(8,128)S(1)}, f32[1,256,2,256]{3,1,2,0:T(8,128)}, u32[]{:S(2)}) copy-start(f32[1,256,2,256]{3,1,2,0:T(8,128)} %get-tuple-element.54) | copy-start | bytes 1572868
  453.8 22.8 %copy-start.17 = (f32[1,64,2,64]{3,1,2,0:T(8,128)S(1)}, f32[1,64,2,64]{3,1,2,0:T(8,128)}, u32[]{:S(2)}) copy-start(f32[1,64,2,64]{3,1,2,0:T(8,128)} %get-tuple-element.56) | copy-start | bytes 98308
  453.8 22.8 %copy-start.20 = (f32[1,64,2,64]{3,1,2,0:T(8,128)S(1)}, f32[1,64,2,64]{3,1,2,0:T(8,128)}, u32[]{:S(2)}) copy-start(f32[1,64,2,64]{3,1,2,0:T(8,128)} %get-tuple-element.65) | copy-start | bytes 98308
  521.0 49.0 %copy-start.10 = (f32[2,2,32,128]{3,1,0,2:T(2,128)}, f32[2,2,32,128]{3,1,0,2:T(2,128)S(1)}, u32[]{:S(2)}) copy-start(f32[2,2,32,128]{3,1,0,2:T(2,128)S(1)} %reduce_sum.150) | copy-start | bytes 196612
  597.4 22.7 %copy-start.18 = (f32[1,64,2,64]{3,1,2,0:T(8,128)S(1)}, f32[1,64,2,64]{3,1,2,0:T(8,128)}, u32[]{:S(2)}) copy-start(f32[1,64,2,64]{3,1,2,0:T(8,128)} %get-tuple-element.56) | copy-start | bytes 98308
  597.4 22.7 %copy-start.21 = (f32[1,64,2,64]{3,1,2,0:T(8,128)S(1)}, f32[1,64,2,64]{3,1,2,0:T(8,128)}, u32[]{:S(2)}) copy-start(f32[1,64,2,64]{3,1,2,0:T(8,128)} %get-tuple-element.65) | copy-start | bytes 98308
  643.4 39.7 %copy-start.23 = (f32[2,2,32,128]{3,1,0,2:T(2,128)S(1)}, f32[2,2,32,128]{3,1,0,2:T(2,128)}, u32[]{:S(2)}) copy-start(f32[2,2,32,128]{3,1,0,2:T(2,128)} %copy-done.22) | copy-start | bytes 196612
  661.4 19.5 %all-to-all-start.11 = ((f32[256,1,1]{2,1,0:T(1,128)}), f32[256,1,1]{2,1,0:T(1,128)S(1)}, u32[]{:S(2)}, u32[]{:S(2)}) async-start(f32[256,1,1]{2,1,0:T(1,128)} %broadcast_in_dim.17), calls=%async_computation.11 | async-start | bytes 262144 | tf_op jit(solution)/shard_map/all_to_all | solution.py:133

commit v4 on v2

--- a/solution.py
+++ b/solution.py
@@ -174,23 +174,39 @@
 
     solution = estimate
     residual = operator(estimate, True)
-    direction = residual
-    norm_now = None
+    direction = image = curvature = norm_now = None
     for iteration in range(ITERS):
         final_turn = iteration + 1 == ITERS
-        image = operator(direction, False) + REG_WEIGHT * direction
-        if norm_now is None:
-            sums = global_sums(jnp.stack([jnp.sum(residual * residual), jnp.sum(direction * image)]))
-            norm_now, curvature = sums[0], sums[1]
+        residual_image = operator(residual, False) + REG_WEIGHT * residual
+        if direction is None:
+            sums = global_sums(
+                jnp.stack([jnp.sum(residual * residual), jnp.sum(residual * residual_image)])
+            )
+            norm_next = sums[0]
+            curvature = sums[1]
+            direction = residual
+            image = residual_image
         else:
-            curvature = global_sums(jnp.stack([jnp.sum(direction * image)]))[0]
+            sums = global_sums(
+                jnp.stack(
+                    [
+                        jnp.sum(residual * residual),
+                        jnp.sum(residual * residual_image),
+                        jnp.sum(residual * image),
+                        jnp.sum(direction * residual_image),
+                    ]
+                )
+            )
+            norm_next = sums[0]
+            ratio = norm_next / norm_now
+            curvature = sums[1] + ratio * (sums[2] + sums[3]) + ratio * ratio * curvature
+            direction = residual + ratio * direction
+            image = residual_image + ratio * image
+        norm_now = norm_next
         step_size = norm_now / curvature
         solution = solution + step_size * direction
         if not final_turn:
             residual = residual - step_size * image
-            norm_next = global_sums(jnp.stack([jnp.sum(residual * residual)]))[0]
-            direction = residual + norm_next / norm_now * direction
-            norm_now = norm_next
     recon = solution
     next_sample = jnp.sqrt(prior_level) * recon + jnp.sqrt(1.0 - prior_level) * noise_pred
     return (recon, next_sample)

time: 463 us -> 445 us (0.961)
  blocking collectives: 213 us -> 194 us
    all_to_all x2 -> x1, blocking collectives: 38.7 us -> 19.2 us  [global_sums(): lax.all_to_all(spread, axes, split_axis=0, concat_axis=0, tiled=True)]
where the time goes in v4:
time: 445 us; the launch traced here: 440 us
  blocking collectives  194 us (44%)
  starting transfers between devices  67.4 us (15%)
  matrix products  50.1 us (11%)
  waiting for transfers between devices  49.7 us (11%)
  other arithmetic  40.1 us (9%)
  local copies, waits for them, and re-layouts  30.5 us (7%)
  between operations  8.69 us (2%)
    all_to_all x3, blocking collectives, coil_term(): lax.all_to_all(back.astype(jnp.bfloat16), 'slab', split_axis=2, concat_ax...  60.9 us
    all_to_all x2, blocking collectives, coil_term(): lax.all_to_all(spectrum.astype(jnp.bfloat16), 'slab', split_axis=3, conca...  42.2 us
    all_gather x3, blocking collectives, gather_rows(): return lax.all_gather(value, 'coil', axis=2, tiled=True)  39.1 us
    all_to_all x2, blocking collectives, combine_coils(): lax.all_to_all(partial_value, 'coil', split_axis=2, concat_axis=0, tiled=...  32.1 us
    dot_general x27, matrix products, conv_layer(): jnp.einsum('aoc,czyx->aozyx', weights[depth_shift, row_shift], window, pr...  25.7 us
    ppermute x6, starting transfers between devices, extended(): lax.ppermute(tail, axis, [(i, (i + 1) % count) for i in range(ends)])  25.6 us
    all_to_all x1, blocking collectives, global_sums(): lax.all_to_all(spread, axes, split_axis=0, concat_axis=0, tiled=True)  19.2 us
    all_to_all x1, starting transfers between devices, coil_term(): lax.all_to_all(spectrum.astype(jnp.bfloat16), 'slab', split_axis=3, conca...  17.5 us
  transfers between devices with their start and end apart: 15, of which 8 were waited for; matrix products, arithmetic and copies ran while one was open for 5% of the time, Pallas kernels for 0%

profile of v4, /device:TPU:1, one launch (start us, length us, event | category | flops | bytes accessed | tf_op | source)
XLA Modules:
  0.0 440.1 jit_solution(14064945362731531405)
XLA Ops:
  1.7 3.9 collective-permute-start
  9.7 3.0 fusion.146
  16.0 4.0 collective-permute-start.2
  20.1 2.1 collective-permute-start.3
  27.6 2.3 convolution_bitcast_fusion.14
  29.9 2.3 convolution_bitcast_fusion.16
  32.3 7.1 %multiply_convert_fusion = (bf16[1,32,2,32,128]{4,1,0,3,2:T(8,128)(2,1)S(1)}, f32[1,32,2,32,128]{4,1,0,3,2:T(8,128)S(1)}) fusion(f32[3,32,2,32,128]{4,1,3,2,0:T(8,128)S(1)} %convolution_bitcast_fusion.9, f32[3,32,2,32,128]{4,1,3,2,0:T(8,128)S(1)} %convolution_bitcast_fusion.10, f32[3,32,2,32,128]{4,1,3,2,0:T(8,128)S(1)} %convolution_bitcast_fusion.11, ...), kind=kLoop, calls=%fused_computation.180 | loop fusion | flops 8388608 | bytes 39322112 | tf_op jit(solution)/shard_map/convert_element_type | solution.py:152
  41.4 4.3 collective-permute-start.4
  47.5 2.9 collective-permute-done.4
  50.4 4.1 collective-permute-done.5
  54.5 4.4 collective-permute-start.6
  58.9 2.1 collective-permute-start.7
  61.0 2.2 convolution_bitcast_fusion.7
  63.3 2.2 convolution_bitcast_fusion.1
  69.0 7.6 %add_convert_fusion.1 = (bf16[32,2,32,128]{3,0,2,1:T(8,128)(2,1)S(1)}, f32[1,32,2,32,128]{4,1,3,2,0:T(8,128)}) fusion(bf16[32,2,32,128]{3,0,2,1:T(8,128)(2,1)S(1)} %multiply_convert_fusion.1, f32[3,32,2,32,128]{4,1,3,2,0:T(8,128)S(1)} %convolution_bitcast_fusion, f32[3,32,2,32,128]{4,1,3,2,0:T(8,128)} %convolution_bitcast_fusion.1, ...), kind=kLoop, calls=%fused_computation.179 | loop fusion | flops 8650752 | bytes 39845888 | tf_op jit(solution)/shard_map/convert_element_type | solution.py:153
  76.6 3.1 collective-permute-start.8
  81.1 4.4 convolution_bitcast_fusion.30
  85.5 3.5 collective-permute-done.9
  89.0 5.9 %collective-permute-start.10 = (bf16[32,4,1,128]{3,0,2,1:T(8,128)(2,1)S(1)}, bf16[32,4,1,128]{3,0,2,1:T(8,128)(2,1)S(1)}, u32[]{:S(2)}, u32[]{:S(2)}) collective-permute-start(bf16[32,4,1,128]{3,0,2,1:T(8,128)(2,1)S(1)} %get-tuple-element.46), channel_id=1, source_target_pairs={{0,1},{1,2},{2,3},{3,4},{4,5},{5,6},{6,7},{8,9},{9,10},{10,11},{11... | collective-permute-start | bytes 98312 | tf_op jit(solution)/shard_map/ppermute | solution.py:25
  94.9 2.3 collective-permute-start.11
  97.7 2.4 collective-permute-done.11
  104.5 11.2 %all_gather.9 = f32[2,2,256,128]{3,0,2,1:T(2,128)S(1)} all-gather(f32[2,2,32,128]{3,0,2,1:T(2,128)S(1)} %get-tuple-element.30), channel_id=1, replica_groups=mesh['slab'=32,'coil'=8] {'coil'}, dimensions={2}, use_global_device_ids=true | all-gather | bytes 589824 | tf_op jit(solution)/shard_map/all_gather | solution.py:135
  120.9 3.7 fusion.15
  124.6 2.0 copy.627
  126.6 17.5 %all-to-all-start = ((bf16[2,2,2,256,128]{4,1,2,0,3:T(2,128)(2,1)}), bf16[2,2,2,256,128]{4,1,2,0,3:T(2,128)(2,1)S(1)}, u32[]{:S(2)}, u32[]{:S(2)}) async-start(bf16[2,2,2,256,128]{4,1,2,0,3:T(2,128)(2,1)} %copy.627), calls=%async_computation | async-start | bytes 1048576 | tf_op jit(solution)/shard_map/all_to_all | solution.py:111
  145.1 2.0 convolution_bitcast_fusion.26
  147.1 13.7 %all-to-all-done = bf16[2,2,2,256,128]{4,1,2,0,3:T(2,128)(2,1)S(1)} async-done(((bf16[2,2,2,256,128]{4,1,2,0,3:T(2,128)(2,1)}), bf16[2,2,2,256,128]{4,1,2,0,3:T(2,128)(2,1)S(1)}, u32[]{:S(2)}, u32[]{:S(2)}) %all-to-all-start) | async-done | bytes 524320 | tf_op jit(solution)/shard_map/all_to_all | solution.py:111
  164.6 20.3 %all_to_all.156 = bf16[2,2,64,8,128]{4,1,3,0,2:T(2,128)(2,1)S(1)} all-to-all(bf16[2,2,64,8,128]{4,1,3,0,2:T(2,128)(2,1)S(1)} %copy.631), channel_id=1, replica_groups=mesh['slab'=32,'coil'=8] {'slab'}, dimensions={2} | all-to-all | bytes 1048576 | tf_op jit(solution)/shard_map/all_to_all | solution.py:120
  187.2 2.0 copy.635
  189.3 16.8 %all_to_all.157 = f32[2,2,256,128]{3,1,0,2:T(2,128)} all-to-all(f32[2,2,256,128]{3,1,0,2:T(2,128)} %copy.635), channel_id=1, replica_groups=mesh['slab'=32,'coil'=8] {'coil'}, dimensions={2} | all-to-all | bytes 1048576 | tf_op jit(solution)/shard_map/all_to_all | solution.py:129
  207.3 14.0 %all_gather.10 = f32[2,2,256,128]{3,1,0,2:T(2,128)S(1)} all-gather(f32[2,2,32,128]{3,1,0,2:T(2,128)S(1)} %reduce_sum.155), channel_id=1, replica_groups=mesh['slab'=32,'coil'=8] {'coil'}, dimensions={2}, use_global_device_ids=true | all-gather | bytes 589824 | tf_op jit(solution)/shard_map/all_gather | solution.py:135
  226.2 3.9 fusion.14
  230.1 2.0 copy.638
  232.1 21.2 %all_to_all.158 = bf16[2,2,2,256,128]{4,1,2,0,3:T(2,128)(2,1)S(1)} all-to-all(bf16[2,2,2,256,128]{4,1,2,0,3:T(2,128)(2,1)} %copy.638), channel_id=1, replica_groups=mesh['slab'=32,'coil'=8] {'slab'}, dimensions={3} | all-to-all | bytes 1048576 | tf_op jit(solution)/shard_map/all_to_all | solution.py:111
  255.8 20.3 %all_to_all.159 = bf16[2,2,64,8,128]{4,1,3,0,2:T(2,128)(2,1)S(1)} all-to-all(bf16[2,2,64,8,128]{4,1,3,0,2:T(2,128)(2,1)S(1)} %copy.642), channel_id=1, replica_groups=mesh['slab'=32,'coil'=8] {'slab'}, dimensions={2} | all-to-all | bytes 1048576 | tf_op jit(solution)/shard_map/all_to_all | solution.py:120
  278.5 2.0 copy.646
  280.5 7.4 %all-to-all-start.5 = ((f32[2,2,256,128]{3,1,0,2:T(2,128)}), f32[2,2,256,128]{3,1,0,2:T(2,128)}, u32[]{:S(2)}, u32[]{:S(2)}) async-start(f32[2,2,256,128]{3,1,0,2:T(2,128)} %copy.646), calls=%async_computation.5 | async-start | bytes 1048576 | tf_op jit(solution)/shard_map/all_to_all | solution.py:129
  288.6 8.8 %all-to-all-done.5 = f32[2,2,256,128]{3,1,0,2:T(2,128)} async-done(((f32[2,2,256,128]{3,1,0,2:T(2,128)}), f32[2,2,256,128]{3,1,0,2:T(2,128)}, u32[]{:S(2)}, u32[]{:S(2)}) %all-to-all-start.5) | async-done | bytes 524320 | tf_op jit(solution)/shard_map/all_to_all | solution.py:129
  300.7 19.2 %all_to_all.160 = f32[256,1,2]{2,1,0:T(1,128)} all-to-all(f32[256,1,2]{2,1,0:T(1,128)S(1)} %broadcast_in_dim.4), channel_id=1, replica_groups=mesh['slab'=32,'coil'=8] {'slab','coil'}, dimensions={0} | all-to-all | bytes 4096 | tf_op jit(solution)/shard_map/all_to_all | solution.py:142
  323.1 13.9 %all_gather.11 = f32[2,2,256,128]{3,0,2,1:T(2,128)S(1)} all-gather(f32[2,2,32,128]{3,0,2,1:T(2,128)S(1)} %multiply_subtract_fusion.3), channel_id=1, replica_groups=mesh['slab'=32,'coil'=8] {'coil'}, dimensions={2}, use_global_device_ids=true | all-gather | bytes 589824 | tf_op jit(solution)/shard_map/all_gather | solution.py:135
  342.2 3.9 fusion.13
  346.1 2.0 copy.655
  348.2 21.0 %all_to_all.161 = bf16[2,2,2,256,128]{4,1,2,0,3:T(2,128)(2,1)S(1)} all-to-all(bf16[2,2,2,256,128]{4,1,2,0,3:T(2,128)(2,1)} %copy.655), channel_id=1, replica_groups=mesh['slab'=32,'coil'=8] {'slab'}, dimensions={3} | all-to-all | bytes 1048576 | tf_op jit(solution)/shard_map/all_to_all | solution.py:111
  371.7 20.3 %all_to_all.162 = bf16[2,2,64,8,128]{4,1,3,0,2:T(2,128)(2,1)S(1)} all-to-all(bf16[2,2,64,8,128]{4,1,3,0,2:T(2,128)(2,1)S(1)} %copy.659), channel_id=1, replica_groups=mesh['slab'=32,'coil'=8] {'slab'}, dimensions={2} | all-to-all | bytes 1048576 | tf_op jit(solution)/shard_map/all_to_all | solution.py:120
  393.9 15.4 %all_to_all.163 = f32[2,2,256,128]{3,1,0,2:T(2,128)S(1)} all-to-all(f32[2,2,256,128]{3,1,0,2:T(2,128)S(1)} %copy.663), channel_id=1, replica_groups=mesh['slab'=32,'coil'=8] {'coil'}, dimensions={2} | all-to-all | bytes 1048576 | tf_op jit(solution)/shard_map/all_to_all | solution.py:129
  410.2 2.6 pad_maximum_fusion.30
  413.6 6.5 %all-to-all-start.10 = ((f32[256,1,4]{2,1,0:T(1,128)}), f32[256,1,4]{2,1,0:T(1,128)S(1)}, u32[]{:S(2)}, u32[]{:S(2)}) async-start(f32[256,1,4]{2,1,0:T(1,128)} %broadcast_in_dim.5), calls=%async_computation.10 | async-start | bytes 262144 | tf_op jit(solution)/shard_map/all_to_all | solution.py:142
  420.3 12.8 %all-to-all-done.10 = f32[256,1,4]{2,1,0:T(1,128)S(1)} async-done(((f32[256,1,4]{2,1,0:T(1,128)}), f32[256,1,4]{2,1,0:T(1,128)S(1)}, u32[]{:S(2)}, u32[]{:S(2)}) %all-to-all-start.10) | async-done | bytes 4128 | tf_op jit(solution)/shard_map/all_to_all | solution.py:142
  (181 shorter events, 68.8 us)
Async XLA Ops:
  0.6 144.4 %copy-start = (f32[2,2,64,8,128]{4,3,2,1,0:T(8,128)S(1)}, f32[2,2,64,8,128]{4,3,2,1,0:T(8,128)}, u32[]{:S(2)}) copy-start(f32[2,2,64,8,128]{4,3,2,1,0:T(8,128)} %param.16) | copy-start | bytes 3145732
  0.6 12.1 %copy-start.26 = (bf16[3,3,3,2,32]{4,3,2,1,0:T(2,128)(2,1)S(1)}, bf16[3,3,3,2,32]{4,3,2,1,0:T(2,128)(2,1)}, u32[]{:S(2)}) copy-start(bf16[3,3,3,2,32]{4,3,2,1,0:T(2,128)(2,1)} %param.13) | copy-start | bytes 10372
  1.7 14.3 %collective-permute-start = (bf16[2,1,32,128]{3,0,2,1:T(2,128)(2,1)S(1)}, bf16[2,1,32,128]{3,0,2,1:T(2,128)(2,1)S(1)}, u32[]{:S(2)}, u32[]{:S(2)}) collective-permute-start(bf16[2,1,32,128]{3,0,2,1:T(2,128)(2,1)S(1)} %get-tuple-element.82), channel_id=1, source_target_pairs={{0,8},{8,16},{16,24},{24,32},{32,40},{40,48},{48,56},{56,64},{64,7... | collective-permute-start | bytes 49160 | tf_op jit(solution)/shard_map/ppermute | solution.py:25
  5.6 10.4 %collective-permute-start.1 = (bf16[2,1,32,128]{3,0,2,1:T(2,128)(2,1)S(1)}, bf16[2,1,32,128]{3,0,2,1:T(2,128)(2,1)S(1)}, u32[]{:S(2)}, u32[]{:S(2)}) collective-permute-start(bf16[2,1,32,128]{3,0,2,1:T(2,128)(2,1)S(1)} %get-tuple-element.83), channel_id=1, source_target_pairs={{8,0},{16,8},{24,16},{32,24},{40,32},{48,40},{56,48},{64,56},{72,6... | collective-permute-start | bytes 49160 | tf_op jit(solution)/shard_map/ppermute | solution.py:27
  9.6 3.7 copy-start.5
  12.7 2.0 copy-start.24
  13.3 8.9 %copy-start.25 = (bf16[3,3,3,32,2]{3,4,2,1,0:T(2,128)(2,1)S(1)}, bf16[3,3,3,32,2]{3,4,2,1,0:T(2,128)(2,1)}, u32[]{:S(2)}) copy-start(bf16[3,3,3,32,2]{3,4,2,1,0:T(2,128)(2,1)} %param.11) | copy-start | bytes 10372
  16.0 7.4 %collective-permute-start.2 = (bf16[2,4,1,128]{3,0,2,1:T(2,128)(2,1)S(1)}, bf16[2,4,1,128]{3,0,2,1:T(2,128)(2,1)S(1)}, u32[]{:S(2)}, u32[]{:S(2)}) collective-permute-start(bf16[2,4,1,128]{3,0,2,1:T(2,128)(2,1)S(1)} %get-tuple-element.78), channel_id=1, source_target_pairs={{0,1},{1,2},{2,3},{3,4},{4,5},{5,6},{6,7},{8,9},{9,10},{10,11},{11... | collective-permute-start | bytes 6152 | tf_op jit(solution)/shard_map/ppermute | solution.py:25
  20.1 4.9 %collective-permute-start.3 = (bf16[2,4,1,128]{3,0,2,1:T(2,128)(2,1)S(1)}, bf16[2,4,1,128]{3,0,2,1:T(2,128)(2,1)S(1)}, u32[]{:S(2)}, u32[]{:S(2)}) collective-permute-start(bf16[2,4,1,128]{3,0,2,1:T(2,128)(2,1)S(1)} %get-tuple-element.79), channel_id=1, source_target_pairs={{1,0},{2,1},{3,2},{4,3},{5,4},{6,5},{7,6},{9,8},{10,9},{11,10},{12... | collective-permute-start | bytes 6152 | tf_op jit(solution)/shard_map/ppermute | solution.py:27
  27.6 4.7 %copy-start.1 = (f32[3,32,2,32,128]{4,1,0,3,2:T(8,128)S(1)}, f32[3,32,2,32,128]{4,1,0,3,2:T(8,128)}, u32[]{:S(2)}) copy-start(f32[3,32,2,32,128]{4,1,0,3,2:T(8,128)} %fusion.146) | copy-start | bytes 9437188
  27.6 4.7 %copy-start.27 = (f32[32]{0:T(128)S(1)}, f32[32]{0:T(128)}, u32[]{:S(2)}) copy-start(f32[32]{0:T(128)} %convolution_bitcast_fusion.39) | copy-start | bytes 388
  39.3 7.6 %copy-start.4 = (bf16[1,32,2,32,128]{4,1,0,3,2:T(8,128)(2,1)}, bf16[1,32,2,32,128]{4,1,0,3,2:T(8,128)(2,1)S(1)}, u32[]{:S(2)}) copy-start(bf16[1,32,2,32,128]{4,1,0,3,2:T(8,128)(2,1)S(1)} %get-tuple-element.34) | copy-start | bytes 1572868
  39.4 7.6 %copy-start.23 = (bf16[3,3,3,32,32]{4,3,2,1,0:T(8,128)(2,1)S(1)}, bf16[3,3,3,32,32]{4,3,2,1,0:T(8,128)(2,1)}, u32[]{:S(2)}) copy-start(bf16[3,3,3,32,32]{4,3,2,1,0:T(8,128)(2,1)} %param.12) | copy-start | bytes 165892
  41.4 9.0 %collective-permute-start.4 = (bf16[32,1,32,128]{3,0,2,1:T(8,128)(2,1)S(1)}, bf16[32,1,32,128]{3,0,2,1:T(8,128)(2,1)S(1)}, u32[]{:S(2)}, u32[]{:S(2)}) collective-permute-start(bf16[32,1,32,128]{3,0,2,1:T(8,128)(2,1)S(1)} %get-tuple-element.64), channel_id=1, source_target_pairs={{0,8},{8,16},{16,24},{24,32},{32,40},{40,48},{48,56},{56,64},{64,7... | collective-permute-start | bytes 786440 | tf_op jit(solution)/shard_map/ppermute | solution.py:25
  45.7 8.8 %collective-permute-start.5 = (bf16[32,1,32,128]{3,0,2,1:T(8,128)(2,1)S(1)}, bf16[32,1,32,128]{3,0,2,1:T(8,128)(2,1)S(1)}, u32[]{:S(2)}, u32[]{:S(2)}) collective-permute-start(bf16[32,1,32,128]{3,0,2,1:T(8,128)(2,1)S(1)} %get-tuple-element.65), channel_id=1, source_target_pairs={{8,0},{16,8},{24,16},{32,24},{40,32},{48,40},{56,48},{64,56},{72,6... | collective-permute-start | bytes 786440 | tf_op jit(solution)/shard_map/ppermute | solution.py:27
  54.5 10.9 %collective-permute-start.6 = (bf16[32,4,1,128]{3,0,2,1:T(8,128)(2,1)S(1)}, bf16[32,4,1,128]{3,0,2,1:T(8,128)(2,1)S(1)}, u32[]{:S(2)}, u32[]{:S(2)}) collective-permute-start(bf16[32,4,1,128]{3,0,2,1:T(8,128)(2,1)S(1)} %get-tuple-element.50), channel_id=1, source_target_pairs={{0,1},{1,2},{2,3},{3,4},{4,5},{5,6},{6,7},{8,9},{9,10},{10,11},{11... | collective-permute-start | bytes 98312 | tf_op jit(solution)/shard_map/ppermute | solution.py:25
  58.9 6.6 %collective-permute-start.7 = (bf16[32,4,1,128]{3,0,2,1:T(8,128)(2,1)S(1)}, bf16[32,4,1,128]{3,0,2,1:T(8,128)(2,1)S(1)}, u32[]{:S(2)}, u32[]{:S(2)}) collective-permute-start(bf16[32,4,1,128]{3,0,2,1:T(8,128)(2,1)S(1)} %get-tuple-element.51), channel_id=1, source_target_pairs={{1,0},{2,1},{3,2},{4,3},{5,4},{6,5},{7,6},{9,8},{10,9},{11,10},{12... | collective-permute-start | bytes 98312 | tf_op jit(solution)/shard_map/ppermute | solution.py:27
  68.9 12.1 %copy-start.29 = (bf16[1,1,3,2,32]{4,3,2,1,0:T(2,128)(2,1)S(1)}, bf16[1,1,3,2,32]{4,3,2,1,0:T(2,128)(2,1)}, u32[]{:S(2)}) copy-start(bf16[1,1,3,2,32]{4,3,2,1,0:T(2,128)(2,1)} %get-tuple-element.88) | copy-start | bytes 1156
  76.6 8.8 %collective-permute-start.8 = (bf16[32,1,32,128]{3,0,2,1:T(8,128)(2,1)S(1)}, bf16[32,1,32,128]{3,0,2,1:T(8,128)(2,1)S(1)}, u32[]{:S(2)}, u32[]{:S(2)}) collective-permute-start(bf16[32,1,32,128]{3,0,2,1:T(8,128)(2,1)S(1)} %get-tuple-element.62), channel_id=1, source_target_pairs={{0,8},{8,16},{16,24},{24,32},{32,40},{40,48},{48,56},{56,64},{64,7... | collective-permute-start | bytes 786440 | tf_op jit(solution)/shard_map/ppermute | solution.py:25
  79.8 9.2 %collective-permute-start.9 = (bf16[32,1,32,128]{3,0,2,1:T(8,128)(2,1)S(1)}, bf16[32,1,32,128]{3,0,2,1:T(8,128)(2,1)S(1)}, u32[]{:S(2)}, u32[]{:S(2)}) collective-permute-start(bf16[32,1,32,128]{3,0,2,1:T(8,128)(2,1)S(1)} %get-tuple-element.63), channel_id=1, source_target_pairs={{8,0},{16,8},{24,16},{32,24},{40,32},{48,40},{56,48},{64,56},{72,6... | collective-permute-start | bytes 786440 | tf_op jit(solution)/shard_map/ppermute | solution.py:27
  89.0 8.7 %collective-permute-start.10 = (bf16[32,4,1,128]{3,0,2,1:T(8,128)(2,1)S(1)}, bf16[32,4,1,128]{3,0,2,1:T(8,128)(2,1)S(1)}, u32[]{:S(2)}, u32[]{:S(2)}) collective-permute-start(bf16[32,4,1,128]{3,0,2,1:T(8,128)(2,1)S(1)} %get-tuple-element.46), channel_id=1, source_target_pairs={{0,1},{1,2},{2,3},{3,4},{4,5},{5,6},{6,7},{8,9},{9,10},{10,11},{11... | collective-permute-start | bytes 98312 | tf_op jit(solution)/shard_map/ppermute | solution.py:25
  94.9 5.2 %collective-permute-start.11 = (bf16[32,4,1,128]{3,0,2,1:T(8,128)(2,1)S(1)}, bf16[32,4,1,128]{3,0,2,1:T(8,128)(2,1)S(1)}, u32[]{:S(2)}, u32[]{:S(2)}) collective-permute-start(bf16[32,4,1,128]{3,0,2,1:T(8,128)(2,1)S(1)} %get-tuple-element.47), channel_id=1, source_target_pairs={{1,0},{2,1},{3,2},{4,3},{5,4},{6,5},{7,6},{9,8},{10,9},{11,10},{12... | collective-permute-start | bytes 98312 | tf_op jit(solution)/shard_map/ppermute | solution.py:27
  100.6 2.7 copy-start.21
  103.3 17.6 %copy-start.3 = (f32[1,256,2,256]{3,1,2,0:T(8,128)S(1)}, f32[1,256,2,256]{3,1,2,0:T(8,128)}, u32[]{:S(2)}) copy-start(f32[1,256,2,256]{3,1,2,0:T(8,128)} %get-tuple-element.56) | copy-start | bytes 1572868
  104.5 12.4 %copy-start.19 = (f32[2,2,32,128]{3,0,2,1:T(2,128)}, f32[2,2,32,128]{3,0,2,1:T(2,128)S(1)}, u32[]{:S(2)}) copy-start(f32[2,2,32,128]{3,0,2,1:T(2,128)S(1)} %get-tuple-element.30) | copy-start | bytes 196612
  119.8 24.3 %copy-start.28 = (s32[64,8]{0,1:T(8,128)S(1)}, s32[64,8]{0,1:T(8,128)}, u32[]{:S(2)}) copy-start(s32[64,8]{0,1:T(8,128)} %param.17) | copy-start | bytes 6148
  126.6 34.2 %all-to-all-start = ((bf16[2,2,2,256,128]{4,1,2,0,3:T(2,128)(2,1)}), bf16[2,2,2,256,128]{4,1,2,0,3:T(2,128)(2,1)S(1)}, u32[]{:S(2)}, u32[]{:S(2)}) async-start(bf16[2,2,2,256,128]{4,1,2,0,3:T(2,128)(2,1)} %copy.627), calls=%async_computation | async-start | bytes 1048576 | tf_op jit(solution)/shard_map/all_to_all | solution.py:111
  145.0 17.9 %copy-start.10 = (f32[1,64,2,64]{3,1,2,0:T(8,128)}, f32[1,64,2,64]{3,1,2,0:T(8,128)S(1)}, u32[]{:S(2)}) copy-start(f32[1,64,2,64]{3,1,2,0:T(8,128)S(1)} %get-tuple-element.80) | copy-start | bytes 98308
  145.0 17.9 %copy-start.13 = (f32[1,64,2,64]{3,1,2,0:T(8,128)}, f32[1,64,2,64]{3,1,2,0:T(8,128)S(1)}, u32[]{:S(2)}) copy-start(f32[1,64,2,64]{3,1,2,0:T(8,128)S(1)} %get-tuple-element.70) | copy-start | bytes 98308
  145.0 17.9 %copy-start.16 = (f32[1,64,2,64]{3,1,2,0:T(8,128)}, f32[1,64,2,64]{3,1,2,0:T(8,128)S(1)}, u32[]{:S(2)}) copy-start(f32[1,64,2,64]{3,1,2,0:T(8,128)S(1)} %get-tuple-element.81) | copy-start | bytes 98308
  145.0 108.5 %copy-start.8 = (f32[1,64,2,64]{3,1,2,0:T(8,128)}, f32[1,64,2,64]{3,1,2,0:T(8,128)S(1)}, u32[]{:S(2)}) copy-start(f32[1,64,2,64]{3,1,2,0:T(8,128)S(1)} %get-tuple-element.71) | copy-start | bytes 98308
  160.9 24.0 %copy-start.2 = (f32[1,256,2,256]{3,1,2,0:T(8,128)S(1)}, f32[1,256,2,256]{3,1,2,0:T(8,128)}, u32[]{:S(2)}) copy-start(f32[1,256,2,256]{3,1,2,0:T(8,128)} %get-tuple-element.66) | copy-start | bytes 1572868
  226.2 27.3 %copy-start.11 = (f32[1,64,2,64]{3,1,2,0:T(8,128)S(1)}, f32[1,64,2,64]{3,1,2,0:T(8,128)}, u32[]{:S(2)}) copy-start(f32[1,64,2,64]{3,1,2,0:T(8,128)} %copy-done.10) | copy-start | bytes 98308
  230.1 24.1 %copy-start.14 = (f32[1,64,2,64]{3,1,2,0:T(8,128)S(1)}, f32[1,64,2,64]{3,1,2,0:T(8,128)}, u32[]{:S(2)}) copy-start(f32[1,64,2,64]{3,1,2,0:T(8,128)} %copy-done.13) | copy-start | bytes 98308
  230.1 24.1 %copy-start.17 = (f32[1,64,2,64]{3,1,2,0:T(8,128)S(1)}, f32[1,64,2,64]{3,1,2,0:T(8,128)}, u32[]{:S(2)}) copy-start(f32[1,64,2,64]{3,1,2,0:T(8,128)} %copy-done.16) | copy-start | bytes 98308
  280.5 16.8 %all-to-all-start.5 = ((f32[2,2,256,128]{3,1,0,2:T(2,128)}), f32[2,2,256,128]{3,1,0,2:T(2,128)}, u32[]{:S(2)}, u32[]{:S(2)}) async-start(f32[2,2,256,128]{3,1,0,2:T(2,128)} %copy.646), calls=%async_computation.5 | async-start | bytes 1048576 | tf_op jit(solution)/shard_map/all_to_all | solution.py:129
  298.6 39.7 %copy-start.6 = (f32[2,2,32,128]{3,1,0,2:T(2,128)}, f32[2,2,32,128]{3,1,0,2:T(2,128)S(1)}, u32[]{:S(2)}) copy-start(f32[2,2,32,128]{3,1,0,2:T(2,128)S(1)} %reduce_sum.159) | copy-start | bytes 196612
  342.2 27.1 %copy-start.9 = (f32[1,64,2,64]{3,1,2,0:T(8,128)S(1)}, f32[1,64,2,64]{3,1,2,0:T(8,128)}, u32[]{:S(2)}) copy-start(f32[1,64,2,64]{3,1,2,0:T(8,128)} %copy-done.8) | copy-start | bytes 98308
  342.2 27.1 %copy-start.12 = (f32[1,64,2,64]{3,1,2,0:T(8,128)S(1)}, f32[1,64,2,64]{3,1,2,0:T(8,128)}, u32[]{:S(2)}) copy-start(f32[1,64,2,64]{3,1,2,0:T(8,128)} %copy-done.10) | copy-start | bytes 98308
  346.1 23.9 %copy-start.15 = (f32[1,64,2,64]{3,1,2,0:T(8,128)S(1)}, f32[1,64,2,64]{3,1,2,0:T(8,128)}, u32[]{:S(2)}) copy-start(f32[1,64,2,64]{3,1,2,0:T(8,128)} %copy-done.13) | copy-start | bytes 98308
  346.1 23.9 %copy-start.18 = (f32[1,64,2,64]{3,1,2,0:T(8,128)S(1)}, f32[1,64,2,64]{3,1,2,0:T(8,128)}, u32[]{:S(2)}) copy-start(f32[1,64,2,64]{3,1,2,0:T(8,128)} %copy-done.16) | copy-start | bytes 98308
  393.3 16.1 %copy-start.7 = (f32[2,2,32,128]{3,1,0,2:T(2,128)S(1)}, f32[2,2,32,128]{3,1,0,2:T(2,128)}, u32[]{:S(2)}) copy-start(f32[2,2,32,128]{3,1,0,2:T(2,128)} %copy-done.6) | copy-start | bytes 196612
  393.3 45.1 %copy-start.20 = (f32[2,2,32,128]{3,0,2,1:T(2,128)S(1)}, f32[2,2,32,128]{3,0,2,1:T(2,128)}, u32[]{:S(2)}) copy-start(f32[2,2,32,128]{3,0,2,1:T(2,128)} %copy-done.19) | copy-start | bytes 196612
  393.3 45.1 %copy-start.22 = (f32[2,2,32,128]{3,0,2,1:T(2,128)S(1)}, f32[2,2,32,128]{3,0,2,1:T(2,128)}, u32[]{:S(2)}) copy-start(f32[2,2,32,128]{3,0,2,1:T(2,128)} %get-tuple-element.31) | copy-start | bytes 196612
  413.6 19.5 %all-to-all-start.10 = ((f32[256,1,4]{2,1,0:T(1,128)}), f32[256,1,4]{2,1,0:T(1,128)S(1)}, u32[]{:S(2)}, u32[]{:S(2)}) async-start(f32[256,1,4]{2,1,0:T(1,128)} %broadcast_in_dim.5), calls=%async_computation.10 | async-start | bytes 262144 | tf_op jit(solution)/shard_map/all_to_all | solution.py:142

commit v5 on v4

--- a/solution.py
+++ b/solution.py
@@ -44,9 +44,8 @@
     return jnp.dot(embed, time_weight, precision=HIGHEST_PRECISION)
 
 
-def conv_layer(inputs, weights):
-    depth, rows, width = (inputs.shape[1], inputs.shape[2], inputs.shape[3])
-    padded = extended(inputs, (("slab", 1), ("coil", 2)), 1)
+def conv_padded(padded, weights):
+    depth, rows, width = (padded.shape[1] - 2, padded.shape[2] - 2, padded.shape[3])
     total = jnp.zeros((weights.shape[3], depth, rows, width), jnp.float32)
     for depth_shift in range(3):
         for row_shift in range(3):
@@ -65,6 +64,34 @@
                 + shifted[2, ..., 2 : width + 2]
             )
     return total
+
+
+def conv_layer(inputs, weights):
+    return conv_padded(extended(inputs, (("slab", 1), ("coil", 2)), 1), weights)
+
+
+def conv_columns(padded, weights):
+    depth, rows, width = (padded.shape[1] - 2, padded.shape[2] - 2, padded.shape[3])
+    wide = jnp.pad(padded, ((0, 0), (0, 0), (0, 0), (1, 1)))
+    windows = [
+        wide[:, a : a + depth, b : b + rows, c : c + width]
+        for a in range(3)
+        for b in range(3)
+        for c in range(3)
+    ]
+    columns = jnp.stack(windows, axis=0).reshape((-1, depth, rows, width))
+    matrix = jnp.transpose(weights, (3, 0, 1, 2, 4)).reshape((weights.shape[3], -1))
+    return jnp.einsum("ok,kzyx->ozyx", matrix, columns, preferred_element_type=jnp.float32)
+
+
+def inside_volume(depth, rows):
+    slab, slabs = lax.axis_index("slab"), lax.axis_size("slab")
+    coil, coils = lax.axis_index("coil"), lax.axis_size("coil")
+    plane = jnp.arange(depth)
+    row = jnp.arange(rows)
+    plane_ok = ~(((plane == 0) & (slab == 0)) | ((plane == depth - 1) & (slab == slabs - 1)))
+    row_ok = ~(((row == 0) & (coil == 0)) | ((row == rows - 1) & (coil == coils - 1)))
+    return plane_ok[:, None, None] & row_ok[None, :, None]
 
 
 def dft_blocks(length, inverse):
@@ -147,10 +174,13 @@
     signal_level = plan_level(step_value)
     prior_level = plan_level(step_value - STRIDE)
     bias = time_bias(step_value, time_weight)
-    hidden = jax.nn.silu(
-        conv_layer(noisy.astype(jnp.bfloat16), w_in) + bias[:, None, None, None]
+    noisy_wide = extended(noisy.astype(jnp.bfloat16), (("slab", 1), ("coil", 2)), 2)
+    hidden_wide = jax.nn.silu(conv_columns(noisy_wide, w_in) + bias[:, None, None, None])
+    hidden_wide = jnp.where(
+        inside_volume(hidden_wide.shape[1], hidden_wide.shape[2]), hidden_wide, 0.0
     ).astype(jnp.bfloat16)
-    mixed = (hidden.astype(jnp.float32) + jax.nn.silu(conv_layer(hidden, w_mid))).astype(
+    hidden = hidden_wide[:, 1:-1, 1:-1, :]
+    mixed = (hidden.astype(jnp.float32) + jax.nn.silu(conv_padded(hidden_wide, w_mid))).astype(
         jnp.bfloat16
     )
     noise_pred = conv_layer(mixed, w_out)

time: 445 us -> 407 us (0.915)
  matrix products: 50.1 us -> 31.6 us
  starting transfers between devices: 67.4 us -> 54 us
  other arithmetic: 40.1 us -> 32.8 us
  local copies, waits for them, and re-layouts: 30.5 us -> 37 us
  waiting for transfers between devices: 49.7 us -> 43.8 us
    dot_general x27 -> x19, matrix products: 25.7 us -> 12.5 us  [the longest x18 11.2 us: conv_padded(): jnp.einsum('aoc,czyx->aozyx', weights[depth_shift, row_shift], window, pr...]
    ppermute x6 -> x4, starting transfers between devices: 25.6 us -> 16.3 us  [extended(): lax.ppermute(tail, axis, [(i, (i + 1) % count) for i in range(ends)])]
    convert_element_type x3 -> x2, other arithmetic: 16.7 us -> 7.87 us  [the longest x1 6.94 us: body(): (hidden.astype(jnp.float32) + jax.nn.silu(conv_padded(hidden_wide, w_mid)...]
    ppermute x6 -> x4, waiting for transfers between devices: 11.6 us -> 7.94 us  [extended(): lax.ppermute(head, axis, [((i + 1) % count, i) for i in range(ends)])]
    ppermute x6 -> x4, starting transfers between devices: 10.4 us -> 7.24 us  [extended(): lax.ppermute(head, axis, [((i + 1) % count, i) for i in range(ends)])]
  transfers between devices with their start and end apart: 15 -> 11, of which waited for: 8 -> 7; matrix products, arithmetic and copies ran while one was open for 5% -> 3% of each run, Pallas kernels for 0% -> 0%
where the time goes in v5:
time: 407 us; the launch traced here: 403 us
  blocking collectives  195 us (48%)
  starting transfers between devices  54 us (13%)
  waiting for transfers between devices  43.8 us (11%)
  local copies, waits for them, and re-layouts  37 us (9%)
  other arithmetic  32.8 us (8%)
  matrix products  31.6 us (8%)
  between operations  8.55 us (2%)
    all_to_all x3, blocking collectives, coil_term(): lax.all_to_all(back.astype(jnp.bfloat16), 'slab', split_axis=2, concat_ax...  60.9 us
    all_to_all x2, blocking collectives, coil_term(): lax.all_to_all(spectrum.astype(jnp.bfloat16), 'slab', split_axis=3, conca...  42.3 us
    all_gather x3, blocking collectives, gather_rows(): return lax.all_gather(value, 'coil', axis=2, tiled=True)  40.4 us
    all_to_all x2, blocking collectives, combine_coils(): lax.all_to_all(partial_value, 'coil', split_axis=2, concat_axis=0, tiled=...  32 us
    all_to_all x1, blocking collectives, global_sums(): lax.all_to_all(spread, axes, split_axis=0, concat_axis=0, tiled=True)  19.2 us
    all_to_all x1, starting transfers between devices, coil_term(): lax.all_to_all(spectrum.astype(jnp.bfloat16), 'slab', split_axis=3, conca...  16.6 us
    ppermute x4, starting transfers between devices, extended(): lax.ppermute(tail, axis, [(i, (i + 1) % count) for i in range(ends)])  16.3 us
    all_to_all x1, waiting for transfers between devices, coil_term(): lax.all_to_all(spectrum.astype(jnp.bfloat16), 'slab', split_axis=3, conca...  13.7 us
  transfers between devices with their start and end apart: 11, of which 7 were waited for; matrix products, arithmetic and copies ran while one was open for 3% of the time, Pallas kernels for 0%

profile of v5, /device:TPU:1, one launch (start us, length us, event | category | flops | bytes accessed | tf_op | source)
XLA Modules:
  0.0 402.6 jit_solution(3429047714752471738)
XLA Ops:
  1.6 3.9 collective-permute-start
  5.5 1.3 collective-permute-start.1
  7.9 1.7 fusion.95
  11.1 2.1 fusion.237
  13.4 4.0 %collective-permute-start.2 = (bf16[2,6,2,128]{3,2,1,0:T(2,128)(2,1)S(1)}, bf16[2,6,2,128]{3,2,1,0:T(2,128)(2,1)S(1)}, u32[]{:S(2)}, u32[]{:S(2)}) collective-permute-start(bf16[2,6,2,128]{3,2,1,0:T(2,128)(2,1)S(1)} %get-tuple-element.62), channel_id=1, source_target_pairs={{0,1},{1,2},{2,3},{3,4},{4,5},{5,6},{6,7},{8,9},{9,10},{10,11},{11... | collective-permute-start | bytes 18440 | tf_op jit(solution)/shard_map/ppermute | solution.py:25
  17.4 2.2 collective-permute-start.3
  19.9 2.5 collective-permute-done.3
  24.8 1.3 fusion.4
  30.0 2.2 convolution_bitcast_fusion.7
  32.2 2.2 convolution_bitcast_fusion.8
  34.4 6.9 %add_convert_fusion = bf16[32,2,32,128]{3,0,2,1:T(8,128)(2,1)S(1)} fusion(f32[3,32,2,32,128]{4,1,3,2,0:T(8,128)S(1)} %convolution_bitcast_fusion, f32[3,32,2,32,128]{4,1,3,2,0:T(8,128)S(1)} %convolution_bitcast_fusion.1, f32[3,32,2,32,128]{4,1,3,2,0:T(8,128)S(1)} %convolution_bitcast_fusion.2, f32[3,32,2,32,128]{4,1,3,2,0:T(8,128)S(1)} %convolution_bitcast_fusion.3, ...), kind=kLoop, calls=%fused_computation.128 | loop fusion | flops 8650752 | bytes 38797312 | tf_op jit(solution)/shard_map/convert_element_type | solution.py:183
  42.2 4.3 %collective-permute-start.4 = (bf16[32,1,32,128]{3,0,2,1:T(8,128)(2,1)}, bf16[32,1,32,128]{3,0,2,1:T(8,128)(2,1)S(1)}, u32[]{:S(2)}, u32[]{:S(2)}) collective-permute-start(bf16[32,1,32,128]{3,0,2,1:T(8,128)(2,1)} %get-tuple-element.54), channel_id=1, source_target_pairs={{0,8},{8,16},{16,24},{24,32},{32,40},{40,48},{48,56},{56,64},{64,7... | collective-permute-start | bytes 786440 | tf_op jit(solution)/shard_map/ppermute | solution.py:25
  51.4 4.1 %collective-permute-done.5 = bf16[32,1,32,128]{3,0,2,1:T(8,128)(2,1)} collective-permute-done((bf16[32,1,32,128]{3,0,2,1:T(8,128)(2,1)}, bf16[32,1,32,128]{3,0,2,1:T(8,128)(2,1)}, u32[]{:S(2)}, u32[]{:S(2)}) %collective-permute-start.5) | collective-permute-done | bytes 262176 | tf_op jit(solution)/shard_map/ppermute | solution.py:27
  56.3 4.1 %collective-permute-start.6 = (bf16[32,4,1,128]{3,0,2,1:T(8,128)(2,1)S(1)}, bf16[32,4,1,128]{3,0,2,1:T(8,128)(2,1)S(1)}, u32[]{:S(2)}, u32[]{:S(2)}) collective-permute-start(bf16[32,4,1,128]{3,0,2,1:T(8,128)(2,1)S(1)} %get-tuple-element.42), channel_id=1, source_target_pairs={{0,1},{1,2},{2,3},{3,4},{4,5},{5,6},{6,7},{8,9},{9,10},{10,11},{11... | collective-permute-start | bytes 98312 | tf_op jit(solution)/shard_map/ppermute | solution.py:25
  60.4 2.4 collective-permute-start.7
  64.3 1.4 collective-permute-done.7
  68.4 1.4 fusion.184
  71.0 13.0 %all_gather.9 = f32[2,2,256,128]{3,0,2,1:T(2,128)S(1)} all-gather(f32[2,2,32,128]{3,0,2,1:T(2,128)S(1)} %get-tuple-element.30), channel_id=1, replica_groups=mesh['slab'=32,'coil'=8] {'coil'}, dimensions={2}, use_global_device_ids=true | all-gather | bytes 589824 | tf_op jit(solution)/shard_map/all_gather | solution.py:162
  86.3 1.8 copy.481
  89.3 2.7 fusion.24
  91.9 2.0 copy.482
  93.9 16.6 %all-to-all-start = ((bf16[2,2,2,256,128]{4,1,2,0,3:T(2,128)(2,1)}), bf16[2,2,2,256,128]{4,1,2,0,3:T(2,128)(2,1)S(1)}, u32[]{:S(2)}, u32[]{:S(2)}) async-start(bf16[2,2,2,256,128]{4,1,2,0,3:T(2,128)(2,1)} %copy.482), calls=%async_computation | async-start | bytes 1048576 | tf_op jit(solution)/shard_map/all_to_all | solution.py:138
  111.5 2.0 convolution_bitcast_fusion.18
  113.5 13.7 %all-to-all-done = bf16[2,2,2,256,128]{4,1,2,0,3:T(2,128)(2,1)S(1)} async-done(((bf16[2,2,2,256,128]{4,1,2,0,3:T(2,128)(2,1)}), bf16[2,2,2,256,128]{4,1,2,0,3:T(2,128)(2,1)S(1)}, u32[]{:S(2)}, u32[]{:S(2)}) %all-to-all-start) | async-done | bytes 524320 | tf_op jit(solution)/shard_map/all_to_all | solution.py:138
  130.8 20.3 %all_to_all.156 = bf16[2,2,64,8,128]{4,1,3,0,2:T(2,128)(2,1)S(1)} all-to-all(bf16[2,2,64,8,128]{4,1,3,0,2:T(2,128)(2,1)S(1)} %copy.486), channel_id=1, replica_groups=mesh['slab'=32,'coil'=8] {'slab'}, dimensions={2} | all-to-all | bytes 1048576 | tf_op jit(solution)/shard_map/all_to_all | solution.py:147
  153.4 2.0 copy.490
  155.5 16.8 %all_to_all.157 = f32[2,2,256,128]{3,1,0,2:T(2,128)} all-to-all(f32[2,2,256,128]{3,1,0,2:T(2,128)} %copy.490), channel_id=1, replica_groups=mesh['slab'=32,'coil'=8] {'coil'}, dimensions={2} | all-to-all | bytes 1048576 | tf_op jit(solution)/shard_map/all_to_all | solution.py:156
  173.5 14.0 %all_gather.10 = f32[2,2,256,128]{3,1,0,2:T(2,128)S(1)} all-gather(f32[2,2,32,128]{3,1,0,2:T(2,128)S(1)} %reduce_sum.155), channel_id=1, replica_groups=mesh['slab'=32,'coil'=8] {'coil'}, dimensions={2}, use_global_device_ids=true | all-gather | bytes 589824 | tf_op jit(solution)/shard_map/all_gather | solution.py:162
  189.6 1.8 copy.492
  192.6 2.7 fusion.23
  195.3 2.0 copy.493
  197.3 21.3 %all_to_all.158 = bf16[2,2,2,256,128]{4,1,2,0,3:T(2,128)(2,1)S(1)} all-to-all(bf16[2,2,2,256,128]{4,1,2,0,3:T(2,128)(2,1)} %copy.493), channel_id=1, replica_groups=mesh['slab'=32,'coil'=8] {'slab'}, dimensions={3} | all-to-all | bytes 1048576 | tf_op jit(solution)/shard_map/all_to_all | solution.py:138
  221.2 20.3 %all_to_all.159 = bf16[2,2,64,8,128]{4,1,3,0,2:T(2,128)(2,1)S(1)} all-to-all(bf16[2,2,64,8,128]{4,1,3,0,2:T(2,128)(2,1)S(1)} %copy.497), channel_id=1, replica_groups=mesh['slab'=32,'coil'=8] {'slab'}, dimensions={2} | all-to-all | bytes 1048576 | tf_op jit(solution)/shard_map/all_to_all | solution.py:147
  243.8 2.0 copy.501
  245.8 7.4 %all-to-all-start.5 = ((f32[2,2,256,128]{3,1,0,2:T(2,128)}), f32[2,2,256,128]{3,1,0,2:T(2,128)}, u32[]{:S(2)}, u32[]{:S(2)}) async-start(f32[2,2,256,128]{3,1,0,2:T(2,128)} %copy.501), calls=%async_computation.5 | async-start | bytes 1048576 | tf_op jit(solution)/shard_map/all_to_all | solution.py:156
  253.9 8.8 %all-to-all-done.5 = f32[2,2,256,128]{3,1,0,2:T(2,128)} async-done(((f32[2,2,256,128]{3,1,0,2:T(2,128)}), f32[2,2,256,128]{3,1,0,2:T(2,128)}, u32[]{:S(2)}, u32[]{:S(2)}) %all-to-all-start.5) | async-done | bytes 524320 | tf_op jit(solution)/shard_map/all_to_all | solution.py:156
  264.7 1.3 pad_maximum_fusion.22
  266.1 19.2 %all_to_all.160 = f32[256,1,2]{2,1,0:T(1,128)S(1)} all-to-all(f32[256,1,2]{2,1,0:T(1,128)S(1)} %broadcast_in_dim.18), channel_id=1, replica_groups=mesh['slab'=32,'coil'=8] {'slab','coil'}, dimensions={0} | all-to-all | bytes 4096 | tf_op jit(solution)/shard_map/all_to_all | solution.py:169
  287.5 13.4 %all_gather.11 = f32[2,2,256,128]{3,0,2,1:T(2,128)S(1)} all-gather(f32[2,2,32,128]{3,0,2,1:T(2,128)S(1)} %multiply_subtract_fusion.3), channel_id=1, replica_groups=mesh['slab'=32,'coil'=8] {'coil'}, dimensions={2}, use_global_device_ids=true | all-gather | bytes 589824 | tf_op jit(solution)/shard_map/all_gather | solution.py:162
  303.2 1.8 copy.509
  306.3 2.7 fusion.22
  308.9 2.0 copy.510
  311.0 21.0 %all_to_all.161 = bf16[2,2,2,256,128]{4,1,2,0,3:T(2,128)(2,1)S(1)} all-to-all(bf16[2,2,2,256,128]{4,1,2,0,3:T(2,128)(2,1)} %copy.510), channel_id=1, replica_groups=mesh['slab'=32,'coil'=8] {'slab'}, dimensions={3} | all-to-all | bytes 1048576 | tf_op jit(solution)/shard_map/all_to_all | solution.py:138
  334.5 20.3 %all_to_all.162 = bf16[2,2,64,8,128]{4,1,3,0,2:T(2,128)(2,1)S(1)} all-to-all(bf16[2,2,64,8,128]{4,1,3,0,2:T(2,128)(2,1)S(1)} %copy.514), channel_id=1, replica_groups=mesh['slab'=32,'coil'=8] {'slab'}, dimensions={2} | all-to-all | bytes 1048576 | tf_op jit(solution)/shard_map/all_to_all | solution.py:147
  356.7 15.2 %all_to_all.163 = f32[2,2,256,128]{3,1,0,2:T(2,128)S(1)} all-to-all(f32[2,2,256,128]{3,1,0,2:T(2,128)S(1)} %copy.518), channel_id=1, replica_groups=mesh['slab'=32,'coil'=8] {'coil'}, dimensions={2} | all-to-all | bytes 1048576 | tf_op jit(solution)/shard_map/all_to_all | solution.py:156
  372.9 2.5 pad_maximum_fusion.23
  376.2 6.5 %all-to-all-start.10 = ((f32[256,1,4]{2,1,0:T(1,128)}), f32[256,1,4]{2,1,0:T(1,128)S(1)}, u32[]{:S(2)}, u32[]{:S(2)}) async-start(f32[256,1,4]{2,1,0:T(1,128)} %broadcast_in_dim.19), calls=%async_computation.10 | async-start | bytes 262144 | tf_op jit(solution)/shard_map/all_to_all | solution.py:169
  382.8 12.8 %all-to-all-done.10 = f32[256,1,4]{2,1,0:T(1,128)S(1)} async-done(((f32[256,1,4]{2,1,0:T(1,128)}), f32[256,1,4]{2,1,0:T(1,128)S(1)}, u32[]{:S(2)}, u32[]{:S(2)}) %all-to-all-start.10) | async-done | bytes 4128 | tf_op jit(solution)/shard_map/all_to_all | solution.py:169
  (193 shorter events, 56.0 us)
Async XLA Ops:
  0.6 110.8 %copy-start = (f32[2,2,64,8,128]{4,3,2,1,0:T(8,128)S(1)}, f32[2,2,64,8,128]{4,3,2,1,0:T(8,128)}, u32[]{:S(2)}) copy-start(f32[2,2,64,8,128]{4,3,2,1,0:T(8,128)} %param.16) | copy-start | bytes 3145732
  0.6 19.0 %copy-start.28 = (f32[32,32]{1,0:T(8,128)S(1)}, f32[32,32]{1,0:T(8,128)}, u32[]{:S(2)}) copy-start(f32[32,32]{1,0:T(8,128)} %param.14) | copy-start | bytes 12292
  0.7 19.2 %copy-start.29 = (bf16[3,3,3,32,2]{3,4,2,1,0:T(2,128)(2,1)S(1)}, bf16[3,3,3,32,2]{3,4,2,1,0:T(2,128)(2,1)}, u32[]{:S(2)}) copy-start(bf16[3,3,3,32,2]{3,4,2,1,0:T(2,128)(2,1)} %param.11) | copy-start | bytes 10372
  1.6 11.7 %collective-permute-start = (bf16[2,2,32,128]{3,2,1,0:T(8,128)(2,1)S(1)}, bf16[2,2,32,128]{3,2,1,0:T(8,128)(2,1)S(1)}, u32[]{:S(2)}, u32[]{:S(2)}) collective-permute-start(bf16[2,2,32,128]{3,2,1,0:T(8,128)(2,1)S(1)} %convert_element_type.175), channel_id=1, source_target_pairs={{0,8},{8,16},{16,24},{24,32},{32,40},{40,48},{48,56},{56,64},{64,7... | collective-permute-start | bytes 98312 | tf_op jit(solution)/shard_map/ppermute | solution.py:25
  5.5 7.8 %collective-permute-start.1 = (bf16[2,2,32,128]{3,2,1,0:T(8,128)(2,1)S(1)}, bf16[2,2,32,128]{3,2,1,0:T(8,128)(2,1)S(1)}, u32[]{:S(2)}, u32[]{:S(2)}) collective-permute-start(bf16[2,2,32,128]{3,2,1,0:T(8,128)(2,1)S(1)} %convert_element_type.175), channel_id=1, source_target_pairs={{8,0},{16,8},{24,16},{32,24},{40,32},{48,40},{56,48},{64,56},{72,6... | collective-permute-start | bytes 98312 | tf_op jit(solution)/shard_map/ppermute | solution.py:27
  13.4 6.5 %collective-permute-start.2 = (bf16[2,6,2,128]{3,2,1,0:T(2,128)(2,1)S(1)}, bf16[2,6,2,128]{3,2,1,0:T(2,128)(2,1)S(1)}, u32[]{:S(2)}, u32[]{:S(2)}) collective-permute-start(bf16[2,6,2,128]{3,2,1,0:T(2,128)(2,1)S(1)} %get-tuple-element.62), channel_id=1, source_target_pairs={{0,1},{1,2},{2,3},{3,4},{4,5},{5,6},{6,7},{8,9},{9,10},{10,11},{11... | collective-permute-start | bytes 18440 | tf_op jit(solution)/shard_map/ppermute | solution.py:25
  17.4 4.9 %collective-permute-start.3 = (bf16[2,6,2,128]{3,2,1,0:T(2,128)(2,1)S(1)}, bf16[2,6,2,128]{3,2,1,0:T(2,128)(2,1)S(1)}, u32[]{:S(2)}, u32[]{:S(2)}) collective-permute-start(bf16[2,6,2,128]{3,2,1,0:T(2,128)(2,1)S(1)} %get-tuple-element.63), channel_id=1, source_target_pairs={{1,0},{2,1},{3,2},{4,3},{5,4},{6,5},{7,6},{9,8},{10,9},{11,10},{12... | collective-permute-start | bytes 18440 | tf_op jit(solution)/shard_map/ppermute | solution.py:27
  24.8 1.4 copy-start.27
  34.4 13.4 %copy-start.11 = (f32[256,1,256]{2,0,1:T(8,128)S(1)}, f32[256,1,256]{2,0,1:T(8,128)}, u32[]{:S(2)}) copy-start(f32[256,1,256]{2,0,1:T(8,128)} %fusion.95) | copy-start | bytes 786436
  42.2 9.3 %collective-permute-start.4 = (bf16[32,1,32,128]{3,0,2,1:T(8,128)(2,1)}, bf16[32,1,32,128]{3,0,2,1:T(8,128)(2,1)S(1)}, u32[]{:S(2)}, u32[]{:S(2)}) collective-permute-start(bf16[32,1,32,128]{3,0,2,1:T(8,128)(2,1)} %get-tuple-element.54), channel_id=1, source_target_pairs={{0,8},{8,16},{16,24},{24,32},{32,40},{40,48},{48,56},{56,64},{64,7... | collective-permute-start | bytes 786440 | tf_op jit(solution)/shard_map/ppermute | solution.py:25
  46.5 9.1 %collective-permute-start.5 = (bf16[32,1,32,128]{3,0,2,1:T(8,128)(2,1)}, bf16[32,1,32,128]{3,0,2,1:T(8,128)(2,1)}, u32[]{:S(2)}, u32[]{:S(2)}) collective-permute-start(bf16[32,1,32,128]{3,0,2,1:T(8,128)(2,1)} %get-tuple-element.55), channel_id=1, source_target_pairs={{8,0},{16,8},{24,16},{32,24},{40,32},{48,40},{56,48},{64,56},{72,6... | collective-permute-start | bytes 786440 | tf_op jit(solution)/shard_map/ppermute | solution.py:27
  56.3 8.0 %collective-permute-start.6 = (bf16[32,4,1,128]{3,0,2,1:T(8,128)(2,1)S(1)}, bf16[32,4,1,128]{3,0,2,1:T(8,128)(2,1)S(1)}, u32[]{:S(2)}, u32[]{:S(2)}) collective-permute-start(bf16[32,4,1,128]{3,0,2,1:T(8,128)(2,1)S(1)} %get-tuple-element.42), channel_id=1, source_target_pairs={{0,1},{1,2},{2,3},{3,4},{4,5},{5,6},{6,7},{8,9},{9,10},{10,11},{11... | collective-permute-start | bytes 98312 | tf_op jit(solution)/shard_map/ppermute | solution.py:25
  60.4 5.2 %collective-permute-start.7 = (bf16[32,4,1,128]{3,0,2,1:T(8,128)(2,1)S(1)}, bf16[32,4,1,128]{3,0,2,1:T(8,128)(2,1)S(1)}, u32[]{:S(2)}, u32[]{:S(2)}) collective-permute-start(bf16[32,4,1,128]{3,0,2,1:T(8,128)(2,1)S(1)} %get-tuple-element.43), channel_id=1, source_target_pairs={{1,0},{2,1},{3,2},{4,3},{5,4},{6,5},{7,6},{9,8},{10,9},{11,10},{12... | collective-permute-start | bytes 98312 | tf_op jit(solution)/shard_map/ppermute | solution.py:27
  67.7 2.2 copy-start.25
  71.0 14.2 %copy-start.23 = (f32[2,2,32,128]{3,0,2,1:T(2,128)}, f32[2,2,32,128]{3,0,2,1:T(2,128)S(1)}, u32[]{:S(2)}) copy-start(f32[2,2,32,128]{3,0,2,1:T(2,128)S(1)} %get-tuple-element.30) | copy-start | bytes 196612
  84.0 5.2 %copy-start.2 = (f32[1,256,2,256]{3,1,2,0:T(8,128)S(1)}, f32[1,256,2,256]{3,1,2,0:T(8,128)}, u32[]{:S(2)}) copy-start(f32[1,256,2,256]{3,1,2,0:T(8,128)} %get-tuple-element.48) | copy-start | bytes 1572868
  88.1 1.2 copy-start.5
  89.2 21.3 %copy-start.30 = (s32[64,8]{0,1:T(8,128)S(1)}, s32[64,8]{0,1:T(8,128)}, u32[]{:S(2)}) copy-start(s32[64,8]{0,1:T(8,128)} %param.17) | copy-start | bytes 6148
  93.9 33.3 %all-to-all-start = ((bf16[2,2,2,256,128]{4,1,2,0,3:T(2,128)(2,1)}), bf16[2,2,2,256,128]{4,1,2,0,3:T(2,128)(2,1)S(1)}, u32[]{:S(2)}, u32[]{:S(2)}) async-start(bf16[2,2,2,256,128]{4,1,2,0,3:T(2,128)(2,1)} %copy.482), calls=%async_computation | async-start | bytes 1048576 | tf_op jit(solution)/shard_map/all_to_all | solution.py:138
  111.4 16.0 %copy-start.14 = (f32[1,64,2,64]{3,1,2,0:T(8,128)}, f32[1,64,2,64]{3,1,2,0:T(8,128)S(1)}, u32[]{:S(2)}) copy-start(f32[1,64,2,64]{3,1,2,0:T(8,128)S(1)} %get-tuple-element.70) | copy-start | bytes 98308
  111.4 17.7 %copy-start.17 = (f32[1,64,2,64]{3,1,2,0:T(8,128)}, f32[1,64,2,64]{3,1,2,0:T(8,128)S(1)}, u32[]{:S(2)}) copy-start(f32[1,64,2,64]{3,1,2,0:T(8,128)S(1)} %get-tuple-element.64) | copy-start | bytes 98308
  111.4 17.7 %copy-start.20 = (f32[1,64,2,64]{3,1,2,0:T(8,128)}, f32[1,64,2,64]{3,1,2,0:T(8,128)S(1)}, u32[]{:S(2)}) copy-start(f32[1,64,2,64]{3,1,2,0:T(8,128)S(1)} %get-tuple-element.71) | copy-start | bytes 98308
  111.4 107.4 %copy-start.12 = (f32[1,64,2,64]{3,1,2,0:T(8,128)}, f32[1,64,2,64]{3,1,2,0:T(8,128)S(1)}, u32[]{:S(2)}) copy-start(f32[1,64,2,64]{3,1,2,0:T(8,128)S(1)} %get-tuple-element.65) | copy-start | bytes 98308
  127.2 1.2 copy-start.8
  129.1 22.1 %copy-start.1 = (f32[1,256,2,256]{3,1,2,0:T(8,128)S(1)}, f32[1,256,2,256]{3,1,2,0:T(8,128)}, u32[]{:S(2)}) copy-start(f32[1,256,2,256]{3,1,2,0:T(8,128)} %get-tuple-element.56) | copy-start | bytes 1572868
  191.4 1.2 copy-start.3
  191.4 1.3 copy-start.6
  195.3 23.5 %copy-start.15 = (f32[1,64,2,64]{3,1,2,0:T(8,128)S(1)}, f32[1,64,2,64]{3,1,2,0:T(8,128)}, u32[]{:S(2)}) copy-start(f32[1,64,2,64]{3,1,2,0:T(8,128)} %copy-done.14) | copy-start | bytes 98308
  197.3 22.1 %copy-start.18 = (f32[1,64,2,64]{3,1,2,0:T(8,128)S(1)}, f32[1,64,2,64]{3,1,2,0:T(8,128)}, u32[]{:S(2)}) copy-start(f32[1,64,2,64]{3,1,2,0:T(8,128)} %copy-done.17) | copy-start | bytes 98308
  197.3 22.1 %copy-start.21 = (f32[1,64,2,64]{3,1,2,0:T(8,128)S(1)}, f32[1,64,2,64]{3,1,2,0:T(8,128)}, u32[]{:S(2)}) copy-start(f32[1,64,2,64]{3,1,2,0:T(8,128)} %copy-done.20) | copy-start | bytes 98308
  245.8 16.9 %all-to-all-start.5 = ((f32[2,2,256,128]{3,1,0,2:T(2,128)}), f32[2,2,256,128]{3,1,0,2:T(2,128)}, u32[]{:S(2)}, u32[]{:S(2)}) async-start(f32[2,2,256,128]{3,1,0,2:T(2,128)} %copy.501), calls=%async_computation.5 | async-start | bytes 1048576 | tf_op jit(solution)/shard_map/all_to_all | solution.py:156
  263.9 38.2 %copy-start.9 = (f32[2,2,32,128]{3,1,0,2:T(2,128)}, f32[2,2,32,128]{3,1,0,2:T(2,128)S(1)}, u32[]{:S(2)}) copy-start(f32[2,2,32,128]{3,1,0,2:T(2,128)S(1)} %reduce_sum.159) | copy-start | bytes 196612
  305.0 1.2 copy-start.4
  305.0 1.3 copy-start.7
  308.9 23.2 %copy-start.13 = (f32[1,64,2,64]{3,1,2,0:T(8,128)S(1)}, f32[1,64,2,64]{3,1,2,0:T(8,128)}, u32[]{:S(2)}) copy-start(f32[1,64,2,64]{3,1,2,0:T(8,128)} %copy-done.12) | copy-start | bytes 98308
  308.9 23.2 %copy-start.16 = (f32[1,64,2,64]{3,1,2,0:T(8,128)S(1)}, f32[1,64,2,64]{3,1,2,0:T(8,128)}, u32[]{:S(2)}) copy-start(f32[1,64,2,64]{3,1,2,0:T(8,128)} %copy-done.14) | copy-start | bytes 98308
  311.0 21.8 %copy-start.19 = (f32[1,64,2,64]{3,1,2,0:T(8,128)S(1)}, f32[1,64,2,64]{3,1,2,0:T(8,128)}, u32[]{:S(2)}) copy-start(f32[1,64,2,64]{3,1,2,0:T(8,128)} %copy-done.17) | copy-start | bytes 98308
  311.0 21.8 %copy-start.22 = (f32[1,64,2,64]{3,1,2,0:T(8,128)S(1)}, f32[1,64,2,64]{3,1,2,0:T(8,128)}, u32[]{:S(2)}) copy-start(f32[1,64,2,64]{3,1,2,0:T(8,128)} %copy-done.20) | copy-start | bytes 98308
  356.3 15.8 %copy-start.10 = (f32[2,2,32,128]{3,1,0,2:T(2,128)S(1)}, f32[2,2,32,128]{3,1,0,2:T(2,128)}, u32[]{:S(2)}) copy-start(f32[2,2,32,128]{3,1,0,2:T(2,128)} %copy-done.9) | copy-start | bytes 196612
  356.3 44.6 %copy-start.24 = (f32[2,2,32,128]{3,0,2,1:T(2,128)S(1)}, f32[2,2,32,128]{3,0,2,1:T(2,128)}, u32[]{:S(2)}) copy-start(f32[2,2,32,128]{3,0,2,1:T(2,128)} %copy-done.23) | copy-start | bytes 196612
  356.4 44.6 %copy-start.26 = (f32[2,2,32,128]{3,0,2,1:T(2,128)S(1)}, f32[2,2,32,128]{3,0,2,1:T(2,128)}, u32[]{:S(2)}) copy-start(f32[2,2,32,128]{3,0,2,1:T(2,128)} %get-tuple-element.31) | copy-start | bytes 196612
  376.2 19.5 %all-to-all-start.10 = ((f32[256,1,4]{2,1,0:T(1,128)}), f32[256,1,4]{2,1,0:T(1,128)S(1)}, u32[]{:S(2)}, u32[]{:S(2)}) async-start(f32[256,1,4]{2,1,0:T(1,128)} %broadcast_in_dim.19), calls=%async_computation.10 | async-start | bytes 262144 | tf_op jit(solution)/shard_map/all_to_all | solution.py:169

commit v6 on v5

--- a/solution.py
+++ b/solution.py
@@ -144,8 +144,9 @@
     else:
         kspace = weight * kspace
     back = along_depth(kspace, inverse_z)
+    link_type = jnp.float32 if with_data else jnp.bfloat16
     slabs = lax.all_to_all(
-        back.astype(jnp.bfloat16), "slab", split_axis=2, concat_axis=3, tiled=True
+        back.astype(link_type), "slab", split_axis=2, concat_axis=3, tiled=True
     ).astype(jnp.float32)
     images = along_rows(slabs, inverse_y)
     return times_conj(sens, images)

time: 407 us -> 420 us (1.032)
  blocking collectives: 195 us -> 206 us
    all_to_all x3, blocking collectives: 60.9 us -> 71.4 us  [coil_term(): lax.all_to_all(back.astype(link_type), 'slab', split_axis=2, concat_axis=...]
where the time goes in v6:
time: 420 us; the launch traced here: 415 us
  blocking collectives  206 us (49%)
  starting transfers between devices  54.1 us (13%)
  waiting for transfers between devices  43.8 us (10%)
  local copies, waits for them, and re-layouts  36.6 us (9%)
  matrix products  33.9 us (8%)
  other arithmetic  32.6 us (8%)
  between operations  8.84 us (2%)
    all_to_all x3, blocking collectives, coil_term(): lax.all_to_all(back.astype(link_type), 'slab', split_axis=2, concat_axis=...  71.4 us
    all_to_all x2, blocking collectives, coil_term(): lax.all_to_all(spectrum.astype(jnp.bfloat16), 'slab', split_axis=3, conca...  42.3 us
    all_gather x3, blocking collectives, gather_rows(): return lax.all_gather(value, 'coil', axis=2, tiled=True)  40.8 us
    all_to_all x2, blocking collectives, combine_coils(): lax.all_to_all(partial_value, 'coil', split_axis=2, concat_axis=0, tiled=...  31.8 us
    all_to_all x1, blocking collectives, global_sums(): lax.all_to_all(spread, axes, split_axis=0, concat_axis=0, tiled=True)  19.2 us
    all_to_all x1, starting transfers between devices, coil_term(): lax.all_to_all(spectrum.astype(jnp.bfloat16), 'slab', split_axis=3, conca...  16.7 us
    ppermute x4, starting transfers between devices, extended(): lax.ppermute(tail, axis, [(i, (i + 1) % count) for i in range(ends)])  16.3 us
    dot_general x6, matrix products, along_rows(): jnp.einsum('pkqn,cqzny->cpzky', blocks, data, precision=HIGHEST_PRECISION)  13.9 us
  transfers between devices with their start and end apart: 11, of which 7 were waited for; matrix products, arithmetic and copies ran while one was open for 3% of the time, Pallas kernels for 0%

profile of v6, /device:TPU:1, one launch (start us, length us, event | category | flops | bytes accessed | tf_op | source)
XLA Modules:
  0.0 415.3 jit_solution(1375958821611919236)
XLA Ops:
  1.6 3.9 collective-permute-start
  5.5 1.3 collective-permute-start.1
  7.9 1.7 fusion.93
  11.1 2.1 fusion.235
  13.4 4.0 collective-permute-start.2
  17.4 2.2 collective-permute-start.3
  19.9 2.5 collective-permute-done.3
  24.8 1.3 fusion.4
  30.0 2.2 convolution_bitcast_fusion.7
  32.2 2.2 convolution_bitcast_fusion.8
  34.4 6.9 %add_convert_fusion = bf16[32,2,32,128]{3,0,2,1:T(8,128)(2,1)S(1)} fusion(f32[3,32,2,32,128]{4,1,3,2,0:T(8,128)S(1)} %convolution_bitcast_fusion, f32[3,32,2,32,128]{4,1,3,2,0:T(8,128)S(1)} %convolution_bitcast_fusion.1, f32[3,32,2,32,128]{4,1,3,2,0:T(8,128)S(1)} %convolution_bitcast_fusion.2, f32[3,32,2,32,128]{4,1,3,2,0:T(8,128)S(1)} %convolution_bitcast_fusion.3, ...), kind=kLoop, calls=%fused_computation.128 | loop fusion | flops 8650752 | bytes 38797312 | tf_op jit(solution)/shard_map/convert_element_type | solution.py:184
  42.2 4.3 %collective-permute-start.4 = (bf16[32,1,32,128]{3,0,2,1:T(8,128)(2,1)}, bf16[32,1,32,128]{3,0,2,1:T(8,128)(2,1)S(1)}, u32[]{:S(2)}, u32[]{:S(2)}) collective-permute-start(bf16[32,1,32,128]{3,0,2,1:T(8,128)(2,1)} %get-tuple-element.54), channel_id=1, source_target_pairs={{0,8},{8,16},{16,24},{24,32},{32,40},{40,48},{48,56},{56,64},{64,7... | collective-permute-start | bytes 786440 | tf_op jit(solution)/shard_map/ppermute | solution.py:25
  51.4 4.1 collective-permute-done.5
  56.3 4.1 collective-permute-start.6
  60.4 2.4 collective-permute-start.7
  64.3 1.4 collective-permute-done.7
  68.4 1.4 fusion.182
  71.0 12.9 %all_gather.9 = f32[2,2,256,128]{3,0,2,1:T(2,128)S(1)} all-gather(f32[2,2,32,128]{3,0,2,1:T(2,128)S(1)} %get-tuple-element.30), channel_id=1, replica_groups=mesh['slab'=32,'coil'=8] {'coil'}, dimensions={2}, use_global_device_ids=true | all-gather | bytes 589824 | tf_op jit(solution)/shard_map/all_gather | solution.py:163
  86.3 1.8 copy.481
  89.2 2.7 fusion.23
  91.8 2.0 copy.482
  93.9 16.7 %all-to-all-start = ((bf16[2,2,2,256,128]{4,1,2,0,3:T(2,128)(2,1)}), bf16[2,2,2,256,128]{4,1,2,0,3:T(2,128)(2,1)}, u32[]{:S(2)}, u32[]{:S(2)}) async-start(bf16[2,2,2,256,128]{4,1,2,0,3:T(2,128)(2,1)} %copy.482), calls=%async_computation | async-start | bytes 1048576 | tf_op jit(solution)/shard_map/all_to_all | solution.py:138
  111.5 2.0 convolution_bitcast_fusion.19
  113.6 13.6 %all-to-all-done = bf16[2,2,2,256,128]{4,1,2,0,3:T(2,128)(2,1)} async-done(((bf16[2,2,2,256,128]{4,1,2,0,3:T(2,128)(2,1)}), bf16[2,2,2,256,128]{4,1,2,0,3:T(2,128)(2,1)}, u32[]{:S(2)}, u32[]{:S(2)}) %all-to-all-start) | async-done | bytes 524320 | tf_op jit(solution)/shard_map/all_to_all | solution.py:138
  131.2 30.8 %all_to_all.156 = f32[2,2,64,8,128]{4,1,3,0,2:T(2,128)S(1)} all-to-all(f32[2,2,64,8,128]{4,1,3,0,2:T(2,128)S(1)} %copy.486), channel_id=1, replica_groups=mesh['slab'=32,'coil'=8] {'slab'}, dimensions={2} | all-to-all | bytes 2097152 | tf_op jit(solution)/shard_map/all_to_all | solution.py:148
  162.1 3.5 convolution_bitcast_fusion.15
  166.6 2.0 copy.490
  168.7 16.6 %all_to_all.157 = f32[2,2,256,128]{3,1,0,2:T(2,128)} all-to-all(f32[2,2,256,128]{3,1,0,2:T(2,128)} %copy.490), channel_id=1, replica_groups=mesh['slab'=32,'coil'=8] {'coil'}, dimensions={2} | all-to-all | bytes 1048576 | tf_op jit(solution)/shard_map/all_to_all | solution.py:157
  186.6 14.2 %all_gather.10 = f32[2,2,256,128]{3,1,0,2:T(2,128)S(1)} all-gather(f32[2,2,32,128]{3,1,0,2:T(2,128)S(1)} %reduce_sum.155), channel_id=1, replica_groups=mesh['slab'=32,'coil'=8] {'coil'}, dimensions={2}, use_global_device_ids=true | all-gather | bytes 589824 | tf_op jit(solution)/shard_map/all_gather | solution.py:163
  202.8 1.8 copy.492
  205.7 2.7 fusion.22
  208.4 2.0 copy.493
  210.4 22.1 %all_to_all.158 = bf16[2,2,2,256,128]{4,1,2,0,3:T(2,128)(2,1)S(1)} all-to-all(bf16[2,2,2,256,128]{4,1,2,0,3:T(2,128)(2,1)} %copy.493), channel_id=1, replica_groups=mesh['slab'=32,'coil'=8] {'slab'}, dimensions={3} | all-to-all | bytes 1048576 | tf_op jit(solution)/shard_map/all_to_all | solution.py:138
  235.1 20.3 %all_to_all.159 = bf16[2,2,64,8,128]{4,1,3,0,2:T(2,128)(2,1)S(1)} all-to-all(bf16[2,2,64,8,128]{4,1,3,0,2:T(2,128)(2,1)S(1)} %copy.497), channel_id=1, replica_groups=mesh['slab'=32,'coil'=8] {'slab'}, dimensions={2} | all-to-all | bytes 1048576 | tf_op jit(solution)/shard_map/all_to_all | solution.py:148
  257.7 2.0 copy.501
  259.8 7.4 %all-to-all-start.5 = ((f32[2,2,256,128]{3,1,0,2:T(2,128)}), f32[2,2,256,128]{3,1,0,2:T(2,128)}, u32[]{:S(2)}, u32[]{:S(2)}) async-start(f32[2,2,256,128]{3,1,0,2:T(2,128)} %copy.501), calls=%async_computation.5 | async-start | bytes 1048576 | tf_op jit(solution)/shard_map/all_to_all | solution.py:157
  267.9 8.8 %all-to-all-done.5 = f32[2,2,256,128]{3,1,0,2:T(2,128)} async-done(((f32[2,2,256,128]{3,1,0,2:T(2,128)}), f32[2,2,256,128]{3,1,0,2:T(2,128)}, u32[]{:S(2)}, u32[]{:S(2)}) %all-to-all-start.5) | async-done | bytes 524320 | tf_op jit(solution)/shard_map/all_to_all | solution.py:157
  279.9 19.2 %all_to_all.160 = f32[256,1,2]{2,1,0:T(1,128)S(1)} all-to-all(f32[256,1,2]{2,1,0:T(1,128)S(1)} %broadcast_in_dim.18), channel_id=1, replica_groups=mesh['slab'=32,'coil'=8] {'slab','coil'}, dimensions={0} | all-to-all | bytes 4096 | tf_op jit(solution)/shard_map/all_to_all | solution.py:170
  301.3 13.7 %all_gather.11 = f32[2,2,256,128]{3,0,2,1:T(2,128)S(1)} all-gather(f32[2,2,32,128]{3,0,2,1:T(2,128)S(1)} %multiply_subtract_fusion.3), channel_id=1, replica_groups=mesh['slab'=32,'coil'=8] {'coil'}, dimensions={2}, use_global_device_ids=true | all-gather | bytes 589824 | tf_op jit(solution)/shard_map/all_gather | solution.py:163
  317.3 1.8 copy.509
  320.1 2.7 fusion.21
  322.8 1.4 copy.510
  324.2 20.2 %all_to_all.161 = bf16[2,2,2,256,128]{4,1,2,0,3:T(2,128)(2,1)S(1)} all-to-all(bf16[2,2,2,256,128]{4,1,2,0,3:T(2,128)(2,1)S(1)} %copy.510), channel_id=1, replica_groups=mesh['slab'=32,'coil'=8] {'slab'}, dimensions={3} | all-to-all | bytes 1048576 | tf_op jit(solution)/shard_map/all_to_all | solution.py:138
  346.9 20.3 %all_to_all.162 = bf16[2,2,64,8,128]{4,1,3,0,2:T(2,128)(2,1)S(1)} all-to-all(bf16[2,2,64,8,128]{4,1,3,0,2:T(2,128)(2,1)S(1)} %copy.514), channel_id=1, replica_groups=mesh['slab'=32,'coil'=8] {'slab'}, dimensions={2} | all-to-all | bytes 1048576 | tf_op jit(solution)/shard_map/all_to_all | solution.py:148
  369.1 15.2 %all_to_all.163 = f32[2,2,256,128]{3,1,0,2:T(2,128)S(1)} all-to-all(f32[2,2,256,128]{3,1,0,2:T(2,128)S(1)} %copy.518), channel_id=1, replica_groups=mesh['slab'=32,'coil'=8] {'coil'}, dimensions={2} | all-to-all | bytes 1048576 | tf_op jit(solution)/shard_map/all_to_all | solution.py:157
  385.3 2.7 pad_maximum_fusion.23
  388.7 6.4 %all-to-all-start.10 = ((f32[256,1,4]{2,1,0:T(1,128)}), f32[256,1,4]{2,1,0:T(1,128)S(1)}, u32[]{:S(2)}, u32[]{:S(2)}) async-start(f32[256,1,4]{2,1,0:T(1,128)} %broadcast_in_dim.19), calls=%async_computation.10 | async-start | bytes 262144 | tf_op jit(solution)/shard_map/all_to_all | solution.py:170
  395.3 12.8 %all-to-all-done.10 = f32[256,1,4]{2,1,0:T(1,128)S(1)} async-done(((f32[256,1,4]{2,1,0:T(1,128)}), f32[256,1,4]{2,1,0:T(1,128)S(1)}, u32[]{:S(2)}, u32[]{:S(2)}) %all-to-all-start.10) | async-done | bytes 4128 | tf_op jit(solution)/shard_map/all_to_all | solution.py:170
  (193 shorter events, 56.1 us)
Async XLA Ops:
  0.6 110.9 %copy-start = (f32[2,2,64,8,128]{4,3,2,1,0:T(8,128)S(1)}, f32[2,2,64,8,128]{4,3,2,1,0:T(8,128)}, u32[]{:S(2)}) copy-start(f32[2,2,64,8,128]{4,3,2,1,0:T(8,128)} %param.16) | copy-start | bytes 3145732
  0.6 19.0 %copy-start.28 = (f32[32,32]{1,0:T(8,128)S(1)}, f32[32,32]{1,0:T(8,128)}, u32[]{:S(2)}) copy-start(f32[32,32]{1,0:T(8,128)} %param.14) | copy-start | bytes 12292
  0.7 19.2 %copy-start.29 = (bf16[3,3,3,32,2]{3,4,2,1,0:T(2,128)(2,1)S(1)}, bf16[3,3,3,32,2]{3,4,2,1,0:T(2,128)(2,1)}, u32[]{:S(2)}) copy-start(bf16[3,3,3,32,2]{3,4,2,1,0:T(2,128)(2,1)} %param.11) | copy-start | bytes 10372
  1.6 11.7 %collective-permute-start = (bf16[2,2,32,128]{3,2,1,0:T(8,128)(2,1)S(1)}, bf16[2,2,32,128]{3,2,1,0:T(8,128)(2,1)S(1)}, u32[]{:S(2)}, u32[]{:S(2)}) collective-permute-start(bf16[2,2,32,128]{3,2,1,0:T(8,128)(2,1)S(1)} %convert_element_type.168), channel_id=1, source_target_pairs={{0,8},{8,16},{16,24},{24,32},{32,40},{40,48},{48,56},{56,64},{64,7... | collective-permute-start | bytes 98312 | tf_op jit(solution)/shard_map/ppermute | solution.py:25
  5.5 7.8 %collective-permute-start.1 = (bf16[2,2,32,128]{3,2,1,0:T(8,128)(2,1)S(1)}, bf16[2,2,32,128]{3,2,1,0:T(8,128)(2,1)S(1)}, u32[]{:S(2)}, u32[]{:S(2)}) collective-permute-start(bf16[2,2,32,128]{3,2,1,0:T(8,128)(2,1)S(1)} %convert_element_type.168), channel_id=1, source_target_pairs={{8,0},{16,8},{24,16},{32,24},{40,32},{48,40},{56,48},{64,56},{72,6... | collective-permute-start | bytes 98312 | tf_op jit(solution)/shard_map/ppermute | solution.py:27
  13.4 6.5 %collective-permute-start.2 = (bf16[2,6,2,128]{3,2,1,0:T(2,128)(2,1)S(1)}, bf16[2,6,2,128]{3,2,1,0:T(2,128)(2,1)S(1)}, u32[]{:S(2)}, u32[]{:S(2)}) collective-permute-start(bf16[2,6,2,128]{3,2,1,0:T(2,128)(2,1)S(1)} %get-tuple-element.62), channel_id=1, source_target_pairs={{0,1},{1,2},{2,3},{3,4},{4,5},{5,6},{6,7},{8,9},{9,10},{10,11},{11... | collective-permute-start | bytes 18440 | tf_op jit(solution)/shard_map/ppermute | solution.py:25
  17.4 4.9 %collective-permute-start.3 = (bf16[2,6,2,128]{3,2,1,0:T(2,128)(2,1)S(1)}, bf16[2,6,2,128]{3,2,1,0:T(2,128)(2,1)S(1)}, u32[]{:S(2)}, u32[]{:S(2)}) collective-permute-start(bf16[2,6,2,128]{3,2,1,0:T(2,128)(2,1)S(1)} %get-tuple-element.63), channel_id=1, source_target_pairs={{1,0},{2,1},{3,2},{4,3},{5,4},{6,5},{7,6},{9,8},{10,9},{11,10},{12... | collective-permute-start | bytes 18440 | tf_op jit(solution)/shard_map/ppermute | solution.py:27
  24.8 1.4 copy-start.27
  34.4 13.4 %copy-start.11 = (f32[256,1,256]{2,0,1:T(8,128)S(1)}, f32[256,1,256]{2,0,1:T(8,128)}, u32[]{:S(2)}) copy-start(f32[256,1,256]{2,0,1:T(8,128)} %fusion.93) | copy-start | bytes 786436
  42.2 9.3 %collective-permute-start.4 = (bf16[32,1,32,128]{3,0,2,1:T(8,128)(2,1)}, bf16[32,1,32,128]{3,0,2,1:T(8,128)(2,1)S(1)}, u32[]{:S(2)}, u32[]{:S(2)}) collective-permute-start(bf16[32,1,32,128]{3,0,2,1:T(8,128)(2,1)} %get-tuple-element.54), channel_id=1, source_target_pairs={{0,8},{8,16},{16,24},{24,32},{32,40},{40,48},{48,56},{56,64},{64,7... | collective-permute-start | bytes 786440 | tf_op jit(solution)/shard_map/ppermute | solution.py:25
  46.4 9.1 %collective-permute-start.5 = (bf16[32,1,32,128]{3,0,2,1:T(8,128)(2,1)}, bf16[32,1,32,128]{3,0,2,1:T(8,128)(2,1)}, u32[]{:S(2)}, u32[]{:S(2)}) collective-permute-start(bf16[32,1,32,128]{3,0,2,1:T(8,128)(2,1)} %get-tuple-element.55), channel_id=1, source_target_pairs={{8,0},{16,8},{24,16},{32,24},{40,32},{48,40},{56,48},{64,56},{72,6... | collective-permute-start | bytes 786440 | tf_op jit(solution)/shard_map/ppermute | solution.py:27
  56.3 8.0 %collective-permute-start.6 = (bf16[32,4,1,128]{3,0,2,1:T(8,128)(2,1)S(1)}, bf16[32,4,1,128]{3,0,2,1:T(8,128)(2,1)S(1)}, u32[]{:S(2)}, u32[]{:S(2)}) collective-permute-start(bf16[32,4,1,128]{3,0,2,1:T(8,128)(2,1)S(1)} %get-tuple-element.42), channel_id=1, source_target_pairs={{0,1},{1,2},{2,3},{3,4},{4,5},{5,6},{6,7},{8,9},{9,10},{10,11},{11... | collective-permute-start | bytes 98312 | tf_op jit(solution)/shard_map/ppermute | solution.py:25
  60.4 5.2 %collective-permute-start.7 = (bf16[32,4,1,128]{3,0,2,1:T(8,128)(2,1)S(1)}, bf16[32,4,1,128]{3,0,2,1:T(8,128)(2,1)S(1)}, u32[]{:S(2)}, u32[]{:S(2)}) collective-permute-start(bf16[32,4,1,128]{3,0,2,1:T(8,128)(2,1)S(1)} %get-tuple-element.43), channel_id=1, source_target_pairs={{1,0},{2,1},{3,2},{4,3},{5,4},{6,5},{7,6},{9,8},{10,9},{11,10},{12... | collective-permute-start | bytes 98312 | tf_op jit(solution)/shard_map/ppermute | solution.py:27
  67.7 2.2 copy-start.25
  71.0 14.2 %copy-start.23 = (f32[2,2,32,128]{3,0,2,1:T(2,128)}, f32[2,2,32,128]{3,0,2,1:T(2,128)S(1)}, u32[]{:S(2)}) copy-start(f32[2,2,32,128]{3,0,2,1:T(2,128)S(1)} %get-tuple-element.30) | copy-start | bytes 196612
  84.0 5.2 %copy-start.1 = (f32[1,256,2,256]{3,1,2,0:T(8,128)S(1)}, f32[1,256,2,256]{3,1,2,0:T(8,128)}, u32[]{:S(2)}) copy-start(f32[1,256,2,256]{3,1,2,0:T(8,128)} %get-tuple-element.56) | copy-start | bytes 1572868
  89.2 21.4 %copy-start.30 = (s32[64,8]{0,1:T(8,128)S(1)}, s32[64,8]{0,1:T(8,128)}, u32[]{:S(2)}) copy-start(s32[64,8]{0,1:T(8,128)} %param.17) | copy-start | bytes 6148
  93.9 33.4 %all-to-all-start = ((bf16[2,2,2,256,128]{4,1,2,0,3:T(2,128)(2,1)}), bf16[2,2,2,256,128]{4,1,2,0,3:T(2,128)(2,1)}, u32[]{:S(2)}, u32[]{:S(2)}) async-start(bf16[2,2,2,256,128]{4,1,2,0,3:T(2,128)(2,1)} %copy.482), calls=%async_computation | async-start | bytes 1048576 | tf_op jit(solution)/shard_map/all_to_all | solution.py:138
  111.5 17.1 %copy-start.17 = (f32[1,64,2,64]{3,1,2,0:T(8,128)}, f32[1,64,2,64]{3,1,2,0:T(8,128)S(1)}, u32[]{:S(2)}) copy-start(f32[1,64,2,64]{3,1,2,0:T(8,128)S(1)} %get-tuple-element.65) | copy-start | bytes 98308
  111.5 17.1 %copy-start.20 = (f32[1,64,2,64]{3,1,2,0:T(8,128)}, f32[1,64,2,64]{3,1,2,0:T(8,128)S(1)}, u32[]{:S(2)}) copy-start(f32[1,64,2,64]{3,1,2,0:T(8,128)S(1)} %get-tuple-element.70) | copy-start | bytes 98308
  111.5 17.8 %copy-start.14 = (f32[1,64,2,64]{3,1,2,0:T(8,128)}, f32[1,64,2,64]{3,1,2,0:T(8,128)S(1)}, u32[]{:S(2)}) copy-start(f32[1,64,2,64]{3,1,2,0:T(8,128)S(1)} %get-tuple-element.71) | copy-start | bytes 98308
  111.5 121.9 %copy-start.12 = (f32[1,64,2,64]{3,1,2,0:T(8,128)}, f32[1,64,2,64]{3,1,2,0:T(8,128)S(1)}, u32[]{:S(2)}) copy-start(f32[1,64,2,64]{3,1,2,0:T(8,128)S(1)} %get-tuple-element.64) | copy-start | bytes 98308
  127.2 1.4 copy-start.8
  131.2 30.9 %copy-start.2 = (f32[1,256,2,256]{3,1,2,0:T(8,128)S(1)}, f32[1,256,2,256]{3,1,2,0:T(8,128)}, u32[]{:S(2)}) copy-start(f32[1,256,2,256]{3,1,2,0:T(8,128)} %get-tuple-element.48) | copy-start | bytes 1572868
  131.2 30.9 %copy-start.5 = (f32[1,256,2,256]{3,1,2,0:T(8,128)S(1)}, f32[1,256,2,256]{3,1,2,0:T(8,128)}, u32[]{:S(2)}) copy-start(f32[1,256,2,256]{3,1,2,0:T(8,128)} %get-tuple-element.57) | copy-start | bytes 1572868
  208.4 24.4 %copy-start.18 = (f32[1,64,2,64]{3,1,2,0:T(8,128)S(1)}, f32[1,64,2,64]{3,1,2,0:T(8,128)}, u32[]{:S(2)}) copy-start(f32[1,64,2,64]{3,1,2,0:T(8,128)} %copy-done.17) | copy-start | bytes 98308
  208.4 24.4 %copy-start.21 = (f32[1,64,2,64]{3,1,2,0:T(8,128)S(1)}, f32[1,64,2,64]{3,1,2,0:T(8,128)}, u32[]{:S(2)}) copy-start(f32[1,64,2,64]{3,1,2,0:T(8,128)} %copy-done.20) | copy-start | bytes 98308
  210.4 23.0 %copy-start.15 = (f32[1,64,2,64]{3,1,2,0:T(8,128)S(1)}, f32[1,64,2,64]{3,1,2,0:T(8,128)}, u32[]{:S(2)}) copy-start(f32[1,64,2,64]{3,1,2,0:T(8,128)} %copy-done.14) | copy-start | bytes 98308
  233.4 22.1 %copy-start.3 = (f32[1,256,2,256]{3,1,2,0:T(8,128)S(1)}, f32[1,256,2,256]{3,1,2,0:T(8,128)}, u32[]{:S(2)}) copy-start(f32[1,256,2,256]{3,1,2,0:T(8,128)} %get-tuple-element.48) | copy-start | bytes 1572868
  233.4 22.1 %copy-start.6 = (f32[1,256,2,256]{3,1,2,0:T(8,128)S(1)}, f32[1,256,2,256]{3,1,2,0:T(8,128)}, u32[]{:S(2)}) copy-start(f32[1,256,2,256]{3,1,2,0:T(8,128)} %get-tuple-element.57) | copy-start | bytes 1572868
  259.8 16.9 %all-to-all-start.5 = ((f32[2,2,256,128]{3,1,0,2:T(2,128)}), f32[2,2,256,128]{3,1,0,2:T(2,128)}, u32[]{:S(2)}, u32[]{:S(2)}) async-start(f32[2,2,256,128]{3,1,0,2:T(2,128)} %copy.501), calls=%async_computation.5 | async-start | bytes 1048576 | tf_op jit(solution)/shard_map/all_to_all | solution.py:157
  277.9 38.3 %copy-start.9 = (f32[2,2,32,128]{3,1,0,2:T(2,128)}, f32[2,2,32,128]{3,1,0,2:T(2,128)S(1)}, u32[]{:S(2)}) copy-start(f32[2,2,32,128]{3,1,0,2:T(2,128)S(1)} %reduce_sum.159) | copy-start | bytes 196612
  322.8 21.7 %copy-start.19 = (f32[1,64,2,64]{3,1,2,0:T(8,128)S(1)}, f32[1,64,2,64]{3,1,2,0:T(8,128)}, u32[]{:S(2)}) copy-start(f32[1,64,2,64]{3,1,2,0:T(8,128)} %copy-done.17) | copy-start | bytes 98308
  322.8 21.7 %copy-start.22 = (f32[1,64,2,64]{3,1,2,0:T(8,128)S(1)}, f32[1,64,2,64]{3,1,2,0:T(8,128)}, u32[]{:S(2)}) copy-start(f32[1,64,2,64]{3,1,2,0:T(8,128)} %copy-done.20) | copy-start | bytes 98308
  324.2 21.0 %copy-start.13 = (f32[1,64,2,64]{3,1,2,0:T(8,128)S(1)}, f32[1,64,2,64]{3,1,2,0:T(8,128)}, u32[]{:S(2)}) copy-start(f32[1,64,2,64]{3,1,2,0:T(8,128)} %copy-done.12) | copy-start | bytes 98308
  324.2 21.0 %copy-start.16 = (f32[1,64,2,64]{3,1,2,0:T(8,128)S(1)}, f32[1,64,2,64]{3,1,2,0:T(8,128)}, u32[]{:S(2)}) copy-start(f32[1,64,2,64]{3,1,2,0:T(8,128)} %copy-done.14) | copy-start | bytes 98308
  345.2 22.1 %copy-start.4 = (f32[1,256,2,256]{3,1,2,0:T(8,128)S(1)}, f32[1,256,2,256]{3,1,2,0:T(8,128)}, u32[]{:S(2)}) copy-start(f32[1,256,2,256]{3,1,2,0:T(8,128)} %get-tuple-element.48) | copy-start | bytes 1572868
  345.2 22.1 %copy-start.7 = (f32[1,256,2,256]{3,1,2,0:T(8,128)S(1)}, f32[1,256,2,256]{3,1,2,0:T(8,128)}, u32[]{:S(2)}) copy-start(f32[1,256,2,256]{3,1,2,0:T(8,128)} %get-tuple-element.57) | copy-start | bytes 1572868
  368.7 15.8 %copy-start.10 = (f32[2,2,32,128]{3,1,0,2:T(2,128)S(1)}, f32[2,2,32,128]{3,1,0,2:T(2,128)}, u32[]{:S(2)}) copy-start(f32[2,2,32,128]{3,1,0,2:T(2,128)} %copy-done.9) | copy-start | bytes 196612
  368.7 44.9 %copy-start.24 = (f32[2,2,32,128]{3,0,2,1:T(2,128)S(1)}, f32[2,2,32,128]{3,0,2,1:T(2,128)}, u32[]{:S(2)}) copy-start(f32[2,2,32,128]{3,0,2,1:T(2,128)} %copy-done.23) | copy-start | bytes 196612
  368.7 44.9 %copy-start.26 = (f32[2,2,32,128]{3,0,2,1:T(2,128)S(1)}, f32[2,2,32,128]{3,0,2,1:T(2,128)}, u32[]{:S(2)}) copy-start(f32[2,2,32,128]{3,0,2,1:T(2,128)} %get-tuple-element.31) | copy-start | bytes 196612
  388.7 19.4 %all-to-all-start.10 = ((f32[256,1,4]{2,1,0:T(1,128)}), f32[256,1,4]{2,1,0:T(1,128)S(1)}, u32[]{:S(2)}, u32[]{:S(2)}) async-start(f32[256,1,4]{2,1,0:T(1,128)} %broadcast_in_dim.19), calls=%async_computation.10 | async-start | bytes 262144 | tf_op jit(solution)/shard_map/all_to_all | solution.py:170

commit v7 on v6

--- a/solution.py
+++ b/solution.py
@@ -12,6 +12,7 @@
 
 REG_WEIGHT = 0.5
 HIGHEST_PRECISION = lax.Precision.HIGHEST
+TRANSFORM_PRECISION = lax.Precision.HIGH
 
 
 def extended(cells, sides, width):
@@ -108,15 +109,15 @@
 
 
 def along_last(data, blocks):
-    return jnp.einsum("pkqn,cqzyn->cpzyk", blocks, data, precision=HIGHEST_PRECISION)
+    return jnp.einsum("pkqn,cqzyn->cpzyk", blocks, data, precision=TRANSFORM_PRECISION)
 
 
 def along_rows(data, blocks):
-    return jnp.einsum("pkqn,cqzny->cpzky", blocks, data, precision=HIGHEST_PRECISION)
+    return jnp.einsum("pkqn,cqzny->cpzky", blocks, data, precision=TRANSFORM_PRECISION)
 
 
 def along_depth(data, blocks):
-    return jnp.einsum("pkqn,cqnyx->cpkyx", blocks, data, precision=HIGHEST_PRECISION)
+    return jnp.einsum("pkqn,cqnyx->cpkyx", blocks, data, precision=TRANSFORM_PRECISION)
 
 
 def times_sens(sens, image):

time: 420 us -> 413 us (0.983)
  matrix products: 33.9 us -> 27 us
    dot_general x13, matrix products: 21.2 us -> 14.3 us  [the longest x6 9.21 us: along_rows(): jnp.einsum('pkqn,cqzny->cpzky', blocks, data, precision=TRANSFORM_PRECISION)]
where the time goes in v7:
time: 413 us; the launch traced here: 408 us
  blocking collectives  205 us (50%)
  starting transfers between devices  53.5 us (13%)
  waiting for transfers between devices  44.6 us (11%)
  local copies, waits for them, and re-layouts  36.6 us (9%)
  other arithmetic  32.6 us (8%)
  matrix products  27 us (7%)
  between operations  8.76 us (2%)
    all_to_all x3, blocking collectives, coil_term(): lax.all_to_all(back.astype(link_type), 'slab', split_axis=2, concat_axis=...  71.8 us
    all_to_all x2, blocking collectives, coil_term(): lax.all_to_all(spectrum.astype(jnp.bfloat16), 'slab', split_axis=3, conca...  42.3 us
    all_gather x3, blocking collectives, gather_rows(): return lax.all_gather(value, 'coil', axis=2, tiled=True)  40.4 us
    all_to_all x2, blocking collectives, combine_coils(): lax.all_to_all(partial_value, 'coil', split_axis=2, concat_axis=0, tiled=...  31.8 us
    all_to_all x1, blocking collectives, global_sums(): lax.all_to_all(spread, axes, split_axis=0, concat_axis=0, tiled=True)  19.2 us
    all_to_all x1, starting transfers between devices, coil_term(): lax.all_to_all(spectrum.astype(jnp.bfloat16), 'slab', split_axis=3, conca...  16.5 us
    ppermute x4, starting transfers between devices, extended(): lax.ppermute(tail, axis, [(i, (i + 1) % count) for i in range(ends)])  16.3 us
    all_to_all x1, waiting for transfers between devices, coil_term(): lax.all_to_all(spectrum.astype(jnp.bfloat16), 'slab', split_axis=3, conca...  14 us
  transfers between devices with their start and end apart: 11, of which 7 were waited for; matrix products, arithmetic and copies ran while one was open for 3% of the time, Pallas kernels for 0%

profile of v7, /device:TPU:1, one launch (start us, length us, event | category | flops | bytes accessed | tf_op | source)
XLA Modules:
  0.0 408.4 jit_solution(13546557899540650942)
XLA Ops:
  1.6 3.9 collective-permute-start
  5.5 1.3 collective-permute-start.1
  7.9 1.7 fusion.93
  11.1 2.1 fusion.235
  13.4 4.0 collective-permute-start.2
  17.4 2.1 collective-permute-start.3
  19.8 2.6 collective-permute-done.3
  24.8 1.3 fusion.4
  30.0 2.2 convolution_bitcast_fusion.7
  32.2 2.2 convolution_bitcast_fusion.8
  34.4 6.9 %add_convert_fusion = bf16[32,2,32,128]{3,0,2,1:T(8,128)(2,1)S(1)} fusion(f32[3,32,2,32,128]{4,1,3,2,0:T(8,128)S(1)} %convolution_bitcast_fusion, f32[3,32,2,32,128]{4,1,3,2,0:T(8,128)S(1)} %convolution_bitcast_fusion.1, f32[3,32,2,32,128]{4,1,3,2,0:T(8,128)S(1)} %convolution_bitcast_fusion.2, f32[3,32,2,32,128]{4,1,3,2,0:T(8,128)S(1)} %convolution_bitcast_fusion.3, ...), kind=kLoop, calls=%fused_computation.128 | loop fusion | flops 8650752 | bytes 38797312 | tf_op jit(solution)/shard_map/convert_element_type | solution.py:185
  42.2 4.3 %collective-permute-start.4 = (bf16[32,1,32,128]{3,0,2,1:T(8,128)(2,1)}, bf16[32,1,32,128]{3,0,2,1:T(8,128)(2,1)S(1)}, u32[]{:S(2)}, u32[]{:S(2)}) collective-permute-start(bf16[32,1,32,128]{3,0,2,1:T(8,128)(2,1)} %get-tuple-element.54), channel_id=1, source_target_pairs={{0,8},{8,16},{16,24},{24,32},{32,40},{40,48},{48,56},{56,64},{64,7... | collective-permute-start | bytes 786440 | tf_op jit(solution)/shard_map/ppermute | solution.py:26
  51.4 4.1 %collective-permute-done.5 = bf16[32,1,32,128]{3,0,2,1:T(8,128)(2,1)} collective-permute-done((bf16[32,1,32,128]{3,0,2,1:T(8,128)(2,1)}, bf16[32,1,32,128]{3,0,2,1:T(8,128)(2,1)}, u32[]{:S(2)}, u32[]{:S(2)}) %collective-permute-start.5) | collective-permute-done | bytes 262176 | tf_op jit(solution)/shard_map/ppermute | solution.py:28
  56.3 4.1 %collective-permute-start.6 = (bf16[32,4,1,128]{3,0,2,1:T(8,128)(2,1)S(1)}, bf16[32,4,1,128]{3,0,2,1:T(8,128)(2,1)S(1)}, u32[]{:S(2)}, u32[]{:S(2)}) collective-permute-start(bf16[32,4,1,128]{3,0,2,1:T(8,128)(2,1)S(1)} %get-tuple-element.42), channel_id=1, source_target_pairs={{0,1},{1,2},{2,3},{3,4},{4,5},{5,6},{6,7},{8,9},{9,10},{10,11},{11... | collective-permute-start | bytes 98312 | tf_op jit(solution)/shard_map/ppermute | solution.py:26
  60.4 2.1 collective-permute-start.7
  64.0 1.7 collective-permute-done.7
  68.4 1.4 fusion.182
  71.0 12.8 %all_gather.9 = f32[2,2,256,128]{3,0,2,1:T(2,128)S(1)} all-gather(f32[2,2,32,128]{3,0,2,1:T(2,128)S(1)} %get-tuple-element.30), channel_id=1, replica_groups=mesh['slab'=32,'coil'=8] {'coil'}, dimensions={2}, use_global_device_ids=true | all-gather | bytes 589824 | tf_op jit(solution)/shard_map/all_gather | solution.py:164
  86.2 1.8 copy.481
  89.1 1.8 fusion.23
  90.9 2.0 copy.482
  92.9 16.5 %all-to-all-start = ((bf16[2,2,2,256,128]{4,1,2,0,3:T(2,128)(2,1)}), bf16[2,2,2,256,128]{4,1,2,0,3:T(2,128)(2,1)}, u32[]{:S(2)}, u32[]{:S(2)}) async-start(bf16[2,2,2,256,128]{4,1,2,0,3:T(2,128)(2,1)} %copy.482), calls=%async_computation | async-start | bytes 1048576 | tf_op jit(solution)/shard_map/all_to_all | solution.py:139
  110.4 1.7 convolution_bitcast_fusion.19
  112.1 14.0 %all-to-all-done = bf16[2,2,2,256,128]{4,1,2,0,3:T(2,128)(2,1)} async-done(((bf16[2,2,2,256,128]{4,1,2,0,3:T(2,128)(2,1)}), bf16[2,2,2,256,128]{4,1,2,0,3:T(2,128)(2,1)}, u32[]{:S(2)}, u32[]{:S(2)}) %all-to-all-start) | async-done | bytes 524320 | tf_op jit(solution)/shard_map/all_to_all | solution.py:139
  129.5 31.2 %all_to_all.156 = f32[2,2,64,8,128]{4,1,3,0,2:T(2,128)S(1)} all-to-all(f32[2,2,64,8,128]{4,1,3,0,2:T(2,128)S(1)} %copy.486), channel_id=1, replica_groups=mesh['slab'=32,'coil'=8] {'slab'}, dimensions={2} | all-to-all | bytes 2097152 | tf_op jit(solution)/shard_map/all_to_all | solution.py:149
  160.8 1.9 convolution_bitcast_fusion.15
  163.7 2.0 copy.490
  165.8 16.6 %all_to_all.157 = f32[2,2,256,128]{3,1,0,2:T(2,128)} all-to-all(f32[2,2,256,128]{3,1,0,2:T(2,128)} %copy.490), channel_id=1, replica_groups=mesh['slab'=32,'coil'=8] {'coil'}, dimensions={2} | all-to-all | bytes 1048576 | tf_op jit(solution)/shard_map/all_to_all | solution.py:158
  183.6 14.0 %all_gather.10 = f32[2,2,256,128]{3,1,0,2:T(2,128)S(1)} all-gather(f32[2,2,32,128]{3,1,0,2:T(2,128)S(1)} %reduce_sum.155), channel_id=1, replica_groups=mesh['slab'=32,'coil'=8] {'coil'}, dimensions={2}, use_global_device_ids=true | all-gather | bytes 589824 | tf_op jit(solution)/shard_map/all_gather | solution.py:164
  199.7 1.8 copy.492
  202.5 1.8 fusion.22
  204.4 2.0 copy.493
  206.4 22.1 %all_to_all.158 = bf16[2,2,2,256,128]{4,1,2,0,3:T(2,128)(2,1)S(1)} all-to-all(bf16[2,2,2,256,128]{4,1,2,0,3:T(2,128)(2,1)} %copy.493), channel_id=1, replica_groups=mesh['slab'=32,'coil'=8] {'slab'}, dimensions={3} | all-to-all | bytes 1048576 | tf_op jit(solution)/shard_map/all_to_all | solution.py:139
  230.5 20.3 %all_to_all.159 = bf16[2,2,64,8,128]{4,1,3,0,2:T(2,128)(2,1)S(1)} all-to-all(bf16[2,2,64,8,128]{4,1,3,0,2:T(2,128)(2,1)S(1)} %copy.497), channel_id=1, replica_groups=mesh['slab'=32,'coil'=8] {'slab'}, dimensions={2} | all-to-all | bytes 1048576 | tf_op jit(solution)/shard_map/all_to_all | solution.py:149
  252.8 2.0 copy.501
  254.9 7.4 %all-to-all-start.5 = ((f32[2,2,256,128]{3,1,0,2:T(2,128)}), f32[2,2,256,128]{3,1,0,2:T(2,128)}, u32[]{:S(2)}, u32[]{:S(2)}) async-start(f32[2,2,256,128]{3,1,0,2:T(2,128)} %copy.501), calls=%async_computation.5 | async-start | bytes 1048576 | tf_op jit(solution)/shard_map/all_to_all | solution.py:158
  262.9 8.8 %all-to-all-done.5 = f32[2,2,256,128]{3,1,0,2:T(2,128)} async-done(((f32[2,2,256,128]{3,1,0,2:T(2,128)}), f32[2,2,256,128]{3,1,0,2:T(2,128)}, u32[]{:S(2)}, u32[]{:S(2)}) %all-to-all-start.5) | async-done | bytes 524320 | tf_op jit(solution)/shard_map/all_to_all | solution.py:158
  275.0 19.2 %all_to_all.160 = f32[256,1,2]{2,1,0:T(1,128)S(1)} all-to-all(f32[256,1,2]{2,1,0:T(1,128)S(1)} %broadcast_in_dim.18), channel_id=1, replica_groups=mesh['slab'=32,'coil'=8] {'slab','coil'}, dimensions={0} | all-to-all | bytes 4096 | tf_op jit(solution)/shard_map/all_to_all | solution.py:171
  296.4 13.6 %all_gather.11 = f32[2,2,256,128]{3,0,2,1:T(2,128)S(1)} all-gather(f32[2,2,32,128]{3,0,2,1:T(2,128)S(1)} %multiply_subtract_fusion.3), channel_id=1, replica_groups=mesh['slab'=32,'coil'=8] {'coil'}, dimensions={2}, use_global_device_ids=true | all-gather | bytes 589824 | tf_op jit(solution)/shard_map/all_gather | solution.py:164
  312.2 1.8 copy.509
  315.1 1.8 fusion.21
  317.0 1.4 copy.510
  318.3 20.2 %all_to_all.161 = bf16[2,2,2,256,128]{4,1,2,0,3:T(2,128)(2,1)S(1)} all-to-all(bf16[2,2,2,256,128]{4,1,2,0,3:T(2,128)(2,1)S(1)} %copy.510), channel_id=1, replica_groups=mesh['slab'=32,'coil'=8] {'slab'}, dimensions={3} | all-to-all | bytes 1048576 | tf_op jit(solution)/shard_map/all_to_all | solution.py:139
  340.4 20.3 %all_to_all.162 = bf16[2,2,64,8,128]{4,1,3,0,2:T(2,128)(2,1)S(1)} all-to-all(bf16[2,2,64,8,128]{4,1,3,0,2:T(2,128)(2,1)S(1)} %copy.514), channel_id=1, replica_groups=mesh['slab'=32,'coil'=8] {'slab'}, dimensions={2} | all-to-all | bytes 1048576 | tf_op jit(solution)/shard_map/all_to_all | solution.py:149
  362.3 15.2 %all_to_all.163 = f32[2,2,256,128]{3,1,0,2:T(2,128)S(1)} all-to-all(f32[2,2,256,128]{3,1,0,2:T(2,128)S(1)} %copy.518), channel_id=1, replica_groups=mesh['slab'=32,'coil'=8] {'coil'}, dimensions={2} | all-to-all | bytes 1048576 | tf_op jit(solution)/shard_map/all_to_all | solution.py:158
  378.6 2.7 pad_maximum_fusion.23
  381.9 6.4 %all-to-all-start.10 = ((f32[256,1,4]{2,1,0:T(1,128)}), f32[256,1,4]{2,1,0:T(1,128)S(1)}, u32[]{:S(2)}, u32[]{:S(2)}) async-start(f32[256,1,4]{2,1,0:T(1,128)} %broadcast_in_dim.19), calls=%async_computation.10 | async-start | bytes 262144 | tf_op jit(solution)/shard_map/all_to_all | solution.py:171
  388.5 12.8 %all-to-all-done.10 = f32[256,1,4]{2,1,0:T(1,128)S(1)} async-done(((f32[256,1,4]{2,1,0:T(1,128)}), f32[256,1,4]{2,1,0:T(1,128)S(1)}, u32[]{:S(2)}, u32[]{:S(2)}) %all-to-all-start.10) | async-done | bytes 4128 | tf_op jit(solution)/shard_map/all_to_all | solution.py:171
  (193 shorter events, 53.6 us)
Async XLA Ops:
  0.6 109.8 %copy-start = (f32[2,2,64,8,128]{4,3,2,1,0:T(8,128)S(1)}, f32[2,2,64,8,128]{4,3,2,1,0:T(8,128)}, u32[]{:S(2)}) copy-start(f32[2,2,64,8,128]{4,3,2,1,0:T(8,128)} %param.16) | copy-start | bytes 3145732
  0.6 18.9 %copy-start.28 = (f32[32,32]{1,0:T(8,128)S(1)}, f32[32,32]{1,0:T(8,128)}, u32[]{:S(2)}) copy-start(f32[32,32]{1,0:T(8,128)} %param.14) | copy-start | bytes 12292
  0.7 19.1 %copy-start.29 = (bf16[3,3,3,32,2]{3,4,2,1,0:T(2,128)(2,1)S(1)}, bf16[3,3,3,32,2]{3,4,2,1,0:T(2,128)(2,1)}, u32[]{:S(2)}) copy-start(bf16[3,3,3,32,2]{3,4,2,1,0:T(2,128)(2,1)} %param.11) | copy-start | bytes 10372
  1.6 11.7 %collective-permute-start = (bf16[2,2,32,128]{3,2,1,0:T(8,128)(2,1)S(1)}, bf16[2,2,32,128]{3,2,1,0:T(8,128)(2,1)S(1)}, u32[]{:S(2)}, u32[]{:S(2)}) collective-permute-start(bf16[2,2,32,128]{3,2,1,0:T(8,128)(2,1)S(1)} %convert_element_type.168), channel_id=1, source_target_pairs={{0,8},{8,16},{16,24},{24,32},{32,40},{40,48},{48,56},{56,64},{64,7... | collective-permute-start | bytes 98312 | tf_op jit(solution)/shard_map/ppermute | solution.py:26
  5.5 7.8 %collective-permute-start.1 = (bf16[2,2,32,128]{3,2,1,0:T(8,128)(2,1)S(1)}, bf16[2,2,32,128]{3,2,1,0:T(8,128)(2,1)S(1)}, u32[]{:S(2)}, u32[]{:S(2)}) collective-permute-start(bf16[2,2,32,128]{3,2,1,0:T(8,128)(2,1)S(1)} %convert_element_type.168), channel_id=1, source_target_pairs={{8,0},{16,8},{24,16},{32,24},{40,32},{48,40},{56,48},{64,56},{72,6... | collective-permute-start | bytes 98312 | tf_op jit(solution)/shard_map/ppermute | solution.py:28
  13.4 6.4 %collective-permute-start.2 = (bf16[2,6,2,128]{3,2,1,0:T(2,128)(2,1)S(1)}, bf16[2,6,2,128]{3,2,1,0:T(2,128)(2,1)S(1)}, u32[]{:S(2)}, u32[]{:S(2)}) collective-permute-start(bf16[2,6,2,128]{3,2,1,0:T(2,128)(2,1)S(1)} %get-tuple-element.62), channel_id=1, source_target_pairs={{0,1},{1,2},{2,3},{3,4},{4,5},{5,6},{6,7},{8,9},{9,10},{10,11},{11... | collective-permute-start | bytes 18440 | tf_op jit(solution)/shard_map/ppermute | solution.py:26
  17.4 4.9 %collective-permute-start.3 = (bf16[2,6,2,128]{3,2,1,0:T(2,128)(2,1)S(1)}, bf16[2,6,2,128]{3,2,1,0:T(2,128)(2,1)S(1)}, u32[]{:S(2)}, u32[]{:S(2)}) collective-permute-start(bf16[2,6,2,128]{3,2,1,0:T(2,128)(2,1)S(1)} %get-tuple-element.63), channel_id=1, source_target_pairs={{1,0},{2,1},{3,2},{4,3},{5,4},{6,5},{7,6},{9,8},{10,9},{11,10},{12... | collective-permute-start | bytes 18440 | tf_op jit(solution)/shard_map/ppermute | solution.py:28
  24.8 1.4 copy-start.27
  34.4 13.4 %copy-start.11 = (f32[256,1,256]{2,0,1:T(8,128)S(1)}, f32[256,1,256]{2,0,1:T(8,128)}, u32[]{:S(2)}) copy-start(f32[256,1,256]{2,0,1:T(8,128)} %fusion.93) | copy-start | bytes 786436
  42.2 9.3 %collective-permute-start.4 = (bf16[32,1,32,128]{3,0,2,1:T(8,128)(2,1)}, bf16[32,1,32,128]{3,0,2,1:T(8,128)(2,1)S(1)}, u32[]{:S(2)}, u32[]{:S(2)}) collective-permute-start(bf16[32,1,32,128]{3,0,2,1:T(8,128)(2,1)} %get-tuple-element.54), channel_id=1, source_target_pairs={{0,8},{8,16},{16,24},{24,32},{32,40},{40,48},{48,56},{56,64},{64,7... | collective-permute-start | bytes 786440 | tf_op jit(solution)/shard_map/ppermute | solution.py:26
  46.4 9.1 %collective-permute-start.5 = (bf16[32,1,32,128]{3,0,2,1:T(8,128)(2,1)}, bf16[32,1,32,128]{3,0,2,1:T(8,128)(2,1)}, u32[]{:S(2)}, u32[]{:S(2)}) collective-permute-start(bf16[32,1,32,128]{3,0,2,1:T(8,128)(2,1)} %get-tuple-element.55), channel_id=1, source_target_pairs={{8,0},{16,8},{24,16},{32,24},{40,32},{48,40},{56,48},{64,56},{72,6... | collective-permute-start | bytes 786440 | tf_op jit(solution)/shard_map/ppermute | solution.py:28
  56.3 7.7 %collective-permute-start.6 = (bf16[32,4,1,128]{3,0,2,1:T(8,128)(2,1)S(1)}, bf16[32,4,1,128]{3,0,2,1:T(8,128)(2,1)S(1)}, u32[]{:S(2)}, u32[]{:S(2)}) collective-permute-start(bf16[32,4,1,128]{3,0,2,1:T(8,128)(2,1)S(1)} %get-tuple-element.42), channel_id=1, source_target_pairs={{0,1},{1,2},{2,3},{3,4},{4,5},{5,6},{6,7},{8,9},{9,10},{10,11},{11... | collective-permute-start | bytes 98312 | tf_op jit(solution)/shard_map/ppermute | solution.py:26
  60.4 5.2 %collective-permute-start.7 = (bf16[32,4,1,128]{3,0,2,1:T(8,128)(2,1)S(1)}, bf16[32,4,1,128]{3,0,2,1:T(8,128)(2,1)S(1)}, u32[]{:S(2)}, u32[]{:S(2)}) collective-permute-start(bf16[32,4,1,128]{3,0,2,1:T(8,128)(2,1)S(1)} %get-tuple-element.43), channel_id=1, source_target_pairs={{1,0},{2,1},{3,2},{4,3},{5,4},{6,5},{7,6},{9,8},{10,9},{11,10},{12... | collective-permute-start | bytes 98312 | tf_op jit(solution)/shard_map/ppermute | solution.py:28
  67.7 2.2 copy-start.25
  71.0 14.0 %copy-start.23 = (f32[2,2,32,128]{3,0,2,1:T(2,128)}, f32[2,2,32,128]{3,0,2,1:T(2,128)S(1)}, u32[]{:S(2)}) copy-start(f32[2,2,32,128]{3,0,2,1:T(2,128)S(1)} %get-tuple-element.30) | copy-start | bytes 196612
  83.9 5.2 %copy-start.1 = (f32[1,256,2,256]{3,1,2,0:T(8,128)S(1)}, f32[1,256,2,256]{3,1,2,0:T(8,128)}, u32[]{:S(2)}) copy-start(f32[1,256,2,256]{3,1,2,0:T(8,128)} %get-tuple-element.56) | copy-start | bytes 1572868
  89.1 20.4 %copy-start.30 = (s32[64,8]{0,1:T(8,128)S(1)}, s32[64,8]{0,1:T(8,128)}, u32[]{:S(2)}) copy-start(s32[64,8]{0,1:T(8,128)} %param.17) | copy-start | bytes 6148
  92.9 33.2 %all-to-all-start = ((bf16[2,2,2,256,128]{4,1,2,0,3:T(2,128)(2,1)}), bf16[2,2,2,256,128]{4,1,2,0,3:T(2,128)(2,1)}, u32[]{:S(2)}, u32[]{:S(2)}) async-start(bf16[2,2,2,256,128]{4,1,2,0,3:T(2,128)(2,1)} %copy.482), calls=%async_computation | async-start | bytes 1048576 | tf_op jit(solution)/shard_map/all_to_all | solution.py:139
  110.3 17.1 %copy-start.17 = (f32[1,64,2,64]{3,1,2,0:T(8,128)}, f32[1,64,2,64]{3,1,2,0:T(8,128)S(1)}, u32[]{:S(2)}) copy-start(f32[1,64,2,64]{3,1,2,0:T(8,128)S(1)} %get-tuple-element.65) | copy-start | bytes 98308
  110.3 17.1 %copy-start.20 = (f32[1,64,2,64]{3,1,2,0:T(8,128)}, f32[1,64,2,64]{3,1,2,0:T(8,128)S(1)}, u32[]{:S(2)}) copy-start(f32[1,64,2,64]{3,1,2,0:T(8,128)S(1)} %get-tuple-element.70) | copy-start | bytes 98308
  110.3 17.7 %copy-start.14 = (f32[1,64,2,64]{3,1,2,0:T(8,128)}, f32[1,64,2,64]{3,1,2,0:T(8,128)S(1)}, u32[]{:S(2)}) copy-start(f32[1,64,2,64]{3,1,2,0:T(8,128)S(1)} %get-tuple-element.71) | copy-start | bytes 98308
  110.4 118.9 %copy-start.12 = (f32[1,64,2,64]{3,1,2,0:T(8,128)}, f32[1,64,2,64]{3,1,2,0:T(8,128)S(1)}, u32[]{:S(2)}) copy-start(f32[1,64,2,64]{3,1,2,0:T(8,128)S(1)} %get-tuple-element.64) | copy-start | bytes 98308
  126.1 1.4 copy-start.8
  129.5 31.3 %copy-start.2 = (f32[1,256,2,256]{3,1,2,0:T(8,128)S(1)}, f32[1,256,2,256]{3,1,2,0:T(8,128)}, u32[]{:S(2)}) copy-start(f32[1,256,2,256]{3,1,2,0:T(8,128)} %get-tuple-element.48) | copy-start | bytes 1572868
  129.5 31.3 %copy-start.5 = (f32[1,256,2,256]{3,1,2,0:T(8,128)S(1)}, f32[1,256,2,256]{3,1,2,0:T(8,128)}, u32[]{:S(2)}) copy-start(f32[1,256,2,256]{3,1,2,0:T(8,128)} %get-tuple-element.57) | copy-start | bytes 1572868
  204.4 24.4 %copy-start.18 = (f32[1,64,2,64]{3,1,2,0:T(8,128)S(1)}, f32[1,64,2,64]{3,1,2,0:T(8,128)}, u32[]{:S(2)}) copy-start(f32[1,64,2,64]{3,1,2,0:T(8,128)} %copy-done.17) | copy-start | bytes 98308
  204.4 24.4 %copy-start.21 = (f32[1,64,2,64]{3,1,2,0:T(8,128)S(1)}, f32[1,64,2,64]{3,1,2,0:T(8,128)}, u32[]{:S(2)}) copy-start(f32[1,64,2,64]{3,1,2,0:T(8,128)} %copy-done.20) | copy-start | bytes 98308
  206.4 22.8 %copy-start.15 = (f32[1,64,2,64]{3,1,2,0:T(8,128)S(1)}, f32[1,64,2,64]{3,1,2,0:T(8,128)}, u32[]{:S(2)}) copy-start(f32[1,64,2,64]{3,1,2,0:T(8,128)} %copy-done.14) | copy-start | bytes 98308
  229.3 21.6 %copy-start.3 = (f32[1,256,2,256]{3,1,2,0:T(8,128)S(1)}, f32[1,256,2,256]{3,1,2,0:T(8,128)}, u32[]{:S(2)}) copy-start(f32[1,256,2,256]{3,1,2,0:T(8,128)} %get-tuple-element.48) | copy-start | bytes 1572868
  229.3 21.6 %copy-start.6 = (f32[1,256,2,256]{3,1,2,0:T(8,128)S(1)}, f32[1,256,2,256]{3,1,2,0:T(8,128)}, u32[]{:S(2)}) copy-start(f32[1,256,2,256]{3,1,2,0:T(8,128)} %get-tuple-element.57) | copy-start | bytes 1572868
  254.9 16.9 %all-to-all-start.5 = ((f32[2,2,256,128]{3,1,0,2:T(2,128)}), f32[2,2,256,128]{3,1,0,2:T(2,128)}, u32[]{:S(2)}, u32[]{:S(2)}) async-start(f32[2,2,256,128]{3,1,0,2:T(2,128)} %copy.501), calls=%async_computation.5 | async-start | bytes 1048576 | tf_op jit(solution)/shard_map/all_to_all | solution.py:158
  272.9 38.2 %copy-start.9 = (f32[2,2,32,128]{3,1,0,2:T(2,128)}, f32[2,2,32,128]{3,1,0,2:T(2,128)S(1)}, u32[]{:S(2)}) copy-start(f32[2,2,32,128]{3,1,0,2:T(2,128)S(1)} %reduce_sum.159) | copy-start | bytes 196612
  317.0 21.7 %copy-start.19 = (f32[1,64,2,64]{3,1,2,0:T(8,128)S(1)}, f32[1,64,2,64]{3,1,2,0:T(8,128)}, u32[]{:S(2)}) copy-start(f32[1,64,2,64]{3,1,2,0:T(8,128)} %copy-done.17) | copy-start | bytes 98308
  317.0 21.7 %copy-start.22 = (f32[1,64,2,64]{3,1,2,0:T(8,128)S(1)}, f32[1,64,2,64]{3,1,2,0:T(8,128)}, u32[]{:S(2)}) copy-start(f32[1,64,2,64]{3,1,2,0:T(8,128)} %copy-done.20) | copy-start | bytes 98308
  318.3 20.9 %copy-start.13 = (f32[1,64,2,64]{3,1,2,0:T(8,128)S(1)}, f32[1,64,2,64]{3,1,2,0:T(8,128)}, u32[]{:S(2)}) copy-start(f32[1,64,2,64]{3,1,2,0:T(8,128)} %copy-done.12) | copy-start | bytes 98308
  318.3 20.9 %copy-start.16 = (f32[1,64,2,64]{3,1,2,0:T(8,128)S(1)}, f32[1,64,2,64]{3,1,2,0:T(8,128)}, u32[]{:S(2)}) copy-start(f32[1,64,2,64]{3,1,2,0:T(8,128)} %copy-done.14) | copy-start | bytes 98308
  339.2 21.6 %copy-start.4 = (f32[1,256,2,256]{3,1,2,0:T(8,128)S(1)}, f32[1,256,2,256]{3,1,2,0:T(8,128)}, u32[]{:S(2)}) copy-start(f32[1,256,2,256]{3,1,2,0:T(8,128)} %get-tuple-element.48) | copy-start | bytes 1572868
  339.2 21.6 %copy-start.7 = (f32[1,256,2,256]{3,1,2,0:T(8,128)S(1)}, f32[1,256,2,256]{3,1,2,0:T(8,128)}, u32[]{:S(2)}) copy-start(f32[1,256,2,256]{3,1,2,0:T(8,128)} %get-tuple-element.57) | copy-start | bytes 1572868
  361.9 15.8 %copy-start.10 = (f32[2,2,32,128]{3,1,0,2:T(2,128)S(1)}, f32[2,2,32,128]{3,1,0,2:T(2,128)}, u32[]{:S(2)}) copy-start(f32[2,2,32,128]{3,1,0,2:T(2,128)} %copy-done.9) | copy-start | bytes 196612
  361.9 44.9 %copy-start.24 = (f32[2,2,32,128]{3,0,2,1:T(2,128)S(1)}, f32[2,2,32,128]{3,0,2,1:T(2,128)}, u32[]{:S(2)}) copy-start(f32[2,2,32,128]{3,0,2,1:T(2,128)} %copy-done.23) | copy-start | bytes 196612
  361.9 44.9 %copy-start.26 = (f32[2,2,32,128]{3,0,2,1:T(2,128)S(1)}, f32[2,2,32,128]{3,0,2,1:T(2,128)}, u32[]{:S(2)}) copy-start(f32[2,2,32,128]{3,0,2,1:T(2,128)} %get-tuple-element.31) | copy-start | bytes 196612
  381.9 19.4 %all-to-all-start.10 = ((f32[256,1,4]{2,1,0:T(1,128)}), f32[256,1,4]{2,1,0:T(1,128)S(1)}, u32[]{:S(2)}, u32[]{:S(2)}) async-start(f32[256,1,4]{2,1,0:T(1,128)} %broadcast_in_dim.19), calls=%async_computation.10 | async-start | bytes 262144 | tf_op jit(solution)/shard_map/all_to_all | solution.py:171
